TPU v7x, 256 devices: a whole 4x4x8 slice. The times are simulated.
256 devices in a mesh: ctx: 8 (over x, core), ch: 32 (over y, z).
Axes of the slice: x: 4, y: 4, z: 8, core: 2. Of those that a mesh axis runs over, the one named last changes fastest.
Arguments:
- tokens_in: bfloat16 [8192, 8192], P(('ctx', 'ch')), may hold values from -6 to 6
- norm_gain: float32 [8192], replicated, may hold values from 0.1 to 1.9
- proj_weight: bfloat16 [3, 8192, 8192], P(None, 'ctx', 'ch'), may hold values from -0.0625 to 0.0625
- conv_weight: float32 [3, 7, 8192], P(None, None, 'ch'), may hold values from -2 to 2
- decay_rate: float32 [16, 8192], P(None, 'ch'), may hold values from 6.1035157e-06 to 0.04
- residue: float32 [16, 8192], P(None, 'ch'), may hold values from -1.5 to 1.5
- skip_gain: float32 [8192], P('ch'), may hold values from -3 to 3
Outputs:
- gated: bfloat16 [8192, 8192], P(('ctx', 'ch'))
All inputs are finite; a program needn't handle non-finite values.
Results may differ from a plain program's by a relative error of at most 0.008.
Values may be sent and summed in bfloat16 or wider, within the bound.
No kernel may reach another device: no remote copies, remote signals or barrier semaphores. Data moves between devices by JAX's collectives and lax.ppermute only.
A program may use at most 128 MiB of HBM per device.

v0:
```python
import jax
import jax.numpy as jnp
from jax import lax
from jax.sharding import PartitionSpec as P

norm_eps = 1e-05


def shifted(shard, axis, by):
    length = lax.axis_size(axis)
    pairs = [(i, i + by) for i in range(length) if 0 <= i + by < length]
    return lax.ppermute(shard, axis, pairs)


def on_device(tokens_in, norm_gain, proj_weight, conv_weight, decay_rate, residue, skip_gain):
    widened = tokens_in.astype(jnp.float32)
    mean_square = jnp.mean(widened * widened, axis=-1, keepdims=True)
    normed = (widened * lax.rsqrt(mean_square + norm_eps) * norm_gain[None, :]).astype(jnp.bfloat16)
    gathered = lax.all_gather(normed, "ch", axis=0, tiled=True)
    row_count = gathered.shape[0]
    chan_count = proj_weight.shape[2]
    summed = jnp.einsum(
        "tf,ifc->itc",
        gathered,
        lax.all_gather(proj_weight, "ctx", axis=1, tiled=True),
        preferred_element_type=jnp.float32,
    )
    projected = summed.astype(jnp.bfloat16)
    tap_count = conv_weight.shape[1]
    reach = tap_count - 1
    rim_rows = shifted(projected[:, row_count - reach :, :], "ctx", 1)
    padded = jnp.concatenate([rim_rows, projected], axis=1).astype(jnp.float32)
    featured = jnp.zeros((3, row_count, chan_count), jnp.float32)
    for shift_idx in range(tap_count):
        featured = (
            featured
            + conv_weight[:, shift_idx, None, :]
            * padded[:, reach - shift_idx : reach - shift_idx + row_count, :]
        )
    queries = featured[0]
    mixed = featured[1] * featured[2]
    highest = lax.Precision.HIGHEST
    in_scale = jnp.sqrt(-jnp.expm1(-2.0 * decay_rate))
    span_rows = min(128, row_count)
    span_count = row_count // span_rows
    positions = jnp.arange(span_rows, dtype=jnp.float32)
    lag_decay = jnp.exp(-decay_rate[:, None, :] * positions[None, :, None])
    impulse = jnp.sum((residue * in_scale)[:, None, :] * lag_decay, axis=0)
    offsets = jnp.arange(span_rows)[:, None] - jnp.arange(span_rows)[None, :]
    lag_table = (offsets[None, :, :] == jnp.arange(span_rows)[:, None, None]).astype(jnp.float32)
    toeplitz = jnp.einsum("lc,lts->cts", impulse, lag_table, precision=highest)
    spans_in = mixed.reshape(span_count, span_rows, chan_count)
    inside = jnp.einsum("cts,jsc->jtc", toeplitz, spans_in, precision=highest)
    end_weight = in_scale[:, None, :] * jnp.exp(
        -decay_rate[:, None, :] * (span_rows - 1.0 - positions)[None, :, None]
    )
    span_ends = jnp.einsum("jsc,msc->jmc", spans_in, end_weight, precision=highest)
    span_decay = jnp.exp(-decay_rate * float(span_rows))

    def advance(carried, span_end):
        return (span_decay * carried + span_end, carried)

    zero_state = jnp.zeros(decay_rate.shape, jnp.float32)
    local_end, starts = lax.scan(advance, zero_state, span_ends)
    whole_decay = jnp.exp(-decay_rate * float(row_count))

    def handoff(unused_turn, incoming):
        return shifted(whole_decay * incoming + local_end, "ctx", 1)

    incoming = lax.fori_loop(0, lax.axis_size("ctx") - 1, handoff, zero_state)
    span_starts = jnp.arange(span_count, dtype=jnp.float32) * float(span_rows)
    starts = (
        starts
        + jnp.exp(-decay_rate[None, :, :] * span_starts[:, None, None]) * incoming[None, :, :]
    )
    out_weight = residue[:, None, :] * jnp.exp(
        -decay_rate[:, None, :] * (positions + 1.0)[None, :, None]
    )
    outside = jnp.einsum("jmc,mtc->jtc", starts, out_weight, precision=highest)
    filtered = (inside + outside).reshape(row_count, chan_count)
    gated = (queries * (filtered + skip_gain[None, :] * mixed)).astype(jnp.bfloat16)
    return lax.all_to_all(gated, "ch", split_axis=0, concat_axis=1, tiled=True)


def solution(mesh):
    in_specs = (
        P(("ctx", "ch"), None),
        P(),
        P(None, "ctx", "ch"),
        P(None, None, "ch"),
        P(None, "ch"),
        P(None, "ch"),
        P("ch"),
    )
    out_specs = P(("ctx", "ch"), None)
    return jax.shard_map(
        on_device, mesh=mesh, in_specs=in_specs, out_specs=out_specs, check_vma=False
    )
```

profile of v0, /device:TPU:32, one launch (start us, length us, event | category | flops | bytes accessed | tf_op | source)
XLA Modules:
  0.0 373.8 jit_solution(1986812862186608656)
XLA Ops:
  8.6 2.0 fusion.40
  10.9 1.7 multiply_reduce_fusion
  12.7 9.6 %fusion.4 = f32[256,128,128]{2,0,1:T(8,128)} fusion(s32[128,128]{1,0:T(8,128)S(1)} %iota_subtract_fusion, f32[128,256]{0,1:T(8,128)S(1)} %multiply_reduce_fusion), kind=kOutput, calls=%fused_computation.8 | convolution fusion | flops 6444548096 | bytes 16973824 | tf_op jit(solution)/shard_map/lc,lts->cts/dot_general | solution.py:51
  22.2 59.4 %all-gather.5.cloned.1.call-done = bf16[3,8192,256]{2,1,0:T(8,128)(2,1)} async-done(((bf16[3,1024,256]{2,1,0:T(8,128)(2,1)}), bf16[3,8192,256]{2,1,0:T(8,128)(2,1)}) %all-gather.5.cloned.1.call-update) | async-done | bytes 12582928 | tf_op jit(solution)/shard_map/all_gather | solution.py:25
  81.6 141.0 %all-gather.3.cloned.1.call-done = bf16[1024,8192]{1,0:T(8,128)(2,1)} async-done(((bf16[32,8192]{1,0:T(8,128)(2,1)}), bf16[1024,8192]{1,0:T(8,128)(2,1)}) %all-gather.3.cloned.1.call-update) | async-done | bytes 16777232 | tf_op jit(solution)/shard_map/all_gather | solution.py:19
  222.6 18.7 %fusion.23 = bf16[3,1024,256]{2,1,0:T(8,128)(2,1)S(1)} fusion(bf16[3,8192,256]{2,1,0:T(8,128)(2,1)} %all-gather.5.cloned.1.call-done, bf16[1024,8192]{1,0:T(8,128)(2,1)} %all-gather.3.cloned.1.call-done), kind=kOutput, calls=%fused_computation.34 | convolution fusion | flops 12885688320 | bytes 30932992 | tf_op jit(solution)/shard_map/tf,ifc->itc/dot_general | solution.py:22
  241.3 1.5 collective-permute-start.1
  244.0 2.6 fusion.6
  247.2 38.4 %fusion.32 = f32[8,128,256]{1,0,2:T(8,128)} fusion(f32[8,128,256]{1,0,2:T(8,128)S(1)} %copy.29, f32[256,128,128]{2,0,1:T(8,128)} %fusion.4), kind=kOutput, calls=%fused_computation.37 | convolution fusion | flops 402653184 | bytes 18874368 | tf_op jit(solution)/shard_map/cts,jsc->jtc/dot_general | solution.py:53
  285.6 5.2 %fusion.29 = f32[8,16,256]{1,0,2:T(8,128)} fusion(f32[8,128,256]{1,0,2:T(8,128)S(1)} %copy.29, f32[128]{0:T(128)S(1)} %iota_subtract_fusion.1, f32[16,256]{0,1:T(8,128)S(1)} %copy.32, f32[16,256]{0,1:T(8,128)S(1)} %copy.28), kind=kOutput, calls=%fused_computation.36 | convolution fusion | flops 51380224 | bytes 1212928 | tf_op jit(solution)/shard_map/jsc,msc->jmc/dot_general | solution.py:57
  290.7 1.6 copy.34
  292.4 4.9 %while.24 = (s32[]{:T(128)}, f32[16,256]{1,0:T(8,128)S(1)}, f32[8,16,256]{2,1,0:T(8,128)}, f32[16,256]{1,0:T(8,128)S(1)}, f32[8,16,256]{2,1,0:T(8,128)S(1)}, /*index=5*/s32[]{:T(128)}, s32[]{:T(128)}) while((s32[]{:T(128)}, f32[16,256]{1,0:T(8,128)S(1)}, f32[8,16,256]{2,1,0:T(8,128)}, f32[16,256]{1,0:T(8,128)S(1)}, ...), condition=%wide.region_3.4_spmd.clone, body=%wide.region_2.3_spmd.clone.sunk | while | flops 16387 | bytes 98408 | solution.py:64
  297.3 35.0 %while.23 = (s32[]{:T(128)}, f32[16,256]{1,0:T(8,128)S(1)}, f32[16,256]{1,0:T(8,128)S(1)}, f32[16,256]{1,0:T(8,128)S(1)}, s32[]{:T(128)}) while((s32[]{:T(128)}, f32[16,256]{1,0:T(8,128)S(1)}, f32[16,256]{1,0:T(8,128)S(1)}, f32[16,256]{1,0:T(8,128)S(1)}, s32[]{:T(128)}) %tuple.55), condition=%wide.region_5.6_spmd, body=%wide.region_4.5_spmd.sunk | while | flops 8194 | bytes 131173 | solution.py:70
  297.3 4.1 %collective-permute-start = (f32[16,256]{1,0:T(8,128)S(1)}, f32[16,256]{1,0:T(8,128)S(1)}, u32[]{:S(2)}, u32[]{:S(2)}) collective-permute-start(f32[16,256]{1,0:T(8,128)S(1)} %multiply_add_fusion.3), channel_id=1, source_target_pairs={{0,32},{32,64},{64,96},{96,128},{128,160},{160,192},{192,224},{1,3... | collective-permute-start | bytes 49160 | tf_op jit(solution)/shard_map/while/body/eval_jaxpr/ppermute | solution.py:12
  302.3 3.9 %collective-permute-start = (f32[16,256]{1,0:T(8,128)S(1)}, f32[16,256]{1,0:T(8,128)S(1)}, u32[]{:S(2)}, u32[]{:S(2)}) collective-permute-start(f32[16,256]{1,0:T(8,128)S(1)} %multiply_add_fusion.3), channel_id=1, source_target_pairs={{0,32},{32,64},{64,96},{96,128},{128,160},{160,192},{192,224},{1,3... | collective-permute-start | bytes 49160 | tf_op jit(solution)/shard_map/while/body/eval_jaxpr/ppermute | solution.py:12
  307.1 4.2 %collective-permute-start = (f32[16,256]{1,0:T(8,128)S(1)}, f32[16,256]{1,0:T(8,128)S(1)}, u32[]{:S(2)}, u32[]{:S(2)}) collective-permute-start(f32[16,256]{1,0:T(8,128)S(1)} %multiply_add_fusion.3), channel_id=1, source_target_pairs={{0,32},{32,64},{64,96},{96,128},{128,160},{160,192},{192,224},{1,3... | collective-permute-start | bytes 49160 | tf_op jit(solution)/shard_map/while/body/eval_jaxpr/ppermute | solution.py:12
  312.1 4.2 %collective-permute-start = (f32[16,256]{1,0:T(8,128)S(1)}, f32[16,256]{1,0:T(8,128)S(1)}, u32[]{:S(2)}, u32[]{:S(2)}) collective-permute-start(f32[16,256]{1,0:T(8,128)S(1)} %multiply_add_fusion.3), channel_id=1, source_target_pairs={{0,32},{32,64},{64,96},{96,128},{128,160},{160,192},{192,224},{1,3... | collective-permute-start | bytes 49160 | tf_op jit(solution)/shard_map/while/body/eval_jaxpr/ppermute | solution.py:12
  317.2 4.2 %collective-permute-start = (f32[16,256]{1,0:T(8,128)S(1)}, f32[16,256]{1,0:T(8,128)S(1)}, u32[]{:S(2)}, u32[]{:S(2)}) collective-permute-start(f32[16,256]{1,0:T(8,128)S(1)} %multiply_add_fusion.3), channel_id=1, source_target_pairs={{0,32},{32,64},{64,96},{96,128},{128,160},{160,192},{192,224},{1,3... | collective-permute-start | bytes 49160 | tf_op jit(solution)/shard_map/while/body/eval_jaxpr/ppermute | solution.py:12
  322.2 4.2 %collective-permute-start = (f32[16,256]{1,0:T(8,128)S(1)}, f32[16,256]{1,0:T(8,128)S(1)}, u32[]{:S(2)}, u32[]{:S(2)}) collective-permute-start(f32[16,256]{1,0:T(8,128)S(1)} %multiply_add_fusion.3), channel_id=1, source_target_pairs={{0,32},{32,64},{64,96},{96,128},{128,160},{160,192},{192,224},{1,3... | collective-permute-start | bytes 49160 | tf_op jit(solution)/shard_map/while/body/eval_jaxpr/ppermute | solution.py:12
  327.3 4.2 %collective-permute-start = (f32[16,256]{1,0:T(8,128)S(1)}, f32[16,256]{1,0:T(8,128)S(1)}, u32[]{:S(2)}, u32[]{:S(2)}) collective-permute-start(f32[16,256]{1,0:T(8,128)S(1)} %multiply_add_fusion.3), channel_id=1, source_target_pairs={{0,32},{32,64},{64,96},{96,128},{128,160},{160,192},{192,224},{1,3... | collective-permute-start | bytes 49160 | tf_op jit(solution)/shard_map/while/body/eval_jaxpr/ppermute | solution.py:12
  333.3 1.3 copy.35
  334.6 5.0 %fusion.35 = f32[8,128,256]{1,0,2:T(8,128)} fusion(f32[8,128,256]{1,0,2:T(8,128)S(1)} %copy-done, f32[8,16,256]{1,0,2:T(8,128)} %copy.35, f32[128]{0:T(128)S(1)} %iota_add_fusion, f32[16,256]{0,1:T(8,128)} %copy.31, f32[16,256]{0,1:T(8,128)S(1)} %copy.28), kind=kOutput, calls=%fused_computation.38 | convolution fusion | flops 51642368 | bytes 2261504 | tf_op jit(solution)/shard_map/jmc,mtc->jtc/dot_general | solution.py:79
  339.6 1.6 copy.36
  341.6 24.6 %all_to_all.16 = bf16[32,32,256]{2,1,0:T(8,128)(2,1)S(1)} all-to-all(bf16[32,32,256]{2,1,0:T(8,128)(2,1)S(1)} %multiply_convert_fusion), channel_id=1, replica_groups=mesh['ctx'=8,'ch'=32] {'ch'}, dimensions={0} | all-to-all | bytes 1048576 | tf_op jit(solution)/shard_map/all_to_all | solution.py:82
  (71 shorter events, 17.0 us)
Async XLA Ops:
  6.5 4.1 %copy-start.3 = (f32[16,256]{1,0:T(8,128)S(1)}, f32[16,256]{1,0:T(8,128)}, u32[]{:S(2)}) copy-start(f32[16,256]{1,0:T(8,128)} %param.15) | copy-start | bytes 49156
  6.5 4.1 %copy-start.1 = (f32[16,256]{1,0:T(8,128)S(1)}, f32[16,256]{1,0:T(8,128)}, u32[]{:S(2)}) copy-start(f32[16,256]{1,0:T(8,128)} %param.16) | copy-start | bytes 49156
  6.5 6.1 %copy-start.2 = (f32[3,7,256]{2,1,0:T(8,128)S(1)}, f32[3,7,256]{2,1,0:T(8,128)}, u32[]{:S(2)}) copy-start(f32[3,7,256]{2,1,0:T(8,128)} %param.14) | copy-start | bytes 64516
  6.5 75.1 %all-gather.5.cloned.1.call-start = ((), (), s32[]{:S(2)}) async-start(), calls=%async_computation.2 | async-start | bytes 14155776 | tf_op jit(solution)/shard_map/all_gather | solution.py:25
  7.3 215.3 %all-gather.3.cloned.1.call-start = ((), (), s32[]{:S(2)}) async-start(), calls=%async_computation.1 | async-start | bytes 17301504 | tf_op jit(solution)/shard_map/all_gather | solution.py:19
  241.3 2.4 collective-permute-start.1
  290.7 43.9 %copy-start = (f32[8,128,256]{1,0,2:T(8,128)S(1)}, f32[8,128,256]{1,0,2:T(8,128)}, u32[]{:S(2)}) copy-start(f32[8,128,256]{1,0,2:T(8,128)} %fusion.32) | copy-start | bytes 3145732
  297.3 4.9 %collective-permute-start = (f32[16,256]{1,0:T(8,128)S(1)}, f32[16,256]{1,0:T(8,128)S(1)}, u32[]{:S(2)}, u32[]{:S(2)}) collective-permute-start(f32[16,256]{1,0:T(8,128)S(1)} %multiply_add_fusion.3), channel_id=1, source_target_pairs={{0,32},{32,64},{64,96},{96,128},{128,160},{160,192},{192,224},{1,3... | collective-permute-start | bytes 49160 | tf_op jit(solution)/shard_map/while/body/eval_jaxpr/ppermute | solution.py:12
  302.3 4.8 %collective-permute-start = (f32[16,256]{1,0:T(8,128)S(1)}, f32[16,256]{1,0:T(8,128)S(1)}, u32[]{:S(2)}, u32[]{:S(2)}) collective-permute-start(f32[16,256]{1,0:T(8,128)S(1)} %multiply_add_fusion.3), channel_id=1, source_target_pairs={{0,32},{32,64},{64,96},{96,128},{128,160},{160,192},{192,224},{1,3... | collective-permute-start | bytes 49160 | tf_op jit(solution)/shard_map/while/body/eval_jaxpr/ppermute | solution.py:12
  307.1 5.0 %collective-permute-start = (f32[16,256]{1,0:T(8,128)S(1)}, f32[16,256]{1,0:T(8,128)S(1)}, u32[]{:S(2)}, u32[]{:S(2)}) collective-permute-start(f32[16,256]{1,0:T(8,128)S(1)} %multiply_add_fusion.3), channel_id=1, source_target_pairs={{0,32},{32,64},{64,96},{96,128},{128,160},{160,192},{192,224},{1,3... | collective-permute-start | bytes 49160 | tf_op jit(solution)/shard_map/while/body/eval_jaxpr/ppermute | solution.py:12
  312.1 5.0 %collective-permute-start = (f32[16,256]{1,0:T(8,128)S(1)}, f32[16,256]{1,0:T(8,128)S(1)}, u32[]{:S(2)}, u32[]{:S(2)}) collective-permute-start(f32[16,256]{1,0:T(8,128)S(1)} %multiply_add_fusion.3), channel_id=1, source_target_pairs={{0,32},{32,64},{64,96},{96,128},{128,160},{160,192},{192,224},{1,3... | collective-permute-start | bytes 49160 | tf_op jit(solution)/shard_map/while/body/eval_jaxpr/ppermute | solution.py:12
  317.2 5.0 %collective-permute-start = (f32[16,256]{1,0:T(8,128)S(1)}, f32[16,256]{1,0:T(8,128)S(1)}, u32[]{:S(2)}, u32[]{:S(2)}) collective-permute-start(f32[16,256]{1,0:T(8,128)S(1)} %multiply_add_fusion.3), channel_id=1, source_target_pairs={{0,32},{32,64},{64,96},{96,128},{128,160},{160,192},{192,224},{1,3... | collective-permute-start | bytes 49160 | tf_op jit(solution)/shard_map/while/body/eval_jaxpr/ppermute | solution.py:12
  322.2 5.0 %collective-permute-start = (f32[16,256]{1,0:T(8,128)S(1)}, f32[16,256]{1,0:T(8,128)S(1)}, u32[]{:S(2)}, u32[]{:S(2)}) collective-permute-start(f32[16,256]{1,0:T(8,128)S(1)} %multiply_add_fusion.3), channel_id=1, source_target_pairs={{0,32},{32,64},{64,96},{96,128},{128,160},{160,192},{192,224},{1,3... | collective-permute-start | bytes 49160 | tf_op jit(solution)/shard_map/while/body/eval_jaxpr/ppermute | solution.py:12
  327.3 5.0 %collective-permute-start = (f32[16,256]{1,0:T(8,128)S(1)}, f32[16,256]{1,0:T(8,128)S(1)}, u32[]{:S(2)}, u32[]{:S(2)}) collective-permute-start(f32[16,256]{1,0:T(8,128)S(1)} %multiply_add_fusion.3), channel_id=1, source_target_pairs={{0,32},{32,64},{64,96},{96,128},{128,160},{160,192},{192,224},{1,3... | collective-permute-start | bytes 49160 | tf_op jit(solution)/shard_map/while/body/eval_jaxpr/ppermute | solution.py:12
  334.6 6.5 %copy-start.4 = (f32[256]{0:T(256)S(1)}, f32[256]{0:T(256)}, u32[]{:S(2)}) copy-start(f32[256]{0:T(256)} %param.17) | copy-start | bytes 3076
Sparse Core Ops, SparseCore 0:
  9.2 72.3 all-gather.4
  84.2 138.3 all-gather.2
where the time goes:
time: 377 us; the launch traced here: 374 us
  waiting for transfers between devices  207 us (55%)
  matrix products  76.7 us (20%)
  starting transfers between devices  30.7 us (8%)
  blocking collectives  24.6 us (7%)
  other arithmetic  14.5 us (4%)
  between operations  13.6 us (4%)
  local copies, waits for them, and re-layouts  6.84 us (2%)
    all_gather x1, waiting for transfers between devices, on_device(): gathered = lax.all_gather(normed, 'ch', axis=0, tiled=True)  141 us
    all_gather x1, waiting for transfers between devices, on_device(): lax.all_gather(proj_weight, 'ctx', axis=1, tiled=True)  59.4 us
    dot_general x1, matrix products, on_device(): inside = jnp.einsum('cts,jsc->jtc', toeplitz, spans_in, precision=highest)  38.4 us
    ppermute x8, starting transfers between devices, shifted(): return lax.ppermute(shard, axis, pairs)  30.6 us
    all_to_all x1, blocking collectives, on_device(): return lax.all_to_all(gated, 'ch', split_axis=0, concat_axis=1, tiled=True)  24.6 us
    dot_general x1, matrix products, on_device(): jnp.einsum('tf,ifc->itc', gathered, lax.all_gather(proj_weight, 'ctx', ax...  18.7 us
    dot_general x1, matrix products, on_device(): toeplitz = jnp.einsum('lc,lts->cts', impulse, lag_table, precision=highest)  9.55 us
  transfers between devices with their start and end apart: 10, of which 9 were waited for; matrix products, arithmetic and copies ran while one was open for 4% of the time, Pallas kernels for 0%

commit v1 on v0

--- a/solution.py
+++ b/solution.py
@@ -12,6 +12,22 @@
     return lax.ppermute(shard, axis, pairs)
 
 
+def gathered_weight(block):
+    count = lax.axis_size("ctx")
+    me = lax.axis_index("ctx")
+    width = block.shape[1]
+    held = [(block, me)]
+    for by in range(2, count, 2):
+        pairs = [(i, (i + by) % count) for i in range(count)]
+        held.append((lax.ppermute(block, "ctx", pairs), (me - by) % count))
+    sibling = [(i, i ^ 1) for i in range(count)]
+    forwarded = [(lax.ppermute(part, "ctx", sibling), src ^ 1) for part, src in held]
+    full = jnp.zeros((block.shape[0], count * width, block.shape[2]), block.dtype)
+    for part, src in held + forwarded:
+        full = lax.dynamic_update_slice(full, part, (0, src * width, 0))
+    return full
+
+
 def on_device(tokens_in, norm_gain, proj_weight, conv_weight, decay_rate, residue, skip_gain):
     widened = tokens_in.astype(jnp.float32)
     mean_square = jnp.mean(widened * widened, axis=-1, keepdims=True)
@@ -22,7 +38,7 @@
     summed = jnp.einsum(
         "tf,ifc->itc",
         gathered,
-        lax.all_gather(proj_weight, "ctx", axis=1, tiled=True),
+        gathered_weight(proj_weight),
         preferred_element_type=jnp.float32,
     )
     projected = summed.astype(jnp.bfloat16)
@@ -62,12 +78,17 @@
 
     zero_state = jnp.zeros(decay_rate.shape, jnp.float32)
     local_end, starts = lax.scan(advance, zero_state, span_ends)
-    whole_decay = jnp.exp(-decay_rate * float(row_count))
-
-    def handoff(unused_turn, incoming):
-        return shifted(whole_decay * incoming + local_end, "ctx", 1)
-
-    incoming = lax.fori_loop(0, lax.axis_size("ctx") - 1, handoff, zero_state)
+    range_count = lax.axis_size("ctx")
+    range_idx = lax.axis_index("ctx")
+    all_ends = lax.all_gather(local_end, "ctx", axis=0)
+    earlier = jnp.arange(range_count)
+    lag = jnp.maximum(range_idx - 1 - earlier, 0).astype(jnp.float32)
+    lag_decay_ends = jnp.where(
+        (earlier < range_idx)[:, None, None],
+        jnp.exp(-decay_rate[None, :, :] * (float(row_count) * lag)[:, None, None]),
+        0.0,
+    )
+    incoming = jnp.sum(lag_decay_ends * all_ends, axis=0)
     span_starts = jnp.arange(span_count, dtype=jnp.float32) * float(span_rows)
     starts = (
         starts

time: 377 us -> 295 us (0.78)
  waiting for transfers between devices: 207 us -> 87.8 us
  local copies, waits for them, and re-layouts: 6.84 us -> 40.9 us
  starting transfers between devices: 30.7 us -> 8.17 us
  blocking collectives: 24.6 us -> 43.4 us
  other arithmetic: 14.5 us -> 20.8 us
    all_gather x1, waiting for transfers between devices: 141 us -> 32.2 us  [on_device(): gathered = lax.all_gather(normed, 'ch', axis=0, tiled=True)]
    all_gather x1 -> x0, waiting for transfers between devices: 59.4 us -> none  [on_device(): lax.all_gather(proj_weight, 'ctx', axis=1, tiled=True)]
    ppermute x0 -> x7, waiting for transfers between devices: none -> 55.6 us  [the longest x3 55.6 us: gathered_weight(): held.append((lax.ppermute(block, 'ctx', pairs), (me - by) % count))]
    ppermute x8 -> x1, starting transfers between devices: 30.6 us -> 1.47 us  [shifted(): return lax.ppermute(shard, axis, pairs)]
    all_gather x0 -> x1, blocking collectives: none -> 17.8 us  [on_device(): all_ends = lax.all_gather(local_end, 'ctx', axis=0)]
    ppermute x0 -> x7, local copies, waits for them, and re-layouts: none -> 14.8 us  [the longest x4 7.78 us: gathered_weight(): lax.ppermute(part, 'ctx', sibling)]
    dynamic_update_slice x0 -> x8, local copies, waits for them, and re-layouts: none -> 11.9 us  [gathered_weight(): full = lax.dynamic_update_slice(full, part, (0, src * width, 0))]
    ppermute x0 -> x7, starting transfers between devices: none -> 6.69 us  [the longest x3 5.73 us: gathered_weight(): held.append((lax.ppermute(block, 'ctx', pairs), (me - by) % count))]
  transfers between devices with their start and end apart: 10 -> 9, of which waited for: 9 -> 3; matrix products, arithmetic and copies ran while one was open for 4% -> 16% of each run, Pallas kernels for 0% -> 0%
where the time goes in v1:
time: 295 us; the launch traced here: 289 us
  waiting for transfers between devices  87.8 us (30%)
  matrix products  73.9 us (25%)
  blocking collectives  43.4 us (15%)
  local copies, waits for them, and re-layouts  40.9 us (14%)
  other arithmetic  20.8 us (7%)
  between operations  14 us (5%)
  starting transfers between devices  8.17 us (3%)
    ppermute x3, waiting for transfers between devices, gathered_weight(): held.append((lax.ppermute(block, 'ctx', pairs), (me - by) % count))  55.6 us
    dot_general x1, matrix products, on_device(): inside = jnp.einsum('cts,jsc->jtc', toeplitz, spans_in, precision=highest)  37.6 us
    all_gather x1, waiting for transfers between devices, on_device(): gathered = lax.all_gather(normed, 'ch', axis=0, tiled=True)  32.2 us
    all_to_all x1, blocking collectives, on_device(): return lax.all_to_all(gated, 'ch', split_axis=0, concat_axis=1, tiled=True)  25.6 us
    dot_general x1, matrix products, on_device(): jnp.einsum('tf,ifc->itc', gathered, gathered_weight(proj_weight), preferr...  18.8 us
    all_gather x1, blocking collectives, on_device(): all_ends = lax.all_gather(local_end, 'ctx', axis=0)  17.8 us
    dynamic_update_slice x8, local copies, waits for them, and re-layouts, gathered_weight(): full = lax.dynamic_update_slice(full, part, (0, src * width, 0))  11.9 us
    dot_general x1, matrix products, on_device(): toeplitz = jnp.einsum('lc,lts->cts', impulse, lag_table, precision=highest)  9.54 us
  transfers between devices with their start and end apart: 9, of which 3 were waited for; matrix products, arithmetic and copies ran while one was open for 16% of the time, Pallas kernels for 0%

profile of v1, /device:TPU:32, one launch (start us, length us, event | category | flops | bytes accessed | tf_op | source)
XLA Modules:
  0.0 289.1 jit_solution(12476396808286807811)
XLA Ops:
  7.9 2.0 fusion.40
  11.6 2.7 collective-permute-start.1
  17.8 1.7 multiply_reduce_fusion
  19.5 6.1 %broadcast_in_dim.15 = bf16[3,8192,256]{1,2,0:T(8,128)(2,1)} broadcast(bf16[]{:T(256)} %constant.30.clone.1), dimensions={} | broadcast | bytes 12582914 | tf_op jit(solution)/shard_map/broadcast_in_dim | solution.py:25
  26.8 21.0 %collective-permute-done = bf16[3,1024,256]{2,1,0:T(8,128)(2,1)} collective-permute-done((bf16[3,1024,256]{2,1,0:T(8,128)(2,1)}, bf16[3,1024,256]{2,1,0:T(8,128)(2,1)}, u32[]{:S(2)}, u32[]{:S(2)}) %collective-permute-start) | collective-permute-done | bytes 1572896 | tf_op jit(solution)/shard_map/ppermute | solution.py:22
  47.9 34.5 %collective-permute-done.1 = bf16[3,1024,256]{2,1,0:T(8,128)(2,1)} collective-permute-done((bf16[3,1024,256]{2,1,0:T(8,128)(2,1)}, bf16[3,1024,256]{2,1,0:T(8,128)(2,1)}, u32[]{:S(2)}, u32[]{:S(2)}) %collective-permute-start.1) | collective-permute-done | bytes 1572896 | tf_op jit(solution)/shard_map/ppermute | solution.py:22
  83.4 9.5 %fusion.4 = f32[256,128,128]{2,0,1:T(8,128)} fusion(s32[128,128]{1,0:T(8,128)S(1)} %iota_subtract_fusion, f32[128,256]{0,1:T(8,128)S(1)} %multiply_reduce_fusion), kind=kOutput, calls=%fused_computation.7 | convolution fusion | flops 6444548096 | bytes 16973824 | tf_op jit(solution)/shard_map/lc,lts->cts/dot_general | solution.py:67
  92.9 2.7 copy.41
  95.7 2.6 copy.42
  98.3 1.7 copy.43
  100.0 1.7 copy.44
  101.8 2.8 constant_dynamic-update-slice_fusion.6
  108.5 1.7 copy.45
  110.2 1.7 copy.46
  111.9 2.6 copy.47
  118.4 32.2 %all-gather.3.cloned.1.call-done = bf16[1024,8192]{1,0:T(8,128)(2,1)} async-done(((bf16[32,8192]{1,0:T(8,128)(2,1)}), bf16[1024,8192]{1,0:T(8,128)(2,1)}) %all-gather.3.cloned.1.call-update) | async-done | bytes 16777232 | tf_op jit(solution)/shard_map/all_gather | solution.py:35
  150.7 18.8 %fusion.23 = bf16[3,1024,256]{1,2,0:T(8,128)(2,1)S(1)} fusion(bf16[3,8192,256]{1,2,0:T(8,128)(2,1)} %constant_dynamic-update-slice_fusion, bf16[1024,8192]{1,0:T(8,128)(2,1)} %all-gather.3.cloned.1.call-done), kind=kOutput, calls=%fused_computation.33 | convolution fusion | flops 12885688320 | bytes 30932992 | tf_op jit(solution)/shard_map/tf,ifc->itc/dot_general | solution.py:38
  172.8 6.3 %fusion.6 = f32[3,1024,256]{1,2,0:T(8,128)S(1)} fusion(f32[3,1030,256]{1,2,0:T(8,128)S(1)} %maximum_convert_fusion, f32[3,256]{1,0:T(4,128)S(1)} %get-tuple-element.91, f32[3,256]{1,0:T(4,128)S(1)} %get-tuple-element.92, f32[3,256]{1,0:T(4,128)S(1)} %get-tuple-element.93, f32[3,256]{1,0:T(4,128)S(1)} %get-tuple-element.94, ...), kind=kLoop, calls=%fused_computation.10 | loop fusion | flops 10223616 | bytes 25187328 | tf_op jit(solution)/shard_map/add | solution.py:52
  180.9 4.0 %fusion.29 = f32[8,16,256]{1,0,2:T(8,128)S(1)} fusion(f32[8,128,256]{1,0,2:T(8,128)S(1)} %bitcast.62, f32[128]{0:T(128)S(1)} %iota_subtract_fusion.1, f32[16,256]{0,1:T(8,128)S(1)} %copy.53, f32[16,256]{0,1:T(8,128)S(1)} %copy.50), kind=kOutput, calls=%fused_computation.35 | convolution fusion | flops 51380224 | bytes 1212928 | tf_op jit(solution)/shard_map/jsc,msc->jmc/dot_general | solution.py:73
  185.3 5.0 %while.14 = (s32[]{:T(128)}, f32[16,256]{1,0:T(8,128)S(1)}, f32[8,16,256]{2,1,0:T(8,128)}, f32[16,256]{1,0:T(8,128)S(1)}, f32[8,16,256]{2,1,0:T(8,128)S(1)}) while((s32[]{:T(128)}, f32[16,256]{1,0:T(8,128)S(1)}, f32[8,16,256]{2,1,0:T(8,128)}, f32[16,256]{1,0:T(8,128)S(1)}, f32[8,16,256]{2,1,0:T(8,128)S(1)}) %tuple.41), condition=%wide.region_3.4_spmd.clone.clone, body=%wide.region_2.3_spmd.clone.sunk.clone | while | flops 16387 | bytes 98892 | solution.py:80
  190.2 17.8 %all-gather = f32[128,256]{1,0:T(8,128)S(1)} all-gather(f32[16,256]{1,0:T(8,128)S(1)} %get-tuple-element.34), channel_id=2, replica_groups=mesh['ctx'=8,'ch'=32] {'ctx'}, dimensions={0}, use_global_device_ids=true | all-gather | bytes 147456 | tf_op jit(solution)/shard_map/all_gather | solution.py:83
  209.6 37.6 %fusion.32 = f32[8,128,256]{1,0,2:T(8,128)S(1)} fusion(f32[8,128,256]{1,0,2:T(8,128)S(1)} %bitcast.63, f32[256,128,128]{2,0,1:T(8,128)} %fusion.4), kind=kOutput, calls=%fused_computation.36 | convolution fusion | flops 402653184 | bytes 18874368 | tf_op jit(solution)/shard_map/cts,jsc->jtc/dot_general | solution.py:69
  247.3 3.9 %fusion.35 = f32[8,128,256]{1,0,2:T(8,128)} fusion(f32[8,128,256]{1,0,2:T(8,128)S(1)} %fusion.32, f32[8,16,256]{1,0,2:T(8,128)S(1)} %copy.55, f32[128]{0:T(128)S(1)} %iota_add_fusion, f32[16,256]{0,1:T(8,128)S(1)} %copy-done.4, f32[16,256]{0,1:T(8,128)S(1)} %copy.50), kind=kOutput, calls=%fused_computation.37 | convolution fusion | flops 51642368 | bytes 2261504 | tf_op jit(solution)/shard_map/jmc,mtc->jtc/dot_general | solution.py:100
  255.6 25.6 %all_to_all.16 = bf16[32,32,256]{2,1,0:T(8,128)(2,1)S(1)} all-to-all(bf16[32,32,256]{2,1,0:T(8,128)(2,1)S(1)} %multiply_convert_fusion), channel_id=1, replica_groups=mesh['ctx'=8,'ch'=32] {'ch'}, dimensions={0} | all-to-all | bytes 1048576 | tf_op jit(solution)/shard_map/all_to_all | solution.py:103
  (88 shorter events, 33.4 us)
Async XLA Ops:
  6.5 10.0 %copy-start.3 = (bf16[3,1024,256]{2,1,0:T(8,128)(2,1)S(1)}, bf16[3,1024,256]{2,1,0:T(8,128)(2,1)}, u32[]{:S(2)}) copy-start(bf16[3,1024,256]{2,1,0:T(8,128)(2,1)} %param.11) | copy-start | bytes 4718596
  6.5 144.1 %all-gather.3.cloned.1.call-start = ((), (), s32[]{:S(2)}) async-start(), calls=%async_computation.1 | async-start | bytes 17301504 | tf_op jit(solution)/shard_map/all_gather | solution.py:35
  7.9 11.5 %copy-start.6 = (f32[3,7,256]{2,1,0:T(8,128)S(1)}, f32[3,7,256]{2,1,0:T(8,128)}, u32[]{:S(2)}) copy-start(f32[3,7,256]{2,1,0:T(8,128)} %param.12) | copy-start | bytes 64516
  10.0 37.9 %collective-permute-start = (bf16[3,1024,256]{2,1,0:T(8,128)(2,1)}, bf16[3,1024,256]{2,1,0:T(8,128)(2,1)}, u32[]{:S(2)}, u32[]{:S(2)}) collective-permute-start(bf16[3,1024,256]{2,1,0:T(8,128)(2,1)} %param.11), channel_id=1, source_target_pairs={{0,64},{32,96},{64,128},{96,160},{128,192},{160,224},{192,0},{224,... | collective-permute-start | bytes 4718600 | tf_op jit(solution)/shard_map/ppermute | solution.py:22
  11.6 70.9 %collective-permute-start.1 = (bf16[3,1024,256]{2,1,0:T(8,128)(2,1)}, bf16[3,1024,256]{2,1,0:T(8,128)(2,1)}, u32[]{:S(2)}, u32[]{:S(2)}) collective-permute-start(bf16[3,1024,256]{2,1,0:T(8,128)(2,1)} %param.11), channel_id=1, source_target_pairs={{0,128},{32,160},{64,192},{96,224},{128,0},{160,32},{192,64},{224,... | collective-permute-start | bytes 4718600 | tf_op jit(solution)/shard_map/ppermute | solution.py:22
  14.3 68.1 %collective-permute-start.2 = (bf16[3,1024,256]{2,1,0:T(8,128)(2,1)}, bf16[3,1024,256]{2,1,0:T(8,128)(2,1)}, u32[]{:S(2)}, u32[]{:S(2)}) collective-permute-start(bf16[3,1024,256]{2,1,0:T(8,128)(2,1)} %param.11), channel_id=1, source_target_pairs={{0,192},{32,224},{64,0},{96,32},{128,64},{160,96},{192,128},{224,1... | collective-permute-start | bytes 4718600 | tf_op jit(solution)/shard_map/ppermute | solution.py:22
  15.7 84.3 %collective-permute-start.3 = (bf16[3,1024,256]{2,1,0:T(8,128)(2,1)}, bf16[3,1024,256]{2,1,0:T(8,128)(2,1)}, u32[]{:S(2)}, u32[]{:S(2)}) collective-permute-start(bf16[3,1024,256]{2,1,0:T(8,128)(2,1)} %param.11), channel_id=1, source_target_pairs={{0,32},{32,0},{64,96},{96,64},{128,160},{160,128},{192,224},{224,1... | collective-permute-start | bytes 4718600 | tf_op jit(solution)/shard_map/ppermute | solution.py:24
  47.9 60.6 %collective-permute-start.4 = (bf16[3,1024,256]{2,1,0:T(8,128)(2,1)}, bf16[3,1024,256]{2,1,0:T(8,128)(2,1)}, u32[]{:S(2)}, u32[]{:S(2)}) collective-permute-start(bf16[3,1024,256]{2,1,0:T(8,128)(2,1)} %collective-permute-done), channel_id=1, source_target_pairs={{0,32},{32,0},{64,96},{96,64},{128,160},{160,128},{192,224},{224,1... | collective-permute-start | bytes 4718600 | tf_op jit(solution)/shard_map/ppermute | solution.py:24
  82.4 27.8 %collective-permute-start.5 = (bf16[3,1024,256]{2,1,0:T(8,128)(2,1)}, bf16[3,1024,256]{2,1,0:T(8,128)(2,1)}, u32[]{:S(2)}, u32[]{:S(2)}) collective-permute-start(bf16[3,1024,256]{2,1,0:T(8,128)(2,1)} %collective-permute-done.1), channel_id=1, source_target_pairs={{0,32},{32,0},{64,96},{96,64},{128,160},{160,128},{192,224},{224,1... | collective-permute-start | bytes 4718600 | tf_op jit(solution)/shard_map/ppermute | solution.py:24
  82.4 29.5 %collective-permute-start.6 = (bf16[3,1024,256]{2,1,0:T(8,128)(2,1)}, bf16[3,1024,256]{2,1,0:T(8,128)(2,1)}, u32[]{:S(2)}, u32[]{:S(2)}) collective-permute-start(bf16[3,1024,256]{2,1,0:T(8,128)(2,1)} %collective-permute-done.2), channel_id=1, source_target_pairs={{0,32},{32,0},{64,96},{96,64},{128,160},{160,128},{192,224},{224,1... | collective-permute-start | bytes 4718600 | tf_op jit(solution)/shard_map/ppermute | solution.py:24
  101.8 2.8 copy-start
  114.5 2.6 copy-start.1
  118.4 52.7 %copy-start.5 = (f32[16,256]{1,0:T(8,128)S(1)}, f32[16,256]{1,0:T(8,128)}, u32[]{:S(2)}) copy-start(f32[16,256]{1,0:T(8,128)} %param.14) | copy-start | bytes 49156
  169.6 2.4 collective-permute-start.7
  209.6 37.7 %copy-start.4 = (f32[16,256]{0,1:T(8,128)S(1)}, f32[16,256]{0,1:T(8,128)}, u32[]{:S(2)}) copy-start(f32[16,256]{0,1:T(8,128)} %copy.52) | copy-start | bytes 49156
  247.2 6.8 %copy-start.2 = (f32[1,1024,256]{2,1,0:T(8,128)S(1)}, f32[1,1024,256]{2,1,0:T(8,128)}, u32[]{:S(2)}) copy-start(f32[1,1024,256]{2,1,0:T(8,128)} %copy.57) | copy-start | bytes 3145732
  247.2 6.8 %copy-start.7 = (f32[256]{0:T(256)S(1)}, f32[256]{0:T(256)}, u32[]{:S(2)}) copy-start(f32[256]{0:T(256)} %param.15) | copy-start | bytes 3076
Sparse Core Ops, SparseCore 0:
  10.1 140.5 all-gather.2

commit v2 on v1

--- a/solution.py
+++ b/solution.py
@@ -28,7 +28,7 @@
     return full
 
 
-def on_device(tokens_in, norm_gain, proj_weight, conv_weight, decay_rate, residue, skip_gain):
+def on_device_body(tokens_in, norm_gain, proj_weight, conv_weight, decay_rate, residue, skip_gain):
     widened = tokens_in.astype(jnp.float32)
     mean_square = jnp.mean(widened * widened, axis=-1, keepdims=True)
     normed = (widened * lax.rsqrt(mean_square + norm_eps) * norm_gain[None, :]).astype(jnp.bfloat16)
@@ -56,21 +56,25 @@
     queries = featured[0]
     mixed = featured[1] * featured[2]
     highest = lax.Precision.HIGHEST
+    high = lax.Precision.HIGH
     in_scale = jnp.sqrt(-jnp.expm1(-2.0 * decay_rate))
     span_rows = min(128, row_count)
     span_count = row_count // span_rows
     positions = jnp.arange(span_rows, dtype=jnp.float32)
-    lag_decay = jnp.exp(-decay_rate[:, None, :] * positions[None, :, None])
-    impulse = jnp.sum((residue * in_scale)[:, None, :] * lag_decay, axis=0)
+    own_rate, own_residue = lax.optimization_barrier((decay_rate, residue))
+    own_scale = jnp.sqrt(-jnp.expm1(-2.0 * own_rate))
+    lag_decay = jnp.exp(-own_rate[:, None, :] * positions[None, :, None])
+    impulse = jnp.sum((own_residue * own_scale)[:, None, :] * lag_decay, axis=0)
     offsets = jnp.arange(span_rows)[:, None] - jnp.arange(span_rows)[None, :]
     lag_table = (offsets[None, :, :] == jnp.arange(span_rows)[:, None, None]).astype(jnp.float32)
     toeplitz = jnp.einsum("lc,lts->cts", impulse, lag_table, precision=highest)
+    toeplitz = lax.optimization_barrier(toeplitz)
     spans_in = mixed.reshape(span_count, span_rows, chan_count)
-    inside = jnp.einsum("cts,jsc->jtc", toeplitz, spans_in, precision=highest)
+    inside = jnp.einsum("cts,jsc->jtc", toeplitz, spans_in, precision=high)
     end_weight = in_scale[:, None, :] * jnp.exp(
         -decay_rate[:, None, :] * (span_rows - 1.0 - positions)[None, :, None]
     )
-    span_ends = jnp.einsum("jsc,msc->jmc", spans_in, end_weight, precision=highest)
+    span_ends = jnp.einsum("jsc,msc->jmc", spans_in, end_weight, precision=high)
     span_decay = jnp.exp(-decay_rate * float(span_rows))
 
     def advance(carried, span_end):
@@ -78,17 +82,10 @@
 
     zero_state = jnp.zeros(decay_rate.shape, jnp.float32)
     local_end, starts = lax.scan(advance, zero_state, span_ends)
-    range_count = lax.axis_size("ctx")
-    range_idx = lax.axis_index("ctx")
-    all_ends = lax.all_gather(local_end, "ctx", axis=0)
-    earlier = jnp.arange(range_count)
-    lag = jnp.maximum(range_idx - 1 - earlier, 0).astype(jnp.float32)
-    lag_decay_ends = jnp.where(
-        (earlier < range_idx)[:, None, None],
-        jnp.exp(-decay_rate[None, :, :] * (float(row_count) * lag)[:, None, None]),
-        0.0,
-    )
-    incoming = jnp.sum(lag_decay_ends * all_ends, axis=0)
+    incoming = zero_state
+    for by in range(1, lax.axis_size("ctx")):
+        carried_end = shifted(local_end, "ctx", by)
+        incoming = incoming + jnp.exp(-decay_rate * float(row_count * (by - 1))) * carried_end
     span_starts = jnp.arange(span_count, dtype=jnp.float32) * float(span_rows)
     starts = (
         starts
@@ -97,7 +94,7 @@
     out_weight = residue[:, None, :] * jnp.exp(
         -decay_rate[:, None, :] * (positions + 1.0)[None, :, None]
     )
-    outside = jnp.einsum("jmc,mtc->jtc", starts, out_weight, precision=highest)
+    outside = jnp.einsum("jmc,mtc->jtc", starts, out_weight, precision=high)
     filtered = (inside + outside).reshape(row_count, chan_count)
     gated = (queries * (filtered + skip_gain[None, :] * mixed)).astype(jnp.bfloat16)
     return lax.all_to_all(gated, "ch", split_axis=0, concat_axis=1, tiled=True)
@@ -115,5 +112,5 @@
     )
     out_specs = P(("ctx", "ch"), None)
     return jax.shard_map(
-        on_device, mesh=mesh, in_specs=in_specs, out_specs=out_specs, check_vma=False
+        on_device_body, mesh=mesh, in_specs=in_specs, out_specs=out_specs, check_vma=False
     )

time: 295 us -> 275 us (0.932); the launches traced: 289 us -> 274 us
  blocking collectives: 43.4 us -> 24.7 us
  starting transfers between devices: 8.17 us -> 25.7 us
  matrix products: 73.9 us -> 61.5 us
  waiting for transfers between devices: 87.8 us -> 91 us
  other arithmetic: 20.8 us -> 17.7 us
    ppermute x1 -> x8, starting transfers between devices: 1.47 us -> 19.4 us  [shifted(): return lax.ppermute(shard, axis, pairs)]
    all_gather x1 -> x0, blocking collectives: 17.8 us -> none  [on_device(): all_ends = lax.all_gather(local_end, 'ctx', axis=0)]
    dot_general x5, matrix products: 73.9 us -> 61.5 us  [the longest x1 25 us: on_device_body(): inside = jnp.einsum('cts,jsc->jtc', toeplitz, spans_in, precision=high)]
    add x3 -> x4, other arithmetic: 7.33 us -> 7.36 us  [the longest x1 6.32 us: on_device_body(): featured + conv_weight[:, shift_idx, None, :] * padded[:, reach - shift_i...]
  transfers between devices with their start and end apart: 9 -> 16, of which waited for: 3 -> 4; matrix products, arithmetic and copies ran while one was open for 16% -> 26% of each run, Pallas kernels for 0% -> 0%
where the time goes in v2:
time: 275 us; the launch traced here: 274 us
  waiting for transfers between devices  91 us (33%)
  matrix products  61.5 us (22%)
  local copies, waits for them, and re-layouts  40 us (15%)
  starting transfers between devices  25.7 us (9%)
  blocking collectives  24.7 us (9%)
  other arithmetic  17.7 us (6%)
  between operations  13.8 us (5%)
    ppermute x3, waiting for transfers between devices, gathered_weight(): held.append((lax.ppermute(block, 'ctx', pairs), (me - by) % count))  58 us
    all_gather x1, waiting for transfers between devices, on_device_body(): gathered = lax.all_gather(normed, 'ch', axis=0, tiled=True)  32.4 us
    dot_general x1, matrix products, on_device_body(): inside = jnp.einsum('cts,jsc->jtc', toeplitz, spans_in, precision=high)  25 us
    all_to_all x1, blocking collectives, on_device_body(): return lax.all_to_all(gated, 'ch', split_axis=0, concat_axis=1, tiled=True)  24.7 us
    ppermute x8, starting transfers between devices, shifted(): return lax.ppermute(shard, axis, pairs)  19.4 us
    dot_general x1, matrix products, on_device_body(): jnp.einsum('tf,ifc->itc', gathered, gathered_weight(proj_weight), preferr...  18.8 us
    dynamic_update_slice x8, local copies, waits for them, and re-layouts, gathered_weight(): full = lax.dynamic_update_slice(full, part, (0, src * width, 0))  11.9 us
    dot_general x1, matrix products, on_device_body(): toeplitz = jnp.einsum('lc,lts->cts', impulse, lag_table, precision=highest)  9.65 us
  transfers between devices with their start and end apart: 16, of which 4 were waited for; matrix products, arithmetic and copies ran while one was open for 26% of the time, Pallas kernels for 0%

profile of v2, /device:TPU:32, one launch (start us, length us, event | category | flops | bytes accessed | tf_op | source)
XLA Modules:
  0.0 274.4 jit_solution(734198381193768150)
XLA Ops:
  8.0 2.0 fusion.40
  11.6 2.7 collective-permute-start.1
  17.1 6.0 %broadcast_in_dim.7 = bf16[3,8192,256]{1,2,0:T(8,128)(2,1)} broadcast(bf16[]{:T(256)} %constant.31.clone.1), dimensions={} | broadcast | bytes 12582914 | tf_op jit(solution)/shard_map/broadcast_in_dim | solution.py:25
  24.4 23.5 %collective-permute-done = bf16[3,1024,256]{2,1,0:T(8,128)(2,1)} collective-permute-done((bf16[3,1024,256]{2,1,0:T(8,128)(2,1)}, bf16[3,1024,256]{2,1,0:T(8,128)(2,1)}, u32[]{:S(2)}, u32[]{:S(2)}) %collective-permute-start) | collective-permute-done | bytes 1572896 | tf_op jit(solution)/shard_map/ppermute | solution.py:22
  47.9 34.5 %collective-permute-done.1 = bf16[3,1024,256]{2,1,0:T(8,128)(2,1)} collective-permute-done((bf16[3,1024,256]{2,1,0:T(8,128)(2,1)}, bf16[3,1024,256]{2,1,0:T(8,128)(2,1)}, u32[]{:S(2)}, u32[]{:S(2)}) %collective-permute-start.1) | collective-permute-done | bytes 1572896 | tf_op jit(solution)/shard_map/ppermute | solution.py:22
  83.0 9.7 %fusion.4 = f32[256,128,128]{2,0,1:T(8,128)} fusion(s32[128,128]{1,0:T(8,128)S(1)} %iota_subtract_fusion, f32[128,256]{1,0:T(8,128)S(1)} %multiply_reduce_fusion), kind=kOutput, calls=%fused_computation.7 | convolution fusion | flops 6444548096 | bytes 16973824 | tf_op jit(solution)/shard_map/lc,lts->cts/dot_general | solution.py:70
  92.6 2.8 %copy.57 = bf16[3,1024,256]{1,2,0:T(8,128)(2,1)} copy(bf16[3,1024,256]{2,1,0:T(8,128)(2,1)} %collective-permute-done) | data formatting | bytes 3145728 | tf_op jit(solution)/shard_map/ppermute | solution.py:22
  95.4 2.6 copy.58
  98.0 1.7 copy.59
  99.8 1.7 copy.60
  101.5 2.8 %constant_dynamic-update-slice_fusion.6 = bf16[3,8192,256]{1,2,0:T(8,128)(2,1)} fusion(bf16[3,8192,256]{1,2,0:T(8,128)(2,1)} %constant_dynamic-update-slice_fusion.7, bf16[3,1024,256]{1,2,0:T(8,128)(2,1)} %copy.57, s32[]{:T(128)S(6)} %select_n.41), kind=kLoop, calls=%fused_computation.71 | loop fusion | bytes 3145732 | tf_op jit(solution)/shard_map/dynamic_update_slice | solution.py:27
  108.3 1.7 copy.61
  110.0 1.7 copy.62
  111.8 2.6 copy.63
  118.3 32.4 %all-gather.2.cloned.1.call-done = bf16[1024,8192]{1,0:T(8,128)(2,1)} async-done(((bf16[32,8192]{1,0:T(8,128)(2,1)}), bf16[1024,8192]{1,0:T(8,128)(2,1)}) %all-gather.2.cloned.1.call-update) | async-done | bytes 16777232 | tf_op jit(solution)/shard_map/all_gather | solution.py:35
  150.7 18.8 %fusion.23 = bf16[3,1024,256]{1,2,0:T(8,128)(2,1)S(1)} fusion(bf16[3,8192,256]{1,2,0:T(8,128)(2,1)} %constant_dynamic-update-slice_fusion, bf16[1024,8192]{1,0:T(8,128)(2,1)} %all-gather.2.cloned.1.call-done), kind=kOutput, calls=%fused_computation.33 | convolution fusion | flops 12885688320 | bytes 30932992 | tf_op jit(solution)/shard_map/tf,ifc->itc/dot_general | solution.py:38
  172.8 6.3 %fusion.6 = f32[3,1024,256]{1,2,0:T(8,128)S(1)} fusion(f32[3,1030,256]{1,2,0:T(8,128)S(1)} %maximum_convert_fusion, f32[3,256]{1,0:T(4,128)S(1)} %get-tuple-element.101, f32[3,256]{1,0:T(4,128)S(1)} %get-tuple-element.102, f32[3,256]{1,0:T(4,128)S(1)} %get-tuple-element.103, f32[3,256]{1,0:T(4,128)S(1)} %get-tuple-element.104, ...), kind=kLoop, calls=%fused_computation.10 | loop fusion | flops 10223616 | bytes 25187328 | tf_op jit(solution)/shard_map/add | solution.py:52
  179.7 3.5 %fusion.29 = f32[8,16,256]{1,0,2:T(8,128)} fusion(f32[8,128,256]{1,0,2:T(8,128)S(1)} %bitcast.59, f32[128]{0:T(128)S(1)} %iota_subtract_fusion.1, f32[16,256]{0,1:T(8,128)S(1)} %copy.69, f32[16,256]{0,1:T(8,128)S(1)} %copy.68), kind=kOutput, calls=%fused_computation.35 | convolution fusion | flops 26214400 | bytes 1212928 | tf_op jit(solution)/shard_map/jsc,msc->jmc/dot_general | solution.py:77
  184.8 4.9 %while.13 = (s32[]{:T(128)}, f32[16,256]{1,0:T(8,128)S(1)}, f32[8,16,256]{2,1,0:T(8,128)}, f32[16,256]{1,0:T(8,128)S(1)}, f32[8,16,256]{2,1,0:T(8,128)S(1)}, /*index=5*/s32[]{:T(128)}, s32[]{:T(128)}) while((s32[]{:T(128)}, f32[16,256]{1,0:T(8,128)S(1)}, f32[8,16,256]{2,1,0:T(8,128)}, f32[16,256]{1,0:T(8,128)S(1)}, ...), condition=%wide.region_3.4_spmd.clone, body=%wide.region_2.3_spmd.clone.sunk | while | flops 16387 | bytes 98908 | solution.py:84
  189.7 6.7 %collective-permute-start.10 = (f32[16,256]{1,0:T(8,128)S(1)}, f32[16,256]{1,0:T(8,128)S(1)}, u32[]{:S(2)}, u32[]{:S(2)}) collective-permute-start(f32[16,256]{1,0:T(8,128)S(1)} %get-tuple-element.38), channel_id=1, source_target_pairs={{0,96},{32,128},{64,160},{96,192},{128,224},{1,97},{33,129},{65,16... | collective-permute-start | bytes 49160 | tf_op jit(solution)/shard_map/ppermute | solution.py:12
  196.4 4.7 %collective-permute-start.11 = (f32[16,256]{1,0:T(8,128)S(1)}, f32[16,256]{1,0:T(8,128)S(1)}, u32[]{:S(2)}, u32[]{:S(2)}) collective-permute-start(f32[16,256]{1,0:T(8,128)S(1)} %get-tuple-element.38), channel_id=1, source_target_pairs={{0,128},{32,160},{64,192},{96,224},{1,129},{33,161},{65,193},{97,2... | collective-permute-start | bytes 49160 | tf_op jit(solution)/shard_map/ppermute | solution.py:12
  208.4 25.0 %fusion.32 = f32[8,128,256]{1,0,2:T(8,128)} fusion(f32[8,128,256]{1,0,2:T(8,128)S(1)} %bitcast.60, f32[256,128,128]{2,0,1:T(8,128)} %fusion.4), kind=kOutput, calls=%fused_computation.36 | convolution fusion | flops 201326592 | bytes 18874368 | tf_op jit(solution)/shard_map/cts,jsc->jtc/dot_general | solution.py:73
  235.7 4.4 %fusion.35 = f32[8,128,256]{1,0,2:T(8,128)} fusion(f32[8,128,256]{1,0,2:T(8,128)} %fusion.32, f32[8,16,256]{1,0,2:T(8,128)S(1)} %copy.71, f32[128]{0:T(128)S(1)} %iota_add_fusion, f32[16,256]{0,1:T(8,128)S(1)} %copy.68, f32[16,256]{0,1:T(8,128)} %copy.67), kind=kOutput, calls=%fused_computation.37 | convolution fusion | flops 26476544 | bytes 2261504 | tf_op jit(solution)/shard_map/jmc,mtc->jtc/dot_general | solution.py:97
  242.0 24.7 %all_to_all.16 = bf16[32,32,256]{2,1,0:T(8,128)(2,1)S(1)} all-to-all(bf16[32,32,256]{2,1,0:T(8,128)(2,1)S(1)} %multiply_convert_fusion), channel_id=1, replica_groups=mesh['ctx'=8,'ch'=32] {'ch'}, dimensions={0} | all-to-all | bytes 1048576 | tf_op jit(solution)/shard_map/all_to_all | solution.py:100
  (97 shorter events, 37.7 us)
Async XLA Ops:
  6.5 9.2 %copy-start.2 = (bf16[3,1024,256]{2,1,0:T(8,128)(2,1)S(1)}, bf16[3,1024,256]{2,1,0:T(8,128)(2,1)}, u32[]{:S(2)}) copy-start(bf16[3,1024,256]{2,1,0:T(8,128)(2,1)} %param.11) | copy-start | bytes 4718596
  6.5 10.1 %copy-start.3 = (f32[16,256]{1,0:T(8,128)S(1)}, f32[16,256]{1,0:T(8,128)}, u32[]{:S(2)}) copy-start(f32[16,256]{1,0:T(8,128)} %param.13) | copy-start | bytes 49156
  6.5 10.1 %copy-start.4 = (f32[16,256]{1,0:T(8,128)S(1)}, f32[16,256]{1,0:T(8,128)}, u32[]{:S(2)}) copy-start(f32[16,256]{1,0:T(8,128)} %param.14) | copy-start | bytes 49156
  6.5 10.5 %copy-start.5 = (f32[3,7,256]{2,1,0:T(8,128)S(1)}, f32[3,7,256]{2,1,0:T(8,128)}, u32[]{:S(2)}) copy-start(f32[3,7,256]{2,1,0:T(8,128)} %param.12) | copy-start | bytes 64516
  6.5 144.2 %all-gather.2.cloned.1.call-start = ((), (), s32[]{:S(2)}) async-start(), calls=%async_computation.1 | async-start | bytes 17301504 | tf_op jit(solution)/shard_map/all_gather | solution.py:35
  10.0 37.9 %collective-permute-start = (bf16[3,1024,256]{2,1,0:T(8,128)(2,1)}, bf16[3,1024,256]{2,1,0:T(8,128)(2,1)}, u32[]{:S(2)}, u32[]{:S(2)}) collective-permute-start(bf16[3,1024,256]{2,1,0:T(8,128)(2,1)} %param.11), channel_id=1, source_target_pairs={{0,64},{32,96},{64,128},{96,160},{128,192},{160,224},{192,0},{224,... | collective-permute-start | bytes 4718600 | tf_op jit(solution)/shard_map/ppermute | solution.py:22
  11.6 70.9 %collective-permute-start.1 = (bf16[3,1024,256]{2,1,0:T(8,128)(2,1)}, bf16[3,1024,256]{2,1,0:T(8,128)(2,1)}, u32[]{:S(2)}, u32[]{:S(2)}) collective-permute-start(bf16[3,1024,256]{2,1,0:T(8,128)(2,1)} %param.11), channel_id=1, source_target_pairs={{0,128},{32,160},{64,192},{96,224},{128,0},{160,32},{192,64},{224,... | collective-permute-start | bytes 4718600 | tf_op jit(solution)/shard_map/ppermute | solution.py:22
  14.3 68.1 %collective-permute-start.2 = (bf16[3,1024,256]{2,1,0:T(8,128)(2,1)}, bf16[3,1024,256]{2,1,0:T(8,128)(2,1)}, u32[]{:S(2)}, u32[]{:S(2)}) collective-permute-start(bf16[3,1024,256]{2,1,0:T(8,128)(2,1)} %param.11), channel_id=1, source_target_pairs={{0,192},{32,224},{64,0},{96,32},{128,64},{160,96},{192,128},{224,1... | collective-permute-start | bytes 4718600 | tf_op jit(solution)/shard_map/ppermute | solution.py:22
  15.7 84.0 %collective-permute-start.3 = (bf16[3,1024,256]{2,1,0:T(8,128)(2,1)}, bf16[3,1024,256]{2,1,0:T(8,128)(2,1)}, u32[]{:S(2)}, u32[]{:S(2)}) collective-permute-start(bf16[3,1024,256]{2,1,0:T(8,128)(2,1)} %param.11), channel_id=1, source_target_pairs={{0,32},{32,0},{64,96},{96,64},{128,160},{160,128},{192,224},{224,1... | collective-permute-start | bytes 4718600 | tf_op jit(solution)/shard_map/ppermute | solution.py:24
  47.9 60.4 %collective-permute-start.4 = (bf16[3,1024,256]{2,1,0:T(8,128)(2,1)}, bf16[3,1024,256]{2,1,0:T(8,128)(2,1)}, u32[]{:S(2)}, u32[]{:S(2)}) collective-permute-start(bf16[3,1024,256]{2,1,0:T(8,128)(2,1)} %collective-permute-done), channel_id=1, source_target_pairs={{0,32},{32,0},{64,96},{96,64},{128,160},{160,128},{192,224},{224,1... | collective-permute-start | bytes 4718600 | tf_op jit(solution)/shard_map/ppermute | solution.py:24
  82.4 27.5 %collective-permute-start.5 = (bf16[3,1024,256]{2,1,0:T(8,128)(2,1)}, bf16[3,1024,256]{2,1,0:T(8,128)(2,1)}, u32[]{:S(2)}, u32[]{:S(2)}) collective-permute-start(bf16[3,1024,256]{2,1,0:T(8,128)(2,1)} %collective-permute-done.1), channel_id=1, source_target_pairs={{0,32},{32,0},{64,96},{96,64},{128,160},{160,128},{192,224},{224,1... | collective-permute-start | bytes 4718600 | tf_op jit(solution)/shard_map/ppermute | solution.py:24
  82.4 29.3 %collective-permute-start.6 = (bf16[3,1024,256]{2,1,0:T(8,128)(2,1)}, bf16[3,1024,256]{2,1,0:T(8,128)(2,1)}, u32[]{:S(2)}, u32[]{:S(2)}) collective-permute-start(bf16[3,1024,256]{2,1,0:T(8,128)(2,1)} %collective-permute-done.2), channel_id=1, source_target_pairs={{0,32},{32,0},{64,96},{96,64},{128,160},{160,128},{192,224},{224,1... | collective-permute-start | bytes 4718600 | tf_op jit(solution)/shard_map/ppermute | solution.py:24
  101.5 2.9 %copy-start = (bf16[3,1024,256]{1,2,0:T(8,128)(2,1)S(1)}, bf16[3,1024,256]{1,2,0:T(8,128)(2,1)}, u32[]{:S(2)}) copy-start(bf16[3,1024,256]{1,2,0:T(8,128)(2,1)} %copy.58) | copy-start | bytes 4718596
  114.4 2.6 copy-start.1
  169.7 2.4 collective-permute-start.7
  189.7 16.1 %collective-permute-start.10 = (f32[16,256]{1,0:T(8,128)S(1)}, f32[16,256]{1,0:T(8,128)S(1)}, u32[]{:S(2)}, u32[]{:S(2)}) collective-permute-start(f32[16,256]{1,0:T(8,128)S(1)} %get-tuple-element.38), channel_id=1, source_target_pairs={{0,96},{32,128},{64,160},{96,192},{128,224},{1,97},{33,129},{65,16... | collective-permute-start | bytes 49160 | tf_op jit(solution)/shard_map/ppermute | solution.py:12
  196.4 10.7 %collective-permute-start.11 = (f32[16,256]{1,0:T(8,128)S(1)}, f32[16,256]{1,0:T(8,128)S(1)}, u32[]{:S(2)}, u32[]{:S(2)}) collective-permute-start(f32[16,256]{1,0:T(8,128)S(1)} %get-tuple-element.38), channel_id=1, source_target_pairs={{0,128},{32,160},{64,192},{96,224},{1,129},{33,161},{65,193},{97,2... | collective-permute-start | bytes 49160 | tf_op jit(solution)/shard_map/ppermute | solution.py:12
  201.9 32.2 %collective-permute-start.12 = (f32[16,256]{1,0:T(8,128)S(1)}, f32[16,256]{1,0:T(8,128)S(1)}, u32[]{:S(2)}, u32[]{:S(2)}) collective-permute-start(f32[16,256]{1,0:T(8,128)S(1)} %get-tuple-element.38), channel_id=1, source_target_pairs={{0,160},{32,192},{64,224},{1,161},{33,193},{65,225},{2,162},{34,19... | collective-permute-start | bytes 49160 | tf_op jit(solution)/shard_map/ppermute | solution.py:12
  203.2 30.9 %collective-permute-start.13 = (f32[16,256]{1,0:T(8,128)S(1)}, f32[16,256]{1,0:T(8,128)S(1)}, u32[]{:S(2)}, u32[]{:S(2)}) collective-permute-start(f32[16,256]{1,0:T(8,128)S(1)} %get-tuple-element.38), channel_id=1, source_target_pairs={{0,192},{32,224},{1,193},{33,225},{2,194},{34,226},{3,195},{35,227... | collective-permute-start | bytes 49160 | tf_op jit(solution)/shard_map/ppermute | solution.py:12
  204.5 29.6 %collective-permute-start.14 = (f32[16,256]{1,0:T(8,128)S(1)}, f32[16,256]{1,0:T(8,128)S(1)}, u32[]{:S(2)}, u32[]{:S(2)}) collective-permute-start(f32[16,256]{1,0:T(8,128)S(1)} %get-tuple-element.38), channel_id=1, source_target_pairs={{0,224},{1,225},{2,226},{3,227},{4,228},{5,229},{6,230},{7,231},{8... | collective-permute-start | bytes 49160 | tf_op jit(solution)/shard_map/ppermute | solution.py:12
  205.8 28.3 %collective-permute-start.8 = (f32[16,256]{1,0:T(8,128)S(1)}, f32[16,256]{1,0:T(8,128)S(1)}, u32[]{:S(2)}, u32[]{:S(2)}) collective-permute-start(f32[16,256]{1,0:T(8,128)S(1)} %get-tuple-element.38), channel_id=1, source_target_pairs={{0,32},{32,64},{64,96},{96,128},{128,160},{160,192},{192,224},{1,3... | collective-permute-start | bytes 49160 | tf_op jit(solution)/shard_map/ppermute | solution.py:12
  207.1 27.1 %collective-permute-start.9 = (f32[16,256]{1,0:T(8,128)S(1)}, f32[16,256]{1,0:T(8,128)S(1)}, u32[]{:S(2)}, u32[]{:S(2)}) collective-permute-start(f32[16,256]{1,0:T(8,128)S(1)} %get-tuple-element.38), channel_id=1, source_target_pairs={{0,64},{32,96},{64,128},{96,160},{128,192},{160,224},{1,65},{33,97... | collective-permute-start | bytes 49160 | tf_op jit(solution)/shard_map/ppermute | solution.py:12
  235.7 6.0 %copy-start.6 = (f32[256]{0:T(256)S(1)}, f32[256]{0:T(256)}, u32[]{:S(2)}) copy-start(f32[256]{0:T(256)} %param.15) | copy-start | bytes 3076
Sparse Core Ops, SparseCore 0:
  10.1 140.5 all-gather.1

commit v3 on v2

--- a/solution.py
+++ b/solution.py
@@ -32,14 +32,17 @@
     widened = tokens_in.astype(jnp.float32)
     mean_square = jnp.mean(widened * widened, axis=-1, keepdims=True)
     normed = (widened * lax.rsqrt(mean_square + norm_eps) * norm_gain[None, :]).astype(jnp.bfloat16)
-    gathered = lax.all_gather(normed, "ch", axis=0, tiled=True)
-    row_count = gathered.shape[0]
+    feature_count = normed.shape[1]
+    half = feature_count // 2
+    gathered_lo = lax.all_gather(normed[:, :half], "ch", axis=0, tiled=True)
+    gathered_hi = lax.all_gather(normed[:, half:], "ch", axis=0, tiled=True)
+    row_count = gathered_lo.shape[0]
     chan_count = proj_weight.shape[2]
+    weight = gathered_weight(proj_weight)
     summed = jnp.einsum(
-        "tf,ifc->itc",
-        gathered,
-        gathered_weight(proj_weight),
-        preferred_element_type=jnp.float32,
+        "tf,ifc->itc", gathered_lo, weight[:, :half], preferred_element_type=jnp.float32
+    ) + jnp.einsum(
+        "tf,ifc->itc", gathered_hi, weight[:, half:], preferred_element_type=jnp.float32
     )
     projected = summed.astype(jnp.bfloat16)
     tap_count = conv_weight.shape[1]

time: 275 us -> 324 us (1.18)
  waiting for transfers between devices: 91 us -> 142 us
  local copies, waits for them, and re-layouts: 40 us -> 32.9 us
  matrix products: 61.5 us -> 66.5 us
    all_gather x1 -> x2, waiting for transfers between devices: 32.4 us -> 82.5 us  [the longest x1 82.5 us: on_device_body(): gathered_lo = lax.all_gather(normed[:, :half], 'ch', axis=0, tiled=True)]
    ppermute x7 -> x0, local copies, waits for them, and re-layouts: 15 us -> none  [the longest x4 7.83 us: gathered_weight(): lax.ppermute(part, 'ctx', sibling)]
    dynamic_update_slice x8, local copies, waits for them, and re-layouts: 11.9 us -> 18.9 us  [gathered_weight(): full = lax.dynamic_update_slice(full, part, (0, src * width, 0))]
    dot_general x1 -> x2, matrix products: 18.8 us -> 23.9 us  [the longest x1 12.1 us: on_device_body(): jnp.einsum('tf,ifc->itc', gathered_hi, weight[:, half:], preferred_elemen...]
  transfers between devices with their start and end apart: 16 -> 17, of which waited for: 4 -> 4; matrix products, arithmetic and copies ran while one was open for 26% -> 23% of each run, Pallas kernels for 0% -> 0%
where the time goes in v3:
time: 324 us; the launch traced here: 323 us
  waiting for transfers between devices  142 us (44%)
  matrix products  66.5 us (21%)
  local copies, waits for them, and re-layouts  32.9 us (10%)
  starting transfers between devices  26 us (8%)
  blocking collectives  24.5 us (8%)
  other arithmetic  16.9 us (5%)
  between operations  13.8 us (4%)
    all_gather x1, waiting for transfers between devices, on_device_body(): gathered_lo = lax.all_gather(normed[:, :half], 'ch', axis=0, tiled=True)  82.5 us
    ppermute x3, waiting for transfers between devices, gathered_weight(): held.append((lax.ppermute(block, 'ctx', pairs), (me - by) % count))  58.6 us
    dot_general x1, matrix products, on_device_body(): inside = jnp.einsum('cts,jsc->jtc', toeplitz, spans_in, precision=high)  25 us
    all_to_all x1, blocking collectives, on_device_body(): return lax.all_to_all(gated, 'ch', split_axis=0, concat_axis=1, tiled=True)  24.5 us
    ppermute x8, starting transfers between devices, shifted(): return lax.ppermute(shard, axis, pairs)  19.4 us
    dynamic_update_slice x8, local copies, waits for them, and re-layouts, gathered_weight(): full = lax.dynamic_update_slice(full, part, (0, src * width, 0))  18.9 us
    dot_general x1, matrix products, on_device_body(): jnp.einsum('tf,ifc->itc', gathered_hi, weight[:, half:], preferred_elemen...  12.1 us
    dot_general x1, matrix products, on_device_body(): jnp.einsum('tf,ifc->itc', gathered_lo, weight[:, :half], preferred_elemen...  11.7 us
  transfers between devices with their start and end apart: 17, of which 4 were waited for; matrix products, arithmetic and copies ran while one was open for 23% of the time, Pallas kernels for 0%

profile of v3, /device:TPU:32, one launch (start us, length us, event | category | flops | bytes accessed | tf_op | source)
XLA Modules:
  0.0 323.1 jit_solution(13767293038945642541)
XLA Ops:
  11.7 1.6 collective-permute-start
  13.3 2.7 collective-permute-start.1
  17.9 31.4 %collective-permute-done = bf16[3,1024,256]{1,2,0:T(8,128)(2,1)} collective-permute-done((bf16[3,1024,256]{1,2,0:T(8,128)(2,1)S(1)}, bf16[3,1024,256]{1,2,0:T(8,128)(2,1)}, u32[]{:S(2)}, u32[]{:S(2)}) %collective-permute-start) | collective-permute-done | bytes 1572896 | tf_op jit(solution)/shard_map/ppermute | solution.py:22
  49.4 6.1 %broadcast_in_dim.7 = bf16[3,8192,256]{1,2,0:T(8,128)(2,1)} broadcast(bf16[]{:T(256)} %constant.31.clone.1), dimensions={} | broadcast | bytes 12582914 | tf_op jit(solution)/shard_map/broadcast_in_dim | solution.py:25
  56.7 27.2 %collective-permute-done.1 = bf16[3,1024,256]{1,2,0:T(8,128)(2,1)} collective-permute-done((bf16[3,1024,256]{1,2,0:T(8,128)(2,1)S(1)}, bf16[3,1024,256]{1,2,0:T(8,128)(2,1)}, u32[]{:S(2)}, u32[]{:S(2)}) %collective-permute-start.1) | collective-permute-done | bytes 1572896 | tf_op jit(solution)/shard_map/ppermute | solution.py:22
  84.7 9.6 %fusion.6 = f32[256,128,128]{2,0,1:T(8,128)} fusion(s32[128,128]{1,0:T(8,128)S(1)} %iota_subtract_fusion, f32[128,256]{1,0:T(8,128)S(1)} %multiply_reduce_fusion), kind=kOutput, calls=%fused_computation.9 | convolution fusion | flops 6444548096 | bytes 16973824 | tf_op jit(solution)/shard_map/lc,lts->cts/dot_general | solution.py:73
  94.3 2.7 constant_dynamic-update-slice_fusion.6
  97.0 2.7 constant_dynamic-update-slice_fusion.5
  101.1 2.7 constant_dynamic-update-slice_fusion.3
  103.8 2.7 constant_dynamic-update-slice_fusion.2
  106.6 2.7 constant_dynamic-update-slice_fusion.1
  109.3 2.7 constant_dynamic-update-slice_fusion
  112.0 12.1 %fusion.2 = f32[3,256,1024]{2,1,0:T(8,128)} fusion(bf16[1024,4096]{1,0:T(8,128)(2,1)} %all-gather.5.cloned.1.call-done, bf16[3,8192,256]{1,2,0:T(8,128)(2,1)} %constant_dynamic-update-slice_fusion), kind=kOutput, calls=%fused_computation.4 | convolution fusion | flops 6442450944 | bytes 17825792 | tf_op jit(solution)/shard_map/tf,ifc->itc/dot_general | solution.py:44
  124.1 82.5 %all-gather.3.cloned.1.call-done = bf16[1024,4096]{1,0:T(8,128)(2,1)} async-done(((bf16[32,4096]{1,0:T(8,128)(2,1)}), bf16[1024,4096]{1,0:T(8,128)(2,1)}) %all-gather.3.cloned.1.call-update) | async-done | bytes 8388624 | tf_op jit(solution)/shard_map/all_gather | solution.py:37
  206.6 11.7 %fusion.28 = bf16[3,1024,256]{1,2,0:T(8,128)(2,1)S(1)} fusion(f32[3,256,1024]{2,1,0:T(8,128)} %fusion.2, bf16[1024,4096]{1,0:T(8,128)(2,1)} %all-gather.3.cloned.1.call-done, bf16[3,8192,256]{1,2,0:T(8,128)(2,1)} %constant_dynamic-update-slice_fusion), kind=kOutput, calls=%fused_computation.37 | convolution fusion | flops 6444023808 | bytes 19398656 | tf_op jit(solution)/shard_map/tf,ifc->itc/dot_general | solution.py:42
  221.6 6.3 %fusion.10 = f32[3,1024,256]{1,2,0:T(8,128)S(1)} fusion(f32[3,1030,256]{1,2,0:T(8,128)S(1)} %maximum_convert_fusion, f32[3,256]{1,0:T(4,128)S(1)} %get-tuple-element.103, f32[3,256]{1,0:T(4,128)S(1)} %get-tuple-element.104, f32[3,256]{1,0:T(4,128)S(1)} %get-tuple-element.105, f32[3,256]{1,0:T(4,128)S(1)} %get-tuple-element.106, ...), kind=kLoop, calls=%fused_computation.14 | loop fusion | flops 10223616 | bytes 25187328 | tf_op jit(solution)/shard_map/add | solution.py:55
  228.5 3.6 %fusion.36 = f32[8,16,256]{1,0,2:T(8,128)} fusion(f32[8,128,256]{1,0,2:T(8,128)S(1)} %bitcast.61, f32[128]{0:T(128)S(1)} %iota_subtract_fusion.1, f32[16,256]{0,1:T(8,128)S(1)} %copy.57, f32[16,256]{0,1:T(8,128)S(1)} %copy.56), kind=kOutput, calls=%fused_computation.39 | convolution fusion | flops 26214400 | bytes 1212928 | tf_op jit(solution)/shard_map/jsc,msc->jmc/dot_general | solution.py:80
  233.6 4.9 %while.13 = (s32[]{:T(128)}, f32[16,256]{1,0:T(8,128)S(1)}, f32[8,16,256]{2,1,0:T(8,128)}, f32[16,256]{1,0:T(8,128)S(1)}, f32[8,16,256]{2,1,0:T(8,128)S(1)}, /*index=5*/s32[]{:T(128)}, s32[]{:T(128)}) while((s32[]{:T(128)}, f32[16,256]{1,0:T(8,128)S(1)}, f32[8,16,256]{2,1,0:T(8,128)}, f32[16,256]{1,0:T(8,128)S(1)}, ...), condition=%wide.region_3.4_spmd.clone, body=%wide.region_2.3_spmd.clone.sunk | while | flops 16387 | bytes 98908 | solution.py:87
  238.6 6.7 %collective-permute-start.10 = (f32[16,256]{1,0:T(8,128)S(1)}, f32[16,256]{1,0:T(8,128)S(1)}, u32[]{:S(2)}, u32[]{:S(2)}) collective-permute-start(f32[16,256]{1,0:T(8,128)S(1)} %get-tuple-element.38), channel_id=1, source_target_pairs={{0,96},{32,128},{64,160},{96,192},{128,224},{1,97},{33,129},{65,16... | collective-permute-start | bytes 49160 | tf_op jit(solution)/shard_map/ppermute | solution.py:12
  245.3 4.7 %collective-permute-start.11 = (f32[16,256]{1,0:T(8,128)S(1)}, f32[16,256]{1,0:T(8,128)S(1)}, u32[]{:S(2)}, u32[]{:S(2)}) collective-permute-start(f32[16,256]{1,0:T(8,128)S(1)} %get-tuple-element.38), channel_id=1, source_target_pairs={{0,128},{32,160},{64,192},{96,224},{1,129},{33,161},{65,193},{97,2... | collective-permute-start | bytes 49160 | tf_op jit(solution)/shard_map/ppermute | solution.py:12
  257.2 25.0 %fusion.39 = f32[8,128,256]{1,0,2:T(8,128)} fusion(f32[8,128,256]{1,0,2:T(8,128)S(1)} %bitcast.62, f32[256,128,128]{2,0,1:T(8,128)} %fusion.6), kind=kOutput, calls=%fused_computation.40 | convolution fusion | flops 201326592 | bytes 18874368 | tf_op jit(solution)/shard_map/cts,jsc->jtc/dot_general | solution.py:76
  284.5 4.4 %fusion.42 = f32[8,128,256]{1,0,2:T(8,128)} fusion(f32[8,128,256]{1,0,2:T(8,128)} %fusion.39, f32[8,16,256]{1,0,2:T(8,128)S(1)} %copy.59, f32[128]{0:T(128)S(1)} %iota_add_fusion, f32[16,256]{0,1:T(8,128)S(1)} %copy.56, f32[16,256]{0,1:T(8,128)} %copy.55), kind=kOutput, calls=%fused_computation.41 | convolution fusion | flops 26476544 | bytes 2261504 | tf_op jit(solution)/shard_map/jmc,mtc->jtc/dot_general | solution.py:100
  288.9 1.6 copy.60
  290.8 24.5 %all_to_all.16 = bf16[32,32,256]{2,1,0:T(8,128)(2,1)S(1)} all-to-all(bf16[32,32,256]{2,1,0:T(8,128)(2,1)S(1)} %multiply_convert_fusion), channel_id=1, replica_groups=mesh['ctx'=8,'ch'=32] {'ch'}, dimensions={0} | all-to-all | bytes 1048576 | tf_op jit(solution)/shard_map/all_to_all | solution.py:103
  (91 shorter events, 31.1 us)
Async XLA Ops:
  6.5 4.3 %copy-start = (bf16[3,1024,256]{2,1,0:T(8,128)(2,1)S(1)}, bf16[3,1024,256]{2,1,0:T(8,128)(2,1)}, u32[]{:S(2)}) copy-start(bf16[3,1024,256]{2,1,0:T(8,128)(2,1)} %param.11) | copy-start | bytes 4718596
  6.5 10.9 %copy-start.3 = (f32[3,7,256]{2,1,0:T(8,128)S(1)}, f32[3,7,256]{2,1,0:T(8,128)}, u32[]{:S(2)}) copy-start(f32[3,7,256]{2,1,0:T(8,128)} %param.12) | copy-start | bytes 64516
  6.5 10.9 %copy-start.1 = (f32[16,256]{1,0:T(8,128)S(1)}, f32[16,256]{1,0:T(8,128)}, u32[]{:S(2)}) copy-start(f32[16,256]{1,0:T(8,128)} %param.13) | copy-start | bytes 49156
  6.5 11.0 %copy-start.2 = (f32[16,256]{1,0:T(8,128)S(1)}, f32[16,256]{1,0:T(8,128)}, u32[]{:S(2)}) copy-start(f32[16,256]{1,0:T(8,128)} %param.14) | copy-start | bytes 49156
  6.5 105.4 %all-gather.5.cloned.1.call-start = ((), (), s32[]{:S(2)}) async-start(), calls=%async_computation.2 | async-start | bytes 8650752 | tf_op jit(solution)/shard_map/all_gather | solution.py:38
  10.0 196.6 %all-gather.3.cloned.1.call-start = ((), (), s32[]{:S(2)}) async-start(), calls=%async_computation.1 | async-start | bytes 8650752 | tf_op jit(solution)/shard_map/all_gather | solution.py:37
  11.7 37.7 %collective-permute-start = (bf16[3,1024,256]{1,2,0:T(8,128)(2,1)S(1)}, bf16[3,1024,256]{1,2,0:T(8,128)(2,1)}, u32[]{:S(2)}, u32[]{:S(2)}) collective-permute-start(bf16[3,1024,256]{1,2,0:T(8,128)(2,1)S(1)} %copy.47), channel_id=1, source_target_pairs={{0,64},{32,96},{64,128},{96,160},{128,192},{160,224},{192,0},{224,... | collective-permute-start | bytes 4718600 | tf_op jit(solution)/shard_map/ppermute | solution.py:22
  13.3 70.6 %collective-permute-start.1 = (bf16[3,1024,256]{1,2,0:T(8,128)(2,1)S(1)}, bf16[3,1024,256]{1,2,0:T(8,128)(2,1)}, u32[]{:S(2)}, u32[]{:S(2)}) collective-permute-start(bf16[3,1024,256]{1,2,0:T(8,128)(2,1)S(1)} %copy.47), channel_id=1, source_target_pairs={{0,128},{32,160},{64,192},{96,224},{128,0},{160,32},{192,64},{224,... | collective-permute-start | bytes 4718600 | tf_op jit(solution)/shard_map/ppermute | solution.py:22
  16.0 67.9 %collective-permute-start.2 = (bf16[3,1024,256]{1,2,0:T(8,128)(2,1)S(1)}, bf16[3,1024,256]{1,2,0:T(8,128)(2,1)S(1)}, u32[]{:S(2)}, u32[]{:S(2)}) collective-permute-start(bf16[3,1024,256]{1,2,0:T(8,128)(2,1)S(1)} %copy.47), channel_id=1, source_target_pairs={{0,192},{32,224},{64,0},{96,32},{128,64},{160,96},{192,128},{224,1... | collective-permute-start | bytes 4718600 | tf_op jit(solution)/shard_map/ppermute | solution.py:22
  17.4 83.7 %collective-permute-start.3 = (bf16[3,1024,256]{1,2,0:T(8,128)(2,1)S(1)}, bf16[3,1024,256]{1,2,0:T(8,128)(2,1)}, u32[]{:S(2)}, u32[]{:S(2)}) collective-permute-start(bf16[3,1024,256]{1,2,0:T(8,128)(2,1)S(1)} %copy.47), channel_id=1, source_target_pairs={{0,32},{32,0},{64,96},{96,64},{128,160},{160,128},{192,224},{224,1... | collective-permute-start | bytes 4718600 | tf_op jit(solution)/shard_map/ppermute | solution.py:24
  49.4 54.5 %collective-permute-start.4 = (bf16[3,1024,256]{1,2,0:T(8,128)(2,1)}, bf16[3,1024,256]{1,2,0:T(8,128)(2,1)}, u32[]{:S(2)}, u32[]{:S(2)}) collective-permute-start(bf16[3,1024,256]{1,2,0:T(8,128)(2,1)} %collective-permute-done), channel_id=1, source_target_pairs={{0,32},{32,0},{64,96},{96,64},{128,160},{160,128},{192,224},{224,1... | collective-permute-start | bytes 4718600 | tf_op jit(solution)/shard_map/ppermute | solution.py:24
  83.9 22.7 %collective-permute-start.5 = (bf16[3,1024,256]{1,2,0:T(8,128)(2,1)}, bf16[3,1024,256]{1,2,0:T(8,128)(2,1)}, u32[]{:S(2)}, u32[]{:S(2)}) collective-permute-start(bf16[3,1024,256]{1,2,0:T(8,128)(2,1)} %collective-permute-done.1), channel_id=1, source_target_pairs={{0,32},{32,0},{64,96},{96,64},{128,160},{160,128},{192,224},{224,1... | collective-permute-start | bytes 4718600 | tf_op jit(solution)/shard_map/ppermute | solution.py:24
  83.9 25.3 %collective-permute-start.6 = (bf16[3,1024,256]{1,2,0:T(8,128)(2,1)S(1)}, bf16[3,1024,256]{1,2,0:T(8,128)(2,1)}, u32[]{:S(2)}, u32[]{:S(2)}) collective-permute-start(bf16[3,1024,256]{1,2,0:T(8,128)(2,1)S(1)} %collective-permute-done.2), channel_id=1, source_target_pairs={{0,32},{32,0},{64,96},{96,64},{128,160},{160,128},{192,224},{224,1... | collective-permute-start | bytes 4718600 | tf_op jit(solution)/shard_map/ppermute | solution.py:24
  218.5 2.4 collective-permute-start.7
  238.6 16.1 %collective-permute-start.10 = (f32[16,256]{1,0:T(8,128)S(1)}, f32[16,256]{1,0:T(8,128)S(1)}, u32[]{:S(2)}, u32[]{:S(2)}) collective-permute-start(f32[16,256]{1,0:T(8,128)S(1)} %get-tuple-element.38), channel_id=1, source_target_pairs={{0,96},{32,128},{64,160},{96,192},{128,224},{1,97},{33,129},{65,16... | collective-permute-start | bytes 49160 | tf_op jit(solution)/shard_map/ppermute | solution.py:12
  245.3 10.7 %collective-permute-start.11 = (f32[16,256]{1,0:T(8,128)S(1)}, f32[16,256]{1,0:T(8,128)S(1)}, u32[]{:S(2)}, u32[]{:S(2)}) collective-permute-start(f32[16,256]{1,0:T(8,128)S(1)} %get-tuple-element.38), channel_id=1, source_target_pairs={{0,128},{32,160},{64,192},{96,224},{1,129},{33,161},{65,193},{97,2... | collective-permute-start | bytes 49160 | tf_op jit(solution)/shard_map/ppermute | solution.py:12
  250.7 32.2 %collective-permute-start.12 = (f32[16,256]{1,0:T(8,128)S(1)}, f32[16,256]{1,0:T(8,128)S(1)}, u32[]{:S(2)}, u32[]{:S(2)}) collective-permute-start(f32[16,256]{1,0:T(8,128)S(1)} %get-tuple-element.38), channel_id=1, source_target_pairs={{0,160},{32,192},{64,224},{1,161},{33,193},{65,225},{2,162},{34,19... | collective-permute-start | bytes 49160 | tf_op jit(solution)/shard_map/ppermute | solution.py:12
  252.0 30.9 %collective-permute-start.13 = (f32[16,256]{1,0:T(8,128)S(1)}, f32[16,256]{1,0:T(8,128)S(1)}, u32[]{:S(2)}, u32[]{:S(2)}) collective-permute-start(f32[16,256]{1,0:T(8,128)S(1)} %get-tuple-element.38), channel_id=1, source_target_pairs={{0,192},{32,224},{1,193},{33,225},{2,194},{34,226},{3,195},{35,227... | collective-permute-start | bytes 49160 | tf_op jit(solution)/shard_map/ppermute | solution.py:12
  253.3 29.6 %collective-permute-start.14 = (f32[16,256]{1,0:T(8,128)S(1)}, f32[16,256]{1,0:T(8,128)S(1)}, u32[]{:S(2)}, u32[]{:S(2)}) collective-permute-start(f32[16,256]{1,0:T(8,128)S(1)} %get-tuple-element.38), channel_id=1, source_target_pairs={{0,224},{1,225},{2,226},{3,227},{4,228},{5,229},{6,230},{7,231},{8... | collective-permute-start | bytes 49160 | tf_op jit(solution)/shard_map/ppermute | solution.py:12
  254.6 28.4 %collective-permute-start.8 = (f32[16,256]{1,0:T(8,128)S(1)}, f32[16,256]{1,0:T(8,128)S(1)}, u32[]{:S(2)}, u32[]{:S(2)}) collective-permute-start(f32[16,256]{1,0:T(8,128)S(1)} %get-tuple-element.38), channel_id=1, source_target_pairs={{0,32},{32,64},{64,96},{96,128},{128,160},{160,192},{192,224},{1,3... | collective-permute-start | bytes 49160 | tf_op jit(solution)/shard_map/ppermute | solution.py:12
  256.0 27.1 %collective-permute-start.9 = (f32[16,256]{1,0:T(8,128)S(1)}, f32[16,256]{1,0:T(8,128)S(1)}, u32[]{:S(2)}, u32[]{:S(2)}) collective-permute-start(f32[16,256]{1,0:T(8,128)S(1)} %get-tuple-element.38), channel_id=1, source_target_pairs={{0,64},{32,96},{64,128},{96,160},{128,192},{160,224},{1,65},{33,97... | collective-permute-start | bytes 49160 | tf_op jit(solution)/shard_map/ppermute | solution.py:12
  284.5 6.0 %copy-start.4 = (f32[256]{0:T(256)S(1)}, f32[256]{0:T(256)}, u32[]{:S(2)}) copy-start(f32[256]{0:T(256)} %param.15) | copy-start | bytes 3076
Sparse Core Ops, SparseCore 0:
  10.2 98.8 all-gather.4
  111.6 94.9 all-gather.2

commit v4 on v2

--- a/solution.py
+++ b/solution.py
@@ -2,6 +2,7 @@
 import jax.numpy as jnp
 from jax import lax
 from jax.sharding import PartitionSpec as P
+from jax.experimental import pallas as pl
 
 norm_eps = 1e-05
 
@@ -10,6 +11,56 @@
     length = lax.axis_size(axis)
     pairs = [(i, i + by) for i in range(length) if 0 <= i + by < length]
     return lax.ppermute(shard, axis, pairs)
+
+
+LANES = 128
+
+
+def modal_kernel(x_ref, r_ref, b_ref, res_ref, y_ref, end_ref):
+    half = r_ref.shape[0] // 2
+    r0, r1 = r_ref[:half, :], r_ref[half:, :]
+    b0, b1 = b_ref[:half, :], b_ref[half:, :]
+    q0, q1 = res_ref[:half, :], res_ref[half:, :]
+    rows = x_ref.shape[0]
+
+    def step8(i, carry):
+        s0, s1 = carry
+        at = pl.multiple_of(i * 8, 8)
+        xb = x_ref[pl.ds(at, 8), :]
+        outs = []
+        for k in range(8):
+            xt = xb[k : k + 1, :]
+            s0 = r0 * s0 + b0 * xt
+            s1 = r1 * s1 + b1 * xt
+            outs.append(jnp.sum(q0 * s0 + q1 * s1, axis=0, keepdims=True))
+        y_ref[pl.ds(at, 8), :] = jnp.concatenate(outs, axis=0)
+        return s0, s1
+
+    zero = jnp.zeros((half, x_ref.shape[1]), jnp.float32)
+    s0, s1 = lax.fori_loop(0, rows // 8, step8, (zero, zero))
+    end_ref[:half, :] = s0
+    end_ref[half:, :] = s1
+
+
+def modal_filter(x, retention, in_scale, residue):
+    rows, chans = x.shape
+    modes = retention.shape[0]
+    col = lambda i: (0, i)
+    return pl.pallas_call(
+        modal_kernel,
+        grid=(chans // LANES,),
+        in_specs=[
+            pl.BlockSpec((rows, LANES), col),
+            pl.BlockSpec((modes, LANES), col),
+            pl.BlockSpec((modes, LANES), col),
+            pl.BlockSpec((modes, LANES), col),
+        ],
+        out_specs=[pl.BlockSpec((rows, LANES), col), pl.BlockSpec((modes, LANES), col)],
+        out_shape=[
+            jax.ShapeDtypeStruct((rows, chans), jnp.float32),
+            jax.ShapeDtypeStruct((modes, chans), jnp.float32),
+        ],
+    )(x, retention, in_scale, residue)
 
 
 def gathered_weight(block):
@@ -55,47 +106,25 @@
         )
     queries = featured[0]
     mixed = featured[1] * featured[2]
-    highest = lax.Precision.HIGHEST
     high = lax.Precision.HIGH
+    retention = jnp.exp(-decay_rate)
     in_scale = jnp.sqrt(-jnp.expm1(-2.0 * decay_rate))
-    span_rows = min(128, row_count)
-    span_count = row_count // span_rows
-    positions = jnp.arange(span_rows, dtype=jnp.float32)
-    own_rate, own_residue = lax.optimization_barrier((decay_rate, residue))
-    own_scale = jnp.sqrt(-jnp.expm1(-2.0 * own_rate))
-    lag_decay = jnp.exp(-own_rate[:, None, :] * positions[None, :, None])
-    impulse = jnp.sum((own_residue * own_scale)[:, None, :] * lag_decay, axis=0)
-    offsets = jnp.arange(span_rows)[:, None] - jnp.arange(span_rows)[None, :]
-    lag_table = (offsets[None, :, :] == jnp.arange(span_rows)[:, None, None]).astype(jnp.float32)
-    toeplitz = jnp.einsum("lc,lts->cts", impulse, lag_table, precision=highest)
-    toeplitz = lax.optimization_barrier(toeplitz)
-    spans_in = mixed.reshape(span_count, span_rows, chan_count)
-    inside = jnp.einsum("cts,jsc->jtc", toeplitz, spans_in, precision=high)
-    end_weight = in_scale[:, None, :] * jnp.exp(
-        -decay_rate[:, None, :] * (span_rows - 1.0 - positions)[None, :, None]
-    )
-    span_ends = jnp.einsum("jsc,msc->jmc", spans_in, end_weight, precision=high)
-    span_decay = jnp.exp(-decay_rate * float(span_rows))
-
-    def advance(carried, span_end):
-        return (span_decay * carried + span_end, carried)
-
+    local_filtered, local_end = modal_filter(mixed, retention, in_scale, residue)
     zero_state = jnp.zeros(decay_rate.shape, jnp.float32)
-    local_end, starts = lax.scan(advance, zero_state, span_ends)
     incoming = zero_state
     for by in range(1, lax.axis_size("ctx")):
         carried_end = shifted(local_end, "ctx", by)
         incoming = incoming + jnp.exp(-decay_rate * float(row_count * (by - 1))) * carried_end
+    span_rows = min(128, row_count)
+    span_count = row_count // span_rows
+    positions = jnp.arange(span_rows, dtype=jnp.float32)
     span_starts = jnp.arange(span_count, dtype=jnp.float32) * float(span_rows)
-    starts = (
-        starts
-        + jnp.exp(-decay_rate[None, :, :] * span_starts[:, None, None]) * incoming[None, :, :]
-    )
+    starts = jnp.exp(-decay_rate[None, :, :] * span_starts[:, None, None]) * incoming[None, :, :]
     out_weight = residue[:, None, :] * jnp.exp(
         -decay_rate[:, None, :] * (positions + 1.0)[None, :, None]
     )
     outside = jnp.einsum("jmc,mtc->jtc", starts, out_weight, precision=high)
-    filtered = (inside + outside).reshape(row_count, chan_count)
+    filtered = local_filtered + outside.reshape(row_count, chan_count)
     gated = (queries * (filtered + skip_gain[None, :] * mixed)).astype(jnp.bfloat16)
     return lax.all_to_all(gated, "ch", split_axis=0, concat_axis=1, tiled=True)
 

time: 275 us -> 245 us (0.89)
  matrix products: 61.5 us -> 22.7 us
  waiting for transfers between devices: 91 us -> 102 us
  Pallas kernels: 0 us -> 9.33 us
  other arithmetic: 17.7 us -> 11 us
    dot_general x3 -> x0, matrix products: 38.2 us -> none  [the longest x1 25 us: on_device_body(): inside = jnp.einsum('cts,jsc->jtc', toeplitz, spans_in, precision=high)]
    pallas_call x0 -> x1, Pallas kernels: none -> 9.33 us  [modal_filter(): pl.pallas_call(modal_kernel, grid=(chans // LANES,), in_specs=[pl.BlockSp...]
    ppermute x3, waiting for transfers between devices: 58 us -> 65.8 us  [gathered_weight(): held.append((lax.ppermute(block, 'ctx', pairs), (me - by) % count))]
    dynamic_update_slice x8 -> x0, other arithmetic: 4.89 us -> none  [on_device_body(): local_end, starts = lax.scan(advance, zero_state, span_ends)]
    add x1, other arithmetic: 6.32 us -> 2.59 us  [on_device_body(): featured + conv_weight[:, shift_idx, None, :] * padded[:, reach - shift_i...]
  transfers between devices with their start and end apart: 16 -> 16, of which waited for: 4 -> 5; matrix products, arithmetic and copies ran while one was open for 26% -> 15% of each run, Pallas kernels for 0% -> 0%
where the time goes in v4:
time: 245 us; the launch traced here: 244 us
  waiting for transfers between devices  102 us (42%)
  local copies, waits for them, and re-layouts  37.3 us (15%)
  blocking collectives  24.2 us (10%)
  starting transfers between devices  23.7 us (10%)
  matrix products  22.7 us (9%)
  between operations  13.7 us (6%)
  other arithmetic  11 us (4%)
  Pallas kernels  9.33 us (4%)
    ppermute x3, waiting for transfers between devices, gathered_weight(): held.append((lax.ppermute(block, 'ctx', pairs), (me - by) % count))  65.8 us
    all_gather x1, waiting for transfers between devices, on_device_body(): gathered = lax.all_gather(normed, 'ch', axis=0, tiled=True)  34.3 us
    all_to_all x1, blocking collectives, on_device_body(): return lax.all_to_all(gated, 'ch', split_axis=0, concat_axis=1, tiled=True)  24.2 us
    dot_general x1, matrix products, on_device_body(): jnp.einsum('tf,ifc->itc', gathered, gathered_weight(proj_weight), preferr...  18.8 us
    ppermute x8, starting transfers between devices, shifted(): return lax.ppermute(shard, axis, pairs)  17.4 us
    dynamic_update_slice x8, local copies, waits for them, and re-layouts, gathered_weight(): full = lax.dynamic_update_slice(full, part, (0, src * width, 0))  11.9 us
    pallas_call x1, Pallas kernels, modal_filter(): pl.pallas_call(modal_kernel, grid=(chans // LANES,), in_specs=[pl.BlockSp...  9.33 us
    ppermute x4, local copies, waits for them, and re-layouts, gathered_weight(): lax.ppermute(part, 'ctx', sibling)  7.77 us
  transfers between devices with their start and end apart: 16, of which 5 were waited for; matrix products, arithmetic and copies ran while one was open for 15% of the time, Pallas kernels for 0%

profile of v4, /device:TPU:32, one launch (start us, length us, event | category | flops | bytes accessed | tf_op | source)
XLA Modules:
  0.0 243.7 jit_solution(3381284630057732656)
XLA Ops:
  7.9 2.0 fusion.23
  10.0 1.6 collective-permute-start
  11.5 2.7 %collective-permute-start.1 = (bf16[3,1024,256]{2,1,0:T(8,128)(2,1)}, bf16[3,1024,256]{2,1,0:T(8,128)(2,1)}, u32[]{:S(2)}, u32[]{:S(2)}) collective-permute-start(bf16[3,1024,256]{2,1,0:T(8,128)(2,1)} %param.9), channel_id=1, source_target_pairs={{0,128},{32,160},{64,192},{96,224},{128,0},{160,32},{192,64},{224,... | collective-permute-start | bytes 4718600 | tf_op jit(solution)/shard_map/ppermute | solution.py:73
  16.6 31.3 %collective-permute-done = bf16[3,1024,256]{2,1,0:T(8,128)(2,1)} collective-permute-done((bf16[3,1024,256]{2,1,0:T(8,128)(2,1)}, bf16[3,1024,256]{2,1,0:T(8,128)(2,1)}, u32[]{:S(2)}, u32[]{:S(2)}) %collective-permute-start) | collective-permute-done | bytes 1572896 | tf_op jit(solution)/shard_map/ppermute | solution.py:73
  47.9 34.5 %collective-permute-done.1 = bf16[3,1024,256]{2,1,0:T(8,128)(2,1)} collective-permute-done((bf16[3,1024,256]{2,1,0:T(8,128)(2,1)}, bf16[3,1024,256]{2,1,0:T(8,128)(2,1)}, u32[]{:S(2)}, u32[]{:S(2)}) %collective-permute-start.1) | collective-permute-done | bytes 1572896 | tf_op jit(solution)/shard_map/ppermute | solution.py:73
  82.9 6.1 %broadcast_in_dim.2 = bf16[3,8192,256]{1,2,0:T(8,128)(2,1)} broadcast(bf16[]{:T(256)} %constant.24.clone.1), dimensions={} | broadcast | bytes 12582914 | tf_op jit(solution)/shard_map/broadcast_in_dim | solution.py:76
  91.0 2.6 %copy.24 = bf16[3,1024,256]{1,2,0:T(8,128)(2,1)} copy(bf16[3,1024,256]{2,1,0:T(8,128)(2,1)} %collective-permute-done) | data formatting | bytes 3145728 | tf_op jit(solution)/shard_map/ppermute | solution.py:73
  93.6 2.6 %copy.25 = bf16[3,1024,256]{1,2,0:T(8,128)(2,1)} copy(bf16[3,1024,256]{2,1,0:T(8,128)(2,1)} %collective-permute-done.1) | data formatting | bytes 3145728 | tf_op jit(solution)/shard_map/ppermute | solution.py:73
  96.2 1.7 copy.26
  97.9 1.7 copy.27
  99.7 2.8 %constant_dynamic-update-slice_fusion.6 = bf16[3,8192,256]{1,2,0:T(8,128)(2,1)} fusion(bf16[3,8192,256]{1,2,0:T(8,128)(2,1)} %constant_dynamic-update-slice_fusion.7, bf16[3,1024,256]{1,2,0:T(8,128)(2,1)} %copy.24, s32[]{:T(128)S(6)} %select_n.41), kind=kLoop, calls=%fused_computation.59 | loop fusion | bytes 3145732 | tf_op jit(solution)/shard_map/dynamic_update_slice | solution.py:78
  106.4 1.7 copy.28
  108.1 1.7 copy.29
  109.9 2.6 %copy.30 = bf16[3,1024,256]{1,2,0:T(8,128)(2,1)} copy(bf16[3,1024,256]{2,1,0:T(8,128)(2,1)} %collective-permute-done.6) | data formatting | bytes 3145728 | tf_op jit(solution)/shard_map/ppermute | solution.py:75
  116.4 34.3 %all-gather.2.cloned.1.call-done = bf16[1024,8192]{1,0:T(8,128)(2,1)} async-done(((bf16[32,8192]{1,0:T(8,128)(2,1)}), bf16[1024,8192]{1,0:T(8,128)(2,1)}) %all-gather.2.cloned.1.call-update) | async-done | bytes 16777232 | tf_op jit(solution)/shard_map/all_gather | solution.py:86
  150.7 18.8 %fusion.15 = bf16[3,1024,256]{2,1,0:T(8,128)(2,1)S(1)} fusion(bf16[3,8192,256]{1,2,0:T(8,128)(2,1)} %constant_dynamic-update-slice_fusion, bf16[1024,8192]{1,0:T(8,128)(2,1)} %all-gather.2.cloned.1.call-done), kind=kOutput, calls=%fused_computation.21 | convolution fusion | flops 12885688320 | bytes 30932992 | tf_op jit(solution)/shard_map/tf,ifc->itc/dot_general | solution.py:89
  171.9 2.6 %fusion.2 = f32[3,1024,256]{2,1,0:T(8,128)S(1)} fusion(f32[3,1030,256]{2,1,0:T(8,128)S(1)} %maximum_convert_fusion, f32[3,256]{1,0:T(4,128)S(1)} %get-tuple-element.20, f32[3,256]{1,0:T(4,128)S(1)} %get-tuple-element.21, f32[3,256]{1,0:T(4,128)S(1)} %get-tuple-element.22, f32[3,256]{1,0:T(4,128)S(1)} %get-tuple-element.23, ...), kind=kLoop, calls=%fused_computation.3 | loop fusion | flops 10223616 | bytes 25187328 | tf_op jit(solution)/shard_map/add | solution.py:103
  175.6 9.3 %shard_map.73 = (f32[1024,256]{1,0:T(8,128)}, f32[16,256]{1,0:T(8,128)}) custom-call(f32[1024,256]{1,0:T(8,128)} %fusion.24.x_ref, f32[16,256]{1,0:T(8,128)} %get-tuple-element.19.r_ref, f32[16,256]{1,0:T(8,128)} %get-tuple-element.18.b_ref, f32[16,256]{1,0:T(8,128)} %res_ref.1), custom_call_target="tpu_custom_call" | custom-call | tf_op jit(solution)/shard_map/pallas_call | solution.py:49
  184.9 5.2 %collective-permute-start.10 = (f32[16,256]{1,0:T(8,128)}, f32[16,256]{1,0:T(8,128)S(1)}, u32[]{:S(2)}, u32[]{:S(2)}) collective-permute-start(f32[16,256]{1,0:T(8,128)} %get-tuple-element.8), channel_id=1, source_target_pairs={{0,96},{32,128},{64,160},{96,192},{128,224},{1,97},{33,129},{65,16... | collective-permute-start | bytes 49160 | tf_op jit(solution)/shard_map/ppermute | solution.py:13
  190.1 4.5 %collective-permute-start.11 = (f32[16,256]{1,0:T(8,128)}, f32[16,256]{1,0:T(8,128)S(1)}, u32[]{:S(2)}, u32[]{:S(2)}) collective-permute-start(f32[16,256]{1,0:T(8,128)} %get-tuple-element.8), channel_id=1, source_target_pairs={{0,128},{32,160},{64,192},{96,224},{1,129},{33,161},{65,193},{97,2... | collective-permute-start | bytes 49160 | tf_op jit(solution)/shard_map/ppermute | solution.py:13
  203.5 3.9 %fusion.18 = f32[8,128,256]{1,0,2:T(8,128)} fusion(f32[128]{0:T(128)} %iota_add_fusion, f32[16,256]{0,1:T(8,128)S(1)} %copy.33, f32[16,256]{0,1:T(8,128)S(1)} %copy.32, f32[16,256]{0,1:T(8,128)S(1)} %copy.35, f32[8]{0:T(128)} %iota_multiply_fusion), kind=kOutput, calls=%fused_computation.22 | convolution fusion | flops 26279936 | bytes 1098272 | tf_op jit(solution)/shard_map/jmc,mtc->jtc/dot_general | solution.py:126
  207.4 2.5 %copy.36 = f32[8,128,256]{2,1,0:T(8,128)} copy(f32[8,128,256]{1,0,2:T(8,128)} %fusion.18) | data formatting | bytes 2097152 | tf_op jit(solution)/shard_map/jmc,mtc->jtc/transpose | solution.py:126
  210.0 1.9 fusion.26
  211.9 24.2 %all_to_all.19 = bf16[32,32,256]{2,1,0:T(8,128)(2,1)S(1)} all-to-all(bf16[32,32,256]{2,1,0:T(8,128)(2,1)S(1)} %bitcast.47), channel_id=1, replica_groups=mesh['ctx'=8,'ch'=32] {'ch'}, dimensions={0} | all-to-all | bytes 1048576 | tf_op jit(solution)/shard_map/all_to_all | solution.py:129
  (66 shorter events, 27.1 us)
Async XLA Ops:
  6.5 9.2 %copy-start.2 = (bf16[3,1024,256]{2,1,0:T(8,128)(2,1)S(1)}, bf16[3,1024,256]{2,1,0:T(8,128)(2,1)}, u32[]{:S(2)}) copy-start(bf16[3,1024,256]{2,1,0:T(8,128)(2,1)} %param.9) | copy-start | bytes 4718596
  6.5 144.1 %all-gather.2.cloned.1.call-start = ((), (), s32[]{:S(2)}) async-start(), calls=%async_computation.1 | async-start | bytes 17301504 | tf_op jit(solution)/shard_map/all_gather | solution.py:86
  10.0 37.9 %collective-permute-start = (bf16[3,1024,256]{2,1,0:T(8,128)(2,1)}, bf16[3,1024,256]{2,1,0:T(8,128)(2,1)}, u32[]{:S(2)}, u32[]{:S(2)}) collective-permute-start(bf16[3,1024,256]{2,1,0:T(8,128)(2,1)} %param.9), channel_id=1, source_target_pairs={{0,64},{32,96},{64,128},{96,160},{128,192},{160,224},{192,0},{224,... | collective-permute-start | bytes 4718600 | tf_op jit(solution)/shard_map/ppermute | solution.py:73
  11.5 70.9 %collective-permute-start.1 = (bf16[3,1024,256]{2,1,0:T(8,128)(2,1)}, bf16[3,1024,256]{2,1,0:T(8,128)(2,1)}, u32[]{:S(2)}, u32[]{:S(2)}) collective-permute-start(bf16[3,1024,256]{2,1,0:T(8,128)(2,1)} %param.9), channel_id=1, source_target_pairs={{0,128},{32,160},{64,192},{96,224},{128,0},{160,32},{192,64},{224,... | collective-permute-start | bytes 4718600 | tf_op jit(solution)/shard_map/ppermute | solution.py:73
  14.3 68.1 %collective-permute-start.2 = (bf16[3,1024,256]{2,1,0:T(8,128)(2,1)}, bf16[3,1024,256]{2,1,0:T(8,128)(2,1)}, u32[]{:S(2)}, u32[]{:S(2)}) collective-permute-start(bf16[3,1024,256]{2,1,0:T(8,128)(2,1)} %param.9), channel_id=1, source_target_pairs={{0,192},{32,224},{64,0},{96,32},{128,64},{160,96},{192,128},{224,1... | collective-permute-start | bytes 4718600 | tf_op jit(solution)/shard_map/ppermute | solution.py:73
  15.7 82.2 %collective-permute-start.3 = (bf16[3,1024,256]{2,1,0:T(8,128)(2,1)}, bf16[3,1024,256]{2,1,0:T(8,128)(2,1)}, u32[]{:S(2)}, u32[]{:S(2)}) collective-permute-start(bf16[3,1024,256]{2,1,0:T(8,128)(2,1)} %param.9), channel_id=1, source_target_pairs={{0,32},{32,0},{64,96},{96,64},{128,160},{160,128},{192,224},{224,1... | collective-permute-start | bytes 4718600 | tf_op jit(solution)/shard_map/ppermute | solution.py:75
  47.9 58.6 %collective-permute-start.4 = (bf16[3,1024,256]{2,1,0:T(8,128)(2,1)}, bf16[3,1024,256]{2,1,0:T(8,128)(2,1)}, u32[]{:S(2)}, u32[]{:S(2)}) collective-permute-start(bf16[3,1024,256]{2,1,0:T(8,128)(2,1)} %collective-permute-done), channel_id=1, source_target_pairs={{0,32},{32,0},{64,96},{96,64},{128,160},{160,128},{192,224},{224,1... | collective-permute-start | bytes 4718600 | tf_op jit(solution)/shard_map/ppermute | solution.py:75
  82.4 25.7 %collective-permute-start.5 = (bf16[3,1024,256]{2,1,0:T(8,128)(2,1)}, bf16[3,1024,256]{2,1,0:T(8,128)(2,1)}, u32[]{:S(2)}, u32[]{:S(2)}) collective-permute-start(bf16[3,1024,256]{2,1,0:T(8,128)(2,1)} %collective-permute-done.1), channel_id=1, source_target_pairs={{0,32},{32,0},{64,96},{96,64},{128,160},{160,128},{192,224},{224,1... | collective-permute-start | bytes 4718600 | tf_op jit(solution)/shard_map/ppermute | solution.py:75
  82.4 27.5 %collective-permute-start.6 = (bf16[3,1024,256]{2,1,0:T(8,128)(2,1)}, bf16[3,1024,256]{2,1,0:T(8,128)(2,1)}, u32[]{:S(2)}, u32[]{:S(2)}) collective-permute-start(bf16[3,1024,256]{2,1,0:T(8,128)(2,1)} %collective-permute-done.2), channel_id=1, source_target_pairs={{0,32},{32,0},{64,96},{96,64},{128,160},{160,128},{192,224},{224,1... | collective-permute-start | bytes 4718600 | tf_op jit(solution)/shard_map/ppermute | solution.py:75
  89.0 1.3 copy-start.5
  89.0 1.3 copy-start.4
  99.7 2.9 %copy-start = (bf16[3,1024,256]{1,2,0:T(8,128)(2,1)S(1)}, bf16[3,1024,256]{1,2,0:T(8,128)(2,1)}, u32[]{:S(2)}) copy-start(bf16[3,1024,256]{1,2,0:T(8,128)(2,1)} %copy.25) | copy-start | bytes 4718596
  112.5 2.6 %copy-start.1 = (bf16[3,1024,256]{1,2,0:T(8,128)(2,1)S(1)}, bf16[3,1024,256]{1,2,0:T(8,128)(2,1)}, u32[]{:S(2)}) copy-start(bf16[3,1024,256]{1,2,0:T(8,128)(2,1)} %copy.30) | copy-start | bytes 4718596
  169.5 2.1 collective-permute-start.7
  174.5 27.7 %copy-start.3 = (f32[16,256]{1,0:T(8,128)S(1)}, f32[16,256]{1,0:T(8,128)}, u32[]{:S(2)}) copy-start(f32[16,256]{1,0:T(8,128)} %res_ref.1) | copy-start | bytes 49156
  184.9 14.1 %collective-permute-start.10 = (f32[16,256]{1,0:T(8,128)}, f32[16,256]{1,0:T(8,128)S(1)}, u32[]{:S(2)}, u32[]{:S(2)}) collective-permute-start(f32[16,256]{1,0:T(8,128)} %get-tuple-element.8), channel_id=1, source_target_pairs={{0,96},{32,128},{64,160},{96,192},{128,224},{1,97},{33,129},{65,16... | collective-permute-start | bytes 49160 | tf_op jit(solution)/shard_map/ppermute | solution.py:13
  190.1 10.2 %collective-permute-start.11 = (f32[16,256]{1,0:T(8,128)}, f32[16,256]{1,0:T(8,128)S(1)}, u32[]{:S(2)}, u32[]{:S(2)}) collective-permute-start(f32[16,256]{1,0:T(8,128)} %get-tuple-element.8), channel_id=1, source_target_pairs={{0,128},{32,160},{64,192},{96,224},{1,129},{33,161},{65,193},{97,2... | collective-permute-start | bytes 49160 | tf_op jit(solution)/shard_map/ppermute | solution.py:13
  195.1 7.2 %collective-permute-start.12 = (f32[16,256]{1,0:T(8,128)}, f32[16,256]{1,0:T(8,128)S(1)}, u32[]{:S(2)}, u32[]{:S(2)}) collective-permute-start(f32[16,256]{1,0:T(8,128)} %get-tuple-element.8), channel_id=1, source_target_pairs={{0,160},{32,192},{64,224},{1,161},{33,193},{65,225},{2,162},{34,19... | collective-permute-start | bytes 49160 | tf_op jit(solution)/shard_map/ppermute | solution.py:13
  196.4 5.9 %collective-permute-start.13 = (f32[16,256]{1,0:T(8,128)}, f32[16,256]{1,0:T(8,128)S(1)}, u32[]{:S(2)}, u32[]{:S(2)}) collective-permute-start(f32[16,256]{1,0:T(8,128)} %get-tuple-element.8), channel_id=1, source_target_pairs={{0,192},{32,224},{1,193},{33,225},{2,194},{34,226},{3,195},{35,227... | collective-permute-start | bytes 49160 | tf_op jit(solution)/shard_map/ppermute | solution.py:13
  197.7 4.6 %collective-permute-start.14 = (f32[16,256]{1,0:T(8,128)}, f32[16,256]{1,0:T(8,128)S(1)}, u32[]{:S(2)}, u32[]{:S(2)}) collective-permute-start(f32[16,256]{1,0:T(8,128)} %get-tuple-element.8), channel_id=1, source_target_pairs={{0,224},{1,225},{2,226},{3,227},{4,228},{5,229},{6,230},{7,231},{8... | collective-permute-start | bytes 49160 | tf_op jit(solution)/shard_map/ppermute | solution.py:13
  199.0 3.3 %collective-permute-start.8 = (f32[16,256]{1,0:T(8,128)}, f32[16,256]{1,0:T(8,128)S(1)}, u32[]{:S(2)}, u32[]{:S(2)}) collective-permute-start(f32[16,256]{1,0:T(8,128)} %get-tuple-element.8), channel_id=1, source_target_pairs={{0,32},{32,64},{64,96},{96,128},{128,160},{160,192},{192,224},{1,3... | collective-permute-start | bytes 49160 | tf_op jit(solution)/shard_map/ppermute | solution.py:13
  200.3 2.9 %collective-permute-start.9 = (f32[16,256]{1,0:T(8,128)}, f32[16,256]{1,0:T(8,128)S(1)}, u32[]{:S(2)}, u32[]{:S(2)}) collective-permute-start(f32[16,256]{1,0:T(8,128)} %get-tuple-element.8), channel_id=1, source_target_pairs={{0,64},{32,96},{64,128},{96,160},{128,192},{160,224},{1,65},{33,97... | collective-permute-start | bytes 49160 | tf_op jit(solution)/shard_map/ppermute | solution.py:13
  203.5 6.5 %copy-start.6 = (f32[256]{0:T(256)S(1)}, f32[256]{0:T(256)}, u32[]{:S(2)}) copy-start(f32[256]{0:T(256)} %param.13) | copy-start | bytes 3076
Sparse Core Ops, SparseCore 0:
  10.1 140.5 all-gather.1

commit v5 on v4

--- a/solution.py
+++ b/solution.py
@@ -45,17 +45,18 @@
 def modal_filter(x, retention, in_scale, residue):
     rows, chans = x.shape
     modes = retention.shape[0]
+    lanes = next((w for w in (2 * LANES, LANES) if chans % w == 0), chans)
     col = lambda i: (0, i)
     return pl.pallas_call(
         modal_kernel,
-        grid=(chans // LANES,),
+        grid=(chans // lanes,),
         in_specs=[
-            pl.BlockSpec((rows, LANES), col),
-            pl.BlockSpec((modes, LANES), col),
-            pl.BlockSpec((modes, LANES), col),
-            pl.BlockSpec((modes, LANES), col),
+            pl.BlockSpec((rows, lanes), col),
+            pl.BlockSpec((modes, lanes), col),
+            pl.BlockSpec((modes, lanes), col),
+            pl.BlockSpec((modes, lanes), col),
         ],
-        out_specs=[pl.BlockSpec((rows, LANES), col), pl.BlockSpec((modes, LANES), col)],
+        out_specs=[pl.BlockSpec((rows, lanes), col), pl.BlockSpec((modes, lanes), col)],
         out_shape=[
             jax.ShapeDtypeStruct((rows, chans), jnp.float32),
             jax.ShapeDtypeStruct((modes, chans), jnp.float32),
@@ -110,11 +111,13 @@
     retention = jnp.exp(-decay_rate)
     in_scale = jnp.sqrt(-jnp.expm1(-2.0 * decay_rate))
     local_filtered, local_end = modal_filter(mixed, retention, in_scale, residue)
-    zero_state = jnp.zeros(decay_rate.shape, jnp.float32)
-    incoming = zero_state
-    for by in range(1, lax.axis_size("ctx")):
-        carried_end = shifted(local_end, "ctx", by)
-        incoming = incoming + jnp.exp(-decay_rate * float(row_count * (by - 1))) * carried_end
+    incoming = shifted(local_end, "ctx", 1)
+    reach = 1
+    while reach < lax.axis_size("ctx"):
+        incoming = incoming + jnp.exp(-decay_rate * float(row_count * reach)) * shifted(
+            incoming, "ctx", reach
+        )
+        reach *= 2
     span_rows = min(128, row_count)
     span_count = row_count // span_rows
     positions = jnp.arange(span_rows, dtype=jnp.float32)

time: 245 us -> 250 us (1.020)
  starting transfers between devices: 23.7 us -> 28 us
    ppermute x8 -> x5, starting transfers between devices: 17.4 us -> 21.7 us  [shifted(): return lax.ppermute(shard, axis, pairs)]
    ppermute x8 -> x5, waiting for transfers between devices: 1.71 us -> 4.3 us  [shifted(): return lax.ppermute(shard, axis, pairs)]
  transfers between devices with their start and end apart: 16 -> 13, of which waited for: 5 -> 8; matrix products, arithmetic and copies ran while one was open for 15% -> 14% of each run, Pallas kernels for 0% -> 0%
where the time goes in v5:
time: 250 us; the launch traced here: 248 us
  waiting for transfers between devices  104 us (42%)
  local copies, waits for them, and re-layouts  38.1 us (15%)
  starting transfers between devices  28 us (11%)
  matrix products  22.7 us (9%)
  blocking collectives  22.3 us (9%)
  between operations  13.6 us (5%)
  other arithmetic  11.6 us (5%)
  Pallas kernels  7.66 us (3%)
    ppermute x3, waiting for transfers between devices, gathered_weight(): held.append((lax.ppermute(block, 'ctx', pairs), (me - by) % count))  65.8 us
    all_gather x1, waiting for transfers between devices, on_device_body(): gathered = lax.all_gather(normed, 'ch', axis=0, tiled=True)  34.2 us
    all_to_all x1, blocking collectives, on_device_body(): return lax.all_to_all(gated, 'ch', split_axis=0, concat_axis=1, tiled=True)  22.3 us
    ppermute x5, starting transfers between devices, shifted(): return lax.ppermute(shard, axis, pairs)  21.7 us
    dot_general x1, matrix products, on_device_body(): jnp.einsum('tf,ifc->itc', gathered, gathered_weight(proj_weight), preferr...  18.8 us
    dynamic_update_slice x8, local copies, waits for them, and re-layouts, gathered_weight(): full = lax.dynamic_update_slice(full, part, (0, src * width, 0))  11.9 us
    ppermute x4, local copies, waits for them, and re-layouts, gathered_weight(): lax.ppermute(part, 'ctx', sibling)  7.83 us
    pallas_call x1, Pallas kernels, modal_filter(): pl.pallas_call(modal_kernel, grid=(chans // lanes,), in_specs=[pl.BlockSp...  7.66 us
  transfers between devices with their start and end apart: 13, of which 8 were waited for; matrix products, arithmetic and copies ran while one was open for 14% of the time, Pallas kernels for 0%

profile of v5, /device:TPU:32, one launch (start us, length us, event | category | flops | bytes accessed | tf_op | source)
XLA Modules:
  0.0 248.3 jit_solution(1112998235130670344)
XLA Ops:
  7.9 2.0 fusion.23
  11.5 2.7 %collective-permute-start.1 = (bf16[3,1024,256]{2,1,0:T(8,128)(2,1)}, bf16[3,1024,256]{2,1,0:T(8,128)(2,1)}, u32[]{:S(2)}, u32[]{:S(2)}) collective-permute-start(bf16[3,1024,256]{2,1,0:T(8,128)(2,1)} %param.9), channel_id=1, source_target_pairs={{0,128},{32,160},{64,192},{96,224},{128,0},{160,32},{192,64},{224,... | collective-permute-start | bytes 4718600 | tf_op jit(solution)/shard_map/ppermute | solution.py:74
  16.6 31.3 %collective-permute-done = bf16[3,1024,256]{2,1,0:T(8,128)(2,1)} collective-permute-done((bf16[3,1024,256]{2,1,0:T(8,128)(2,1)}, bf16[3,1024,256]{2,1,0:T(8,128)(2,1)}, u32[]{:S(2)}, u32[]{:S(2)}) %collective-permute-start) | collective-permute-done | bytes 1572896 | tf_op jit(solution)/shard_map/ppermute | solution.py:74
  47.9 34.5 %collective-permute-done.1 = bf16[3,1024,256]{2,1,0:T(8,128)(2,1)} collective-permute-done((bf16[3,1024,256]{2,1,0:T(8,128)(2,1)}, bf16[3,1024,256]{2,1,0:T(8,128)(2,1)}, u32[]{:S(2)}, u32[]{:S(2)}) %collective-permute-start.1) | collective-permute-done | bytes 1572896 | tf_op jit(solution)/shard_map/ppermute | solution.py:74
  82.9 6.1 %broadcast_in_dim.2 = bf16[3,8192,256]{1,2,0:T(8,128)(2,1)} broadcast(bf16[]{:T(256)} %constant.21.clone.1), dimensions={} | broadcast | bytes 12582914 | tf_op jit(solution)/shard_map/broadcast_in_dim | solution.py:77
  91.0 2.6 %copy.24 = bf16[3,1024,256]{1,2,0:T(8,128)(2,1)} copy(bf16[3,1024,256]{2,1,0:T(8,128)(2,1)} %collective-permute-done) | data formatting | bytes 3145728 | tf_op jit(solution)/shard_map/ppermute | solution.py:74
  93.6 2.6 %copy.25 = bf16[3,1024,256]{1,2,0:T(8,128)(2,1)} copy(bf16[3,1024,256]{2,1,0:T(8,128)(2,1)} %collective-permute-done.1) | data formatting | bytes 3145728 | tf_op jit(solution)/shard_map/ppermute | solution.py:74
  98.0 1.7 copy.27
  99.7 2.9 %constant_dynamic-update-slice_fusion.6 = bf16[3,8192,256]{1,2,0:T(8,128)(2,1)} fusion(bf16[3,8192,256]{1,2,0:T(8,128)(2,1)} %constant_dynamic-update-slice_fusion.7, bf16[3,1024,256]{1,2,0:T(8,128)(2,1)} %copy.24, s32[]{:T(128)S(6)} %select_n.41), kind=kLoop, calls=%fused_computation.61 | loop fusion | bytes 3145732 | tf_op jit(solution)/shard_map/dynamic_update_slice | solution.py:79
  106.5 1.7 copy.28
  108.2 1.7 copy.29
  109.9 2.7 %copy.30 = bf16[3,1024,256]{1,2,0:T(8,128)(2,1)} copy(bf16[3,1024,256]{2,1,0:T(8,128)(2,1)} %collective-permute-done.6) | data formatting | bytes 3145728 | tf_op jit(solution)/shard_map/ppermute | solution.py:76
  116.5 34.2 %all-gather.2.cloned.1.call-done = bf16[1024,8192]{1,0:T(8,128)(2,1)} async-done(((bf16[32,8192]{1,0:T(8,128)(2,1)}), bf16[1024,8192]{1,0:T(8,128)(2,1)}) %all-gather.2.cloned.1.call-update) | async-done | bytes 16777232 | tf_op jit(solution)/shard_map/all_gather | solution.py:87
  150.7 18.8 %fusion.15 = bf16[3,1024,256]{2,1,0:T(8,128)(2,1)S(1)} fusion(bf16[3,8192,256]{1,2,0:T(8,128)(2,1)} %constant_dynamic-update-slice_fusion, bf16[1024,8192]{1,0:T(8,128)(2,1)} %all-gather.2.cloned.1.call-done), kind=kOutput, calls=%fused_computation.21 | convolution fusion | flops 12885688320 | bytes 30932992 | tf_op jit(solution)/shard_map/tf,ifc->itc/dot_general | solution.py:90
  171.9 2.6 %fusion.2 = f32[3,1024,256]{2,1,0:T(8,128)S(1)} fusion(f32[3,1030,256]{2,1,0:T(8,128)S(1)} %maximum_convert_fusion, f32[3,256]{1,0:T(4,128)S(1)} %get-tuple-element.20, f32[3,256]{1,0:T(4,128)S(1)} %get-tuple-element.21, f32[3,256]{1,0:T(4,128)S(1)} %get-tuple-element.22, f32[3,256]{1,0:T(4,128)S(1)} %get-tuple-element.23, ...), kind=kLoop, calls=%fused_computation.3 | loop fusion | flops 10223616 | bytes 25187328 | tf_op jit(solution)/shard_map/add | solution.py:104
  175.6 7.7 %shard_map.73 = (f32[1024,256]{1,0:T(8,128)}, f32[16,256]{1,0:T(8,128)}) custom-call(f32[1024,256]{1,0:T(8,128)} %fusion.24.x_ref, f32[16,256]{1,0:T(8,128)} %get-tuple-element.19.r_ref, f32[16,256]{1,0:T(8,128)} %get-tuple-element.18.b_ref, f32[16,256]{1,0:T(8,128)} %res_ref.1), custom_call_target="tpu_custom_call" | custom-call | tf_op jit(solution)/shard_map/pallas_call | solution.py:50
  183.3 4.1 %collective-permute-start.8 = (f32[16,256]{1,0:T(8,128)}, f32[16,256]{1,0:T(8,128)S(1)}, u32[]{:S(2)}, u32[]{:S(2)}) collective-permute-start(f32[16,256]{1,0:T(8,128)} %get-tuple-element.8), channel_id=1, source_target_pairs={{0,32},{32,64},{64,96},{96,128},{128,160},{160,192},{192,224},{1,3... | collective-permute-start | bytes 49160 | tf_op jit(solution)/shard_map/ppermute | solution.py:13
  188.4 4.2 %collective-permute-start.9 = (f32[16,256]{1,0:T(8,128)S(1)}, f32[16,256]{1,0:T(8,128)S(1)}, u32[]{:S(2)}, u32[]{:S(2)}) collective-permute-start(f32[16,256]{1,0:T(8,128)S(1)} %collective-permute-done.8), channel_id=1, source_target_pairs={{0,32},{32,64},{64,96},{96,128},{128,160},{160,192},{192,224},{1,3... | collective-permute-start | bytes 49160 | tf_op jit(solution)/shard_map/ppermute | solution.py:13
  193.4 6.4 %collective-permute-start.10 = (f32[16,256]{1,0:T(8,128)S(1)}, f32[16,256]{1,0:T(8,128)S(1)}, u32[]{:S(2)}, u32[]{:S(2)}) collective-permute-start(f32[16,256]{1,0:T(8,128)S(1)} %multiply_add_fusion.2), channel_id=1, source_target_pairs={{0,64},{32,96},{64,128},{96,160},{128,192},{160,224},{1,65},{33,97... | collective-permute-start | bytes 49160 | tf_op jit(solution)/shard_map/ppermute | solution.py:13
  201.3 5.7 %collective-permute-start.11 = (f32[16,256]{1,0:T(8,128)S(1)}, f32[16,256]{1,0:T(8,128)S(1)}, u32[]{:S(2)}, u32[]{:S(2)}) collective-permute-start(f32[16,256]{1,0:T(8,128)S(1)} %multiply_add_fusion.1), channel_id=1, source_target_pairs={{0,128},{32,160},{64,192},{96,224},{1,129},{33,161},{65,193},{97,2... | collective-permute-start | bytes 49160 | tf_op jit(solution)/shard_map/ppermute | solution.py:13
  210.0 3.9 %fusion.18 = f32[8,128,256]{1,0,2:T(8,128)} fusion(f32[128]{0:T(128)} %iota_add_fusion, f32[16,256]{0,1:T(8,128)S(1)} %copy.33, f32[16,256]{0,1:T(8,128)S(1)} %copy.32, f32[16,256]{0,1:T(8,128)S(1)} %copy.35, f32[8]{0:T(128)} %iota_multiply_fusion), kind=kOutput, calls=%fused_computation.22 | convolution fusion | flops 26279936 | bytes 1098272 | tf_op jit(solution)/shard_map/jmc,mtc->jtc/dot_general | solution.py:129
  213.9 2.5 %copy.36 = f32[8,128,256]{2,1,0:T(8,128)} copy(f32[8,128,256]{1,0,2:T(8,128)} %fusion.18) | data formatting | bytes 2097152 | tf_op jit(solution)/shard_map/jmc,mtc->jtc/transpose | solution.py:129
  216.4 1.9 fusion.26
  218.3 22.3 %all_to_all.19 = bf16[32,32,256]{2,1,0:T(8,128)(2,1)S(1)} all-to-all(bf16[32,32,256]{2,1,0:T(8,128)(2,1)S(1)} %bitcast.47), channel_id=1, replica_groups=mesh['ctx'=8,'ch'=32] {'ch'}, dimensions={0} | all-to-all | bytes 1048576 | tf_op jit(solution)/shard_map/all_to_all | solution.py:132
  (62 shorter events, 27.9 us)
Async XLA Ops:
  6.5 9.2 %copy-start.2 = (bf16[3,1024,256]{2,1,0:T(8,128)(2,1)S(1)}, bf16[3,1024,256]{2,1,0:T(8,128)(2,1)}, u32[]{:S(2)}) copy-start(bf16[3,1024,256]{2,1,0:T(8,128)(2,1)} %param.9) | copy-start | bytes 4718596
  6.5 144.1 %all-gather.2.cloned.1.call-start = ((), (), s32[]{:S(2)}) async-start(), calls=%async_computation.1 | async-start | bytes 17301504 | tf_op jit(solution)/shard_map/all_gather | solution.py:87
  10.0 37.9 %collective-permute-start = (bf16[3,1024,256]{2,1,0:T(8,128)(2,1)}, bf16[3,1024,256]{2,1,0:T(8,128)(2,1)}, u32[]{:S(2)}, u32[]{:S(2)}) collective-permute-start(bf16[3,1024,256]{2,1,0:T(8,128)(2,1)} %param.9), channel_id=1, source_target_pairs={{0,64},{32,96},{64,128},{96,160},{128,192},{160,224},{192,0},{224,... | collective-permute-start | bytes 4718600 | tf_op jit(solution)/shard_map/ppermute | solution.py:74
  11.5 70.9 %collective-permute-start.1 = (bf16[3,1024,256]{2,1,0:T(8,128)(2,1)}, bf16[3,1024,256]{2,1,0:T(8,128)(2,1)}, u32[]{:S(2)}, u32[]{:S(2)}) collective-permute-start(bf16[3,1024,256]{2,1,0:T(8,128)(2,1)} %param.9), channel_id=1, source_target_pairs={{0,128},{32,160},{64,192},{96,224},{128,0},{160,32},{192,64},{224,... | collective-permute-start | bytes 4718600 | tf_op jit(solution)/shard_map/ppermute | solution.py:74
  14.3 68.1 %collective-permute-start.2 = (bf16[3,1024,256]{2,1,0:T(8,128)(2,1)}, bf16[3,1024,256]{2,1,0:T(8,128)(2,1)}, u32[]{:S(2)}, u32[]{:S(2)}) collective-permute-start(bf16[3,1024,256]{2,1,0:T(8,128)(2,1)} %param.9), channel_id=1, source_target_pairs={{0,192},{32,224},{64,0},{96,32},{128,64},{160,96},{192,128},{224,1... | collective-permute-start | bytes 4718600 | tf_op jit(solution)/shard_map/ppermute | solution.py:74
  15.7 82.3 %collective-permute-start.3 = (bf16[3,1024,256]{2,1,0:T(8,128)(2,1)}, bf16[3,1024,256]{2,1,0:T(8,128)(2,1)}, u32[]{:S(2)}, u32[]{:S(2)}) collective-permute-start(bf16[3,1024,256]{2,1,0:T(8,128)(2,1)} %param.9), channel_id=1, source_target_pairs={{0,32},{32,0},{64,96},{96,64},{128,160},{160,128},{192,224},{224,1... | collective-permute-start | bytes 4718600 | tf_op jit(solution)/shard_map/ppermute | solution.py:76
  47.9 58.6 %collective-permute-start.4 = (bf16[3,1024,256]{2,1,0:T(8,128)(2,1)}, bf16[3,1024,256]{2,1,0:T(8,128)(2,1)}, u32[]{:S(2)}, u32[]{:S(2)}) collective-permute-start(bf16[3,1024,256]{2,1,0:T(8,128)(2,1)} %collective-permute-done), channel_id=1, source_target_pairs={{0,32},{32,0},{64,96},{96,64},{128,160},{160,128},{192,224},{224,1... | collective-permute-start | bytes 4718600 | tf_op jit(solution)/shard_map/ppermute | solution.py:76
  82.4 25.8 %collective-permute-start.5 = (bf16[3,1024,256]{2,1,0:T(8,128)(2,1)}, bf16[3,1024,256]{2,1,0:T(8,128)(2,1)}, u32[]{:S(2)}, u32[]{:S(2)}) collective-permute-start(bf16[3,1024,256]{2,1,0:T(8,128)(2,1)} %collective-permute-done.1), channel_id=1, source_target_pairs={{0,32},{32,0},{64,96},{96,64},{128,160},{160,128},{192,224},{224,1... | collective-permute-start | bytes 4718600 | tf_op jit(solution)/shard_map/ppermute | solution.py:76
  82.4 27.5 %collective-permute-start.6 = (bf16[3,1024,256]{2,1,0:T(8,128)(2,1)}, bf16[3,1024,256]{2,1,0:T(8,128)(2,1)}, u32[]{:S(2)}, u32[]{:S(2)}) collective-permute-start(bf16[3,1024,256]{2,1,0:T(8,128)(2,1)} %collective-permute-done.2), channel_id=1, source_target_pairs={{0,32},{32,0},{64,96},{96,64},{128,160},{160,128},{192,224},{224,1... | collective-permute-start | bytes 4718600 | tf_op jit(solution)/shard_map/ppermute | solution.py:76
  89.0 1.3 copy-start.5
  89.0 1.4 copy-start.3
  99.7 2.9 %copy-start = (bf16[3,1024,256]{1,2,0:T(8,128)(2,1)S(1)}, bf16[3,1024,256]{1,2,0:T(8,128)(2,1)}, u32[]{:S(2)}) copy-start(bf16[3,1024,256]{1,2,0:T(8,128)(2,1)} %copy.25) | copy-start | bytes 4718596
  112.6 2.6 %copy-start.1 = (bf16[3,1024,256]{1,2,0:T(8,128)(2,1)S(1)}, bf16[3,1024,256]{1,2,0:T(8,128)(2,1)}, u32[]{:S(2)}) copy-start(bf16[3,1024,256]{1,2,0:T(8,128)(2,1)} %copy.30) | copy-start | bytes 4718596
  169.5 2.1 collective-permute-start.7
  174.5 33.1 %copy-start.4 = (f32[16,256]{1,0:T(8,128)S(1)}, f32[16,256]{1,0:T(8,128)}, u32[]{:S(2)}) copy-start(f32[16,256]{1,0:T(8,128)} %res_ref.1) | copy-start | bytes 49156
  183.3 5.1 %collective-permute-start.8 = (f32[16,256]{1,0:T(8,128)}, f32[16,256]{1,0:T(8,128)S(1)}, u32[]{:S(2)}, u32[]{:S(2)}) collective-permute-start(f32[16,256]{1,0:T(8,128)} %get-tuple-element.8), channel_id=1, source_target_pairs={{0,32},{32,64},{64,96},{96,128},{128,160},{160,192},{192,224},{1,3... | collective-permute-start | bytes 49160 | tf_op jit(solution)/shard_map/ppermute | solution.py:13
  188.4 5.0 %collective-permute-start.9 = (f32[16,256]{1,0:T(8,128)S(1)}, f32[16,256]{1,0:T(8,128)S(1)}, u32[]{:S(2)}, u32[]{:S(2)}) collective-permute-start(f32[16,256]{1,0:T(8,128)S(1)} %collective-permute-done.8), channel_id=1, source_target_pairs={{0,32},{32,64},{64,96},{96,128},{128,160},{160,192},{192,224},{1,3... | collective-permute-start | bytes 49160 | tf_op jit(solution)/shard_map/ppermute | solution.py:13
  193.4 7.8 %collective-permute-start.10 = (f32[16,256]{1,0:T(8,128)S(1)}, f32[16,256]{1,0:T(8,128)S(1)}, u32[]{:S(2)}, u32[]{:S(2)}) collective-permute-start(f32[16,256]{1,0:T(8,128)S(1)} %multiply_add_fusion.2), channel_id=1, source_target_pairs={{0,64},{32,96},{64,128},{96,160},{128,192},{160,224},{1,65},{33,97... | collective-permute-start | bytes 49160 | tf_op jit(solution)/shard_map/ppermute | solution.py:13
  201.3 7.1 %collective-permute-start.11 = (f32[16,256]{1,0:T(8,128)S(1)}, f32[16,256]{1,0:T(8,128)S(1)}, u32[]{:S(2)}, u32[]{:S(2)}) collective-permute-start(f32[16,256]{1,0:T(8,128)S(1)} %multiply_add_fusion.1), channel_id=1, source_target_pairs={{0,128},{32,160},{64,192},{96,224},{1,129},{33,161},{65,193},{97,2... | collective-permute-start | bytes 49160 | tf_op jit(solution)/shard_map/ppermute | solution.py:13
  209.2 7.3 %copy-start.6 = (f32[256]{0:T(256)S(1)}, f32[256]{0:T(256)}, u32[]{:S(2)}) copy-start(f32[256]{0:T(256)} %param.13) | copy-start | bytes 3076
Sparse Core Ops, SparseCore 0:
  10.1 140.5 all-gather.1

commit v6 on v5

--- a/solution.py
+++ b/solution.py
@@ -111,13 +111,13 @@
     retention = jnp.exp(-decay_rate)
     in_scale = jnp.sqrt(-jnp.expm1(-2.0 * decay_rate))
     local_filtered, local_end = modal_filter(mixed, retention, in_scale, residue)
-    incoming = shifted(local_end, "ctx", 1)
-    reach = 1
-    while reach < lax.axis_size("ctx"):
-        incoming = incoming + jnp.exp(-decay_rate * float(row_count * reach)) * shifted(
-            incoming, "ctx", reach
-        )
-        reach *= 2
+    range_count = lax.axis_size("ctx")
+    later = jnp.arange(range_count) - lax.axis_index("ctx") - 1
+    lag = (float(row_count) * jnp.maximum(later, 0).astype(jnp.float32))[:, None, None]
+    sent = jnp.where((later >= 0)[:, None, None], jnp.exp(-decay_rate[None] * lag), 0.0)
+    sent = sent * local_end[None]
+    received = lax.all_to_all(sent, "ctx", split_axis=0, concat_axis=0, tiled=True)
+    incoming = jnp.sum(received, axis=0)
     span_rows = min(128, row_count)
     span_count = row_count // span_rows
     positions = jnp.arange(span_rows, dtype=jnp.float32)

time: 250 us -> 242 us (0.968)
  starting transfers between devices: 28 us -> 14.7 us
  blocking collectives: 22.3 us -> 24.9 us
    ppermute x5 -> x1, starting transfers between devices: 21.7 us -> 1.29 us  [shifted(): return lax.ppermute(shard, axis, pairs)]
    ppermute x3, waiting for transfers between devices: 65.8 us -> 58.4 us  [gathered_weight(): held.append((lax.ppermute(block, 'ctx', pairs), (me - by) % count))]
    all_gather x1, waiting for transfers between devices: 34.2 us -> 41.4 us  [on_device_body(): gathered = lax.all_gather(normed, 'ch', axis=0, tiled=True)]
    all_to_all x0 -> x1, starting transfers between devices: none -> 7.16 us  [on_device_body(): lax.all_to_all(sent, 'ctx', split_axis=0, concat_axis=0, tiled=True)]
    all_to_all x0 -> x1, waiting for transfers between devices: none -> 4.12 us  [on_device_body(): lax.all_to_all(sent, 'ctx', split_axis=0, concat_axis=0, tiled=True)]
    ppermute x5 -> x1, waiting for transfers between devices: 4.3 us -> 0.79 us  [shifted(): return lax.ppermute(shard, axis, pairs)]
    all_to_all x1, blocking collectives: 22.3 us -> 24.9 us  [on_device_body(): return lax.all_to_all(gated, 'ch', split_axis=0, concat_axis=1, tiled=True)]
  transfers between devices with their start and end apart: 13 -> 10, of which waited for: 8 -> 5; matrix products, arithmetic and copies ran while one was open for 14% -> 15% of each run, Pallas kernels for 0% -> 0%
where the time goes in v6:
time: 242 us
  waiting for transfers between devices  105 us (43%)
  local copies, waits for them, and re-layouts  39.4 us (16%)
  blocking collectives  24.9 us (10%)
  matrix products  22.8 us (9%)
  starting transfers between devices  14.7 us (6%)
  other arithmetic  13.9 us (6%)
  between operations  13.7 us (6%)
  Pallas kernels  7.62 us (3%)
    ppermute x3, waiting for transfers between devices, gathered_weight(): held.append((lax.ppermute(block, 'ctx', pairs), (me - by) % count))  58.4 us
    all_gather x1, waiting for transfers between devices, on_device_body(): gathered = lax.all_gather(normed, 'ch', axis=0, tiled=True)  41.4 us
    all_to_all x1, blocking collectives, on_device_body(): return lax.all_to_all(gated, 'ch', split_axis=0, concat_axis=1, tiled=True)  24.9 us
    dot_general x1, matrix products, on_device_body(): jnp.einsum('tf,ifc->itc', gathered, gathered_weight(proj_weight), preferr...  18.8 us
    dynamic_update_slice x8, local copies, waits for them, and re-layouts, gathered_weight(): full = lax.dynamic_update_slice(full, part, (0, src * width, 0))  12.1 us
    ppermute x4, local copies, waits for them, and re-layouts, gathered_weight(): lax.ppermute(part, 'ctx', sibling)  7.79 us
    pallas_call x1, Pallas kernels, modal_filter(): pl.pallas_call(modal_kernel, grid=(chans // lanes,), in_specs=[pl.BlockSp...  7.62 us
    all_to_all x1, starting transfers between devices, on_device_body(): lax.all_to_all(sent, 'ctx', split_axis=0, concat_axis=0, tiled=True)  7.16 us
  transfers between devices with their start and end apart: 10, of which 5 were waited for; matrix products, arithmetic and copies ran while one was open for 15% of the time, Pallas kernels for 0%

profile of v6, /device:TPU:32, one launch (start us, length us, event | category | flops | bytes accessed | tf_op | source)
XLA Modules:
  0.0 241.7 jit_solution(2115145366765738878)
XLA Ops:
  7.9 2.0 fusion.23
  10.0 1.6 collective-permute-start
  11.5 2.7 %collective-permute-start.1 = (bf16[3,1024,256]{2,1,0:T(8,128)(2,1)}, bf16[3,1024,256]{2,1,0:T(8,128)(2,1)}, u32[]{:S(2)}, u32[]{:S(2)}) collective-permute-start(bf16[3,1024,256]{2,1,0:T(8,128)(2,1)} %param.9), channel_id=1, source_target_pairs={{0,128},{32,160},{64,192},{96,224},{128,0},{160,32},{192,64},{224,... | collective-permute-start | bytes 4718600 | tf_op jit(solution)/shard_map/ppermute | solution.py:74
  16.7 6.1 %broadcast_in_dim.14 = bf16[3,8192,256]{1,2,0:T(8,128)(2,1)} broadcast(bf16[]{:T(256)} %constant.44.clone.1), dimensions={} | broadcast | bytes 12582914 | tf_op jit(solution)/shard_map/broadcast_in_dim | solution.py:77
  24.0 23.8 %collective-permute-done = bf16[3,1024,256]{2,1,0:T(8,128)(2,1)} collective-permute-done((bf16[3,1024,256]{2,1,0:T(8,128)(2,1)}, bf16[3,1024,256]{2,1,0:T(8,128)(2,1)}, u32[]{:S(2)}, u32[]{:S(2)}) %collective-permute-start) | collective-permute-done | bytes 1572896 | tf_op jit(solution)/shard_map/ppermute | solution.py:74
  47.9 34.5 %collective-permute-done.1 = bf16[3,1024,256]{2,1,0:T(8,128)(2,1)} collective-permute-done((bf16[3,1024,256]{2,1,0:T(8,128)(2,1)}, bf16[3,1024,256]{2,1,0:T(8,128)(2,1)}, u32[]{:S(2)}, u32[]{:S(2)}) %collective-permute-start.1) | collective-permute-done | bytes 1572896 | tf_op jit(solution)/shard_map/ppermute | solution.py:74
  83.6 2.6 %copy.39 = bf16[3,1024,256]{1,2,0:T(8,128)(2,1)} copy(bf16[3,1024,256]{2,1,0:T(8,128)(2,1)} %collective-permute-done) | data formatting | bytes 3145728 | tf_op jit(solution)/shard_map/ppermute | solution.py:74
  86.2 2.6 %copy.40 = bf16[3,1024,256]{1,2,0:T(8,128)(2,1)} copy(bf16[3,1024,256]{2,1,0:T(8,128)(2,1)} %collective-permute-done.1) | data formatting | bytes 3145728 | tf_op jit(solution)/shard_map/ppermute | solution.py:74
  88.8 1.7 copy.41
  90.6 1.7 copy.42
  92.3 3.1 %constant_dynamic-update-slice_fusion.6 = bf16[3,8192,256]{1,2,0:T(8,128)(2,1)} fusion(bf16[3,8192,256]{1,2,0:T(8,128)(2,1)} %constant_dynamic-update-slice_fusion.7, bf16[3,1024,256]{1,2,0:T(8,128)(2,1)} %copy.39, s32[]{:T(128)S(6)} %select_n.45), kind=kLoop, calls=%fused_computation.54 | loop fusion | bytes 3145732 | tf_op jit(solution)/shard_map/dynamic_update_slice | solution.py:79
  99.2 1.7 copy.43
  101.0 1.7 copy.44
  102.7 2.6 %copy.45 = bf16[3,1024,256]{1,2,0:T(8,128)(2,1)} copy(bf16[3,1024,256]{2,1,0:T(8,128)(2,1)} %collective-permute-done.6) | data formatting | bytes 3145728 | tf_op jit(solution)/shard_map/ppermute | solution.py:76
  109.3 41.4 %all-gather.2.cloned.1.call-done = bf16[1024,8192]{1,0:T(8,128)(2,1)} async-done(((bf16[32,8192]{1,0:T(8,128)(2,1)}), bf16[1024,8192]{1,0:T(8,128)(2,1)}) %all-gather.2.cloned.1.call-update) | async-done | bytes 16777232 | tf_op jit(solution)/shard_map/all_gather | solution.py:87
  150.7 18.8 %fusion.15 = bf16[3,1024,256]{2,1,0:T(8,128)(2,1)S(1)} fusion(bf16[3,8192,256]{1,2,0:T(8,128)(2,1)} %constant_dynamic-update-slice_fusion, bf16[1024,8192]{1,0:T(8,128)(2,1)} %all-gather.2.cloned.1.call-done), kind=kOutput, calls=%fused_computation.21 | convolution fusion | flops 12885688320 | bytes 30932992 | tf_op jit(solution)/shard_map/tf,ifc->itc/dot_general | solution.py:90
  171.9 2.6 %fusion.2 = f32[3,1024,256]{2,1,0:T(8,128)S(1)} fusion(f32[3,1030,256]{2,1,0:T(8,128)S(1)} %maximum_convert_fusion, f32[3,256]{1,0:T(4,128)S(1)} %get-tuple-element.19, f32[3,256]{1,0:T(4,128)S(1)} %get-tuple-element.20, f32[3,256]{1,0:T(4,128)S(1)} %get-tuple-element.21, f32[3,256]{1,0:T(4,128)S(1)} %get-tuple-element.22, ...), kind=kLoop, calls=%fused_computation.3 | loop fusion | flops 10223616 | bytes 25187328 | tf_op jit(solution)/shard_map/add | solution.py:104
  175.6 7.6 %shard_map.73 = (f32[1024,256]{1,0:T(8,128)}, f32[16,256]{1,0:T(8,128)}) custom-call(f32[1024,256]{1,0:T(8,128)} %fusion.24.x_ref, f32[16,256]{1,0:T(8,128)} %get-tuple-element.17.r_ref, f32[16,256]{1,0:T(8,128)} %get-tuple-element.18.b_ref, f32[16,256]{1,0:T(8,128)} %res_ref.1), custom_call_target="tpu_custom_call" | custom-call | tf_op jit(solution)/shard_map/pallas_call | solution.py:50
  184.7 7.2 %all-to-all-start = ((f32[8,16,256]{2,1,0:T(8,128)}), f32[8,16,256]{2,1,0:T(8,128)S(1)}, u32[]{:S(2)}, u32[]{:S(2)}) async-start(f32[8,16,256]{2,1,0:T(8,128)} %select_multiply_fusion), calls=%async_computation | async-start | bytes 262144 | tf_op jit(solution)/shard_map/all_to_all | solution.py:119
  193.8 4.1 %all-to-all-done = f32[8,16,256]{2,1,0:T(8,128)S(1)} async-done(((f32[8,16,256]{2,1,0:T(8,128)}), f32[8,16,256]{2,1,0:T(8,128)S(1)}, u32[]{:S(2)}, u32[]{:S(2)}) %all-to-all-start) | async-done | bytes 131104 | tf_op jit(solution)/shard_map/all_to_all | solution.py:119
  200.7 4.0 %fusion.18 = f32[8,128,256]{1,0,2:T(8,128)} fusion(f32[8,16,256]{1,0,2:T(8,128)} %copy.49, f32[128]{0:T(128)} %iota_add_fusion, f32[16,256]{0,1:T(8,128)S(1)} %copy.48, f32[16,256]{0,1:T(8,128)S(1)} %copy.47), kind=kOutput, calls=%fused_computation.22 | convolution fusion | flops 26214400 | bytes 1212928 | tf_op jit(solution)/shard_map/jmc,mtc->jtc/dot_general | solution.py:129
  204.7 2.5 %copy.50 = f32[8,128,256]{2,1,0:T(8,128)} copy(f32[8,128,256]{1,0,2:T(8,128)} %fusion.18) | data formatting | bytes 2097152 | tf_op jit(solution)/shard_map/jmc,mtc->jtc/transpose | solution.py:129
  207.3 1.9 fusion.26
  209.2 24.9 %all_to_all.24 = bf16[32,32,256]{2,1,0:T(8,128)(2,1)S(1)} all-to-all(bf16[32,32,256]{2,1,0:T(8,128)(2,1)S(1)} %bitcast.48), channel_id=1, replica_groups=mesh['ctx'=8,'ch'=32] {'ch'}, dimensions={0} | all-to-all | bytes 1048576 | tf_op jit(solution)/shard_map/all_to_all | solution.py:132
  (56 shorter events, 24.5 us)
Async XLA Ops:
  6.5 9.2 %copy-start.2 = (bf16[3,1024,256]{2,1,0:T(8,128)(2,1)S(1)}, bf16[3,1024,256]{2,1,0:T(8,128)(2,1)}, u32[]{:S(2)}) copy-start(bf16[3,1024,256]{2,1,0:T(8,128)(2,1)} %param.9) | copy-start | bytes 4718596
  6.5 144.1 %all-gather.2.cloned.1.call-start = ((), (), s32[]{:S(2)}) async-start(), calls=%async_computation.2 | async-start | bytes 17301504 | tf_op jit(solution)/shard_map/all_gather | solution.py:87
  10.0 37.9 %collective-permute-start = (bf16[3,1024,256]{2,1,0:T(8,128)(2,1)}, bf16[3,1024,256]{2,1,0:T(8,128)(2,1)}, u32[]{:S(2)}, u32[]{:S(2)}) collective-permute-start(bf16[3,1024,256]{2,1,0:T(8,128)(2,1)} %param.9), channel_id=1, source_target_pairs={{0,64},{32,96},{64,128},{96,160},{128,192},{160,224},{192,0},{224,... | collective-permute-start | bytes 4718600 | tf_op jit(solution)/shard_map/ppermute | solution.py:74
  11.5 70.9 %collective-permute-start.1 = (bf16[3,1024,256]{2,1,0:T(8,128)(2,1)}, bf16[3,1024,256]{2,1,0:T(8,128)(2,1)}, u32[]{:S(2)}, u32[]{:S(2)}) collective-permute-start(bf16[3,1024,256]{2,1,0:T(8,128)(2,1)} %param.9), channel_id=1, source_target_pairs={{0,128},{32,160},{64,192},{96,224},{128,0},{160,32},{192,64},{224,... | collective-permute-start | bytes 4718600 | tf_op jit(solution)/shard_map/ppermute | solution.py:74
  14.3 68.1 %collective-permute-start.2 = (bf16[3,1024,256]{2,1,0:T(8,128)(2,1)}, bf16[3,1024,256]{2,1,0:T(8,128)(2,1)}, u32[]{:S(2)}, u32[]{:S(2)}) collective-permute-start(bf16[3,1024,256]{2,1,0:T(8,128)(2,1)} %param.9), channel_id=1, source_target_pairs={{0,192},{32,224},{64,0},{96,32},{128,64},{160,96},{192,128},{224,1... | collective-permute-start | bytes 4718600 | tf_op jit(solution)/shard_map/ppermute | solution.py:74
  15.7 74.8 %collective-permute-start.3 = (bf16[3,1024,256]{2,1,0:T(8,128)(2,1)}, bf16[3,1024,256]{2,1,0:T(8,128)(2,1)}, u32[]{:S(2)}, u32[]{:S(2)}) collective-permute-start(bf16[3,1024,256]{2,1,0:T(8,128)(2,1)} %param.9), channel_id=1, source_target_pairs={{0,32},{32,0},{64,96},{96,64},{128,160},{160,128},{192,224},{224,1... | collective-permute-start | bytes 4718600 | tf_op jit(solution)/shard_map/ppermute | solution.py:76
  22.7 1.3 copy-start.3
  22.7 60.2 %copy-start.4 = (f32[16,256]{1,0:T(8,128)S(1)}, f32[16,256]{1,0:T(8,128)}, u32[]{:S(2)}) copy-start(f32[16,256]{1,0:T(8,128)} %param.11) | copy-start | bytes 49156
  47.9 51.4 %collective-permute-start.4 = (bf16[3,1024,256]{2,1,0:T(8,128)(2,1)}, bf16[3,1024,256]{2,1,0:T(8,128)(2,1)}, u32[]{:S(2)}, u32[]{:S(2)}) collective-permute-start(bf16[3,1024,256]{2,1,0:T(8,128)(2,1)} %collective-permute-done), channel_id=1, source_target_pairs={{0,32},{32,0},{64,96},{96,64},{128,160},{160,128},{192,224},{224,1... | collective-permute-start | bytes 4718600 | tf_op jit(solution)/shard_map/ppermute | solution.py:76
  82.4 18.6 %collective-permute-start.5 = (bf16[3,1024,256]{2,1,0:T(8,128)(2,1)}, bf16[3,1024,256]{2,1,0:T(8,128)(2,1)}, u32[]{:S(2)}, u32[]{:S(2)}) collective-permute-start(bf16[3,1024,256]{2,1,0:T(8,128)(2,1)} %collective-permute-done.1), channel_id=1, source_target_pairs={{0,32},{32,0},{64,96},{96,64},{128,160},{160,128},{192,224},{224,1... | collective-permute-start | bytes 4718600 | tf_op jit(solution)/shard_map/ppermute | solution.py:76
  82.4 20.3 %collective-permute-start.6 = (bf16[3,1024,256]{2,1,0:T(8,128)(2,1)}, bf16[3,1024,256]{2,1,0:T(8,128)(2,1)}, u32[]{:S(2)}, u32[]{:S(2)}) collective-permute-start(bf16[3,1024,256]{2,1,0:T(8,128)(2,1)} %collective-permute-done.2), channel_id=1, source_target_pairs={{0,32},{32,0},{64,96},{96,64},{128,160},{160,128},{192,224},{224,1... | collective-permute-start | bytes 4718600 | tf_op jit(solution)/shard_map/ppermute | solution.py:76
  92.3 3.1 %copy-start = (bf16[3,1024,256]{1,2,0:T(8,128)(2,1)S(1)}, bf16[3,1024,256]{1,2,0:T(8,128)(2,1)}, u32[]{:S(2)}) copy-start(bf16[3,1024,256]{1,2,0:T(8,128)(2,1)} %copy.40) | copy-start | bytes 4718596
  105.4 2.6 %copy-start.1 = (bf16[3,1024,256]{1,2,0:T(8,128)(2,1)S(1)}, bf16[3,1024,256]{1,2,0:T(8,128)(2,1)}, u32[]{:S(2)}) copy-start(bf16[3,1024,256]{1,2,0:T(8,128)(2,1)} %copy.45) | copy-start | bytes 4718596
  169.5 2.1 collective-permute-start.7
  184.7 13.3 %all-to-all-start = ((f32[8,16,256]{2,1,0:T(8,128)}), f32[8,16,256]{2,1,0:T(8,128)S(1)}, u32[]{:S(2)}, u32[]{:S(2)}) async-start(f32[8,16,256]{2,1,0:T(8,128)} %select_multiply_fusion), calls=%async_computation | async-start | bytes 262144 | tf_op jit(solution)/shard_map/all_to_all | solution.py:119
  200.7 6.6 %copy-start.5 = (f32[256]{0:T(256)S(1)}, f32[256]{0:T(256)}, u32[]{:S(2)}) copy-start(f32[256]{0:T(256)} %param.13) | copy-start | bytes 3076
Sparse Core Ops, SparseCore 0:
  10.1 140.5 all-gather.1

commit v7 on v6

--- a/solution.py
+++ b/solution.py
@@ -16,52 +16,94 @@
 LANES = 128
 
 
-def modal_kernel(x_ref, r_ref, b_ref, res_ref, y_ref, end_ref):
+def ends_kernel(x_ref, r_ref, b_ref, end_ref):
+    half = r_ref.shape[0] // 2
+    r0, r1 = r_ref[:half, :], r_ref[half:, :]
+    b0, b1 = b_ref[:half, :], b_ref[half:, :]
+
+    def step8(i, carry):
+        s0, s1 = carry
+        xb = x_ref[pl.ds(pl.multiple_of(i * 8, 8), 8), :]
+        for k in range(8):
+            xt = xb[k : k + 1, :]
+            s0 = r0 * s0 + b0 * xt
+            s1 = r1 * s1 + b1 * xt
+        return s0, s1
+
+    zero = jnp.zeros((half, x_ref.shape[1]), jnp.float32)
+    s0, s1 = lax.fori_loop(0, x_ref.shape[0] // 8, step8, (zero, zero))
+    end_ref[:half, :] = s0
+    end_ref[half:, :] = s1
+
+
+def gate_kernel(x_ref, q_ref, r_ref, b_ref, res_ref, skip_ref, init_ref, out_ref):
     half = r_ref.shape[0] // 2
     r0, r1 = r_ref[:half, :], r_ref[half:, :]
     b0, b1 = b_ref[:half, :], b_ref[half:, :]
     q0, q1 = res_ref[:half, :], res_ref[half:, :]
-    rows = x_ref.shape[0]
+    skip = skip_ref[...]
 
-    def step8(i, carry):
+    def step16(i, carry):
         s0, s1 = carry
-        at = pl.multiple_of(i * 8, 8)
-        xb = x_ref[pl.ds(at, 8), :]
+        at = pl.multiple_of(i * 16, 16)
+        xb = x_ref[pl.ds(at, 16), :]
         outs = []
-        for k in range(8):
+        for k in range(16):
             xt = xb[k : k + 1, :]
             s0 = r0 * s0 + b0 * xt
             s1 = r1 * s1 + b1 * xt
             outs.append(jnp.sum(q0 * s0 + q1 * s1, axis=0, keepdims=True))
-        y_ref[pl.ds(at, 8), :] = jnp.concatenate(outs, axis=0)
+        filtered = jnp.concatenate(outs, axis=0)
+        out_ref[pl.ds(at, 16), :] = (q_ref[pl.ds(at, 16), :] * (filtered + skip * xb)).astype(
+            out_ref.dtype
+        )
         return s0, s1
 
-    zero = jnp.zeros((half, x_ref.shape[1]), jnp.float32)
-    s0, s1 = lax.fori_loop(0, rows // 8, step8, (zero, zero))
-    end_ref[:half, :] = s0
-    end_ref[half:, :] = s1
+    lax.fori_loop(0, x_ref.shape[0] // 16, step16, (init_ref[:half, :], init_ref[half:, :]))
 
 
-def modal_filter(x, retention, in_scale, residue):
+def lane_block(chans):
+    return next((w for w in (2 * LANES, LANES) if chans % w == 0), chans)
+
+
+def modal_ends(x, retention, in_scale):
     rows, chans = x.shape
     modes = retention.shape[0]
-    lanes = next((w for w in (2 * LANES, LANES) if chans % w == 0), chans)
+    lanes = lane_block(chans)
     col = lambda i: (0, i)
     return pl.pallas_call(
-        modal_kernel,
+        ends_kernel,
         grid=(chans // lanes,),
         in_specs=[
             pl.BlockSpec((rows, lanes), col),
             pl.BlockSpec((modes, lanes), col),
             pl.BlockSpec((modes, lanes), col),
+        ],
+        out_specs=pl.BlockSpec((modes, lanes), col),
+        out_shape=jax.ShapeDtypeStruct((modes, chans), jnp.float32),
+    )(x, retention, in_scale)
+
+
+def modal_gate(x, queries, retention, in_scale, residue, skip_gain, incoming):
+    rows, chans = x.shape
+    modes = retention.shape[0]
+    lanes = lane_block(chans)
+    col = lambda i: (0, i)
+    return pl.pallas_call(
+        gate_kernel,
+        grid=(chans // lanes,),
+        in_specs=[
+            pl.BlockSpec((rows, lanes), col),
+            pl.BlockSpec((rows, lanes), col),
+            pl.BlockSpec((modes, lanes), col),
+            pl.BlockSpec((modes, lanes), col),
+            pl.BlockSpec((modes, lanes), col),
+            pl.BlockSpec((1, lanes), col),
             pl.BlockSpec((modes, lanes), col),
         ],
-        out_specs=[pl.BlockSpec((rows, lanes), col), pl.BlockSpec((modes, lanes), col)],
-        out_shape=[
-            jax.ShapeDtypeStruct((rows, chans), jnp.float32),
-            jax.ShapeDtypeStruct((modes, chans), jnp.float32),
-        ],
-    )(x, retention, in_scale, residue)
+        out_specs=pl.BlockSpec((rows, lanes), col),
+        out_shape=jax.ShapeDtypeStruct((rows, chans), jnp.bfloat16),
+    )(x, queries, retention, in_scale, residue, skip_gain.reshape(1, chans), incoming)
 
 
 def gathered_weight(block):
@@ -107,10 +149,9 @@
         )
     queries = featured[0]
     mixed = featured[1] * featured[2]
-    high = lax.Precision.HIGH
     retention = jnp.exp(-decay_rate)
     in_scale = jnp.sqrt(-jnp.expm1(-2.0 * decay_rate))
-    local_filtered, local_end = modal_filter(mixed, retention, in_scale, residue)
+    local_end = modal_ends(mixed, retention, in_scale)
     range_count = lax.axis_size("ctx")
     later = jnp.arange(range_count) - lax.axis_index("ctx") - 1
     lag = (float(row_count) * jnp.maximum(later, 0).astype(jnp.float32))[:, None, None]
@@ -118,17 +159,7 @@
     sent = sent * local_end[None]
     received = lax.all_to_all(sent, "ctx", split_axis=0, concat_axis=0, tiled=True)
     incoming = jnp.sum(received, axis=0)
-    span_rows = min(128, row_count)
-    span_count = row_count // span_rows
-    positions = jnp.arange(span_rows, dtype=jnp.float32)
-    span_starts = jnp.arange(span_count, dtype=jnp.float32) * float(span_rows)
-    starts = jnp.exp(-decay_rate[None, :, :] * span_starts[:, None, None]) * incoming[None, :, :]
-    out_weight = residue[:, None, :] * jnp.exp(
-        -decay_rate[:, None, :] * (positions + 1.0)[None, :, None]
-    )
-    outside = jnp.einsum("jmc,mtc->jtc", starts, out_weight, precision=high)
-    filtered = local_filtered + outside.reshape(row_count, chan_count)
-    gated = (queries * (filtered + skip_gain[None, :] * mixed)).astype(jnp.bfloat16)
+    gated = modal_gate(mixed, queries, retention, in_scale, residue, skip_gain, incoming)
     return lax.all_to_all(gated, "ch", split_axis=0, concat_axis=1, tiled=True)
 
 

time: 242 us -> 235 us (0.971)
  blocking collectives: 24.9 us -> 38.1 us
  starting transfers between devices: 14.7 us -> 7.54 us
  local copies, waits for them, and re-layouts: 39.4 us -> 34.6 us
  matrix products: 22.8 us -> 18.8 us
  other arithmetic: 13.9 us -> 9.9 us
  waiting for transfers between devices: 105 us -> 101 us
  Pallas kernels: 7.62 us -> 11.6 us
    all_to_all x0 -> x1, blocking collectives: none -> 13.1 us  [on_device_body(): lax.all_to_all(sent, 'ctx', split_axis=0, concat_axis=0, tiled=True)]
    all_to_all x1 -> x0, starting transfers between devices: 7.16 us -> none  [on_device_body(): lax.all_to_all(sent, 'ctx', split_axis=0, concat_axis=0, tiled=True)]
    all_to_all x1 -> x0, waiting for transfers between devices: 4.12 us -> none  [on_device_body(): lax.all_to_all(sent, 'ctx', split_axis=0, concat_axis=0, tiled=True)]
    dot_general x1 -> x0, matrix products: 4.04 us -> none  [on_device_body(): outside = jnp.einsum('jmc,mtc->jtc', starts, out_weight, precision=high)]
    pallas_call x1 -> x2, Pallas kernels: 7.62 us -> 11.6 us  [the longest x1 7.35 us: modal_gate(): pl.pallas_call(gate_kernel, grid=(chans // lanes,), in_specs=[pl.BlockSpe...]
    transpose x1 -> x0, local copies, waits for them, and re-layouts: 2.53 us -> none  [on_device_body(): outside = jnp.einsum('jmc,mtc->jtc', starts, out_weight, precision=high)]
    mul x3 -> x0, other arithmetic: 2.47 us -> none  [the longest x1 1.12 us: on_device_body(): mixed = featured[1] * featured[2]]
  transfers between devices with their start and end apart: 10 -> 9, of which waited for: 5 -> 4; matrix products, arithmetic and copies ran while one was open for 15% -> 15% of each run, Pallas kernels for 0% -> 0%
where the time goes in v7:
time: 235 us
  waiting for transfers between devices  101 us (43%)
  blocking collectives  38.1 us (16%)
  local copies, waits for them, and re-layouts  34.6 us (15%)
  matrix products  18.8 us (8%)
  between operations  13.6 us (6%)
  Pallas kernels  11.6 us (5%)
  other arithmetic  9.9 us (4%)
  starting transfers between devices  7.54 us (3%)
    ppermute x3, waiting for transfers between devices, gathered_weight(): held.append((lax.ppermute(block, 'ctx', pairs), (me - by) % count))  58.4 us
    all_gather x1, waiting for transfers between devices, on_device_body(): gathered = lax.all_gather(normed, 'ch', axis=0, tiled=True)  41.4 us
    all_to_all x1, blocking collectives, on_device_body(): return lax.all_to_all(gated, 'ch', split_axis=0, concat_axis=1, tiled=True)  25.1 us
    dot_general x1, matrix products, on_device_body(): jnp.einsum('tf,ifc->itc', gathered, gathered_weight(proj_weight), preferr...  18.8 us
    all_to_all x1, blocking collectives, on_device_body(): lax.all_to_all(sent, 'ctx', split_axis=0, concat_axis=0, tiled=True)  13.1 us
    dynamic_update_slice x8, local copies, waits for them, and re-layouts, gathered_weight(): full = lax.dynamic_update_slice(full, part, (0, src * width, 0))  12.1 us
    ppermute x4, local copies, waits for them, and re-layouts, gathered_weight(): lax.ppermute(part, 'ctx', sibling)  7.79 us
    pallas_call x1, Pallas kernels, modal_gate(): pl.pallas_call(gate_kernel, grid=(chans // lanes,), in_specs=[pl.BlockSpe...  7.35 us
  transfers between devices with their start and end apart: 9, of which 4 were waited for; matrix products, arithmetic and copies ran while one was open for 15% of the time, Pallas kernels for 0%

profile of v7, /device:TPU:32, one launch (start us, length us, event | category | flops | bytes accessed | tf_op | source)
XLA Modules:
  0.0 234.8 jit_solution(12322396622896889469)
XLA Ops:
  6.5 1.4 fusion.14
  7.9 2.0 fusion.16
  10.0 1.6 collective-permute-start
  11.5 2.7 %collective-permute-start.1 = (bf16[3,1024,256]{2,1,0:T(8,128)(2,1)}, bf16[3,1024,256]{2,1,0:T(8,128)(2,1)}, u32[]{:S(2)}, u32[]{:S(2)}) collective-permute-start(bf16[3,1024,256]{2,1,0:T(8,128)(2,1)} %param.9), channel_id=1, source_target_pairs={{0,128},{32,160},{64,192},{96,224},{128,0},{160,32},{192,64},{224,... | collective-permute-start | bytes 4718600 | tf_op jit(solution)/shard_map/ppermute | solution.py:116
  14.3 1.4 collective-permute-start.2
  16.7 6.1 %broadcast_in_dim.14 = bf16[3,8192,256]{1,2,0:T(8,128)(2,1)} broadcast(bf16[]{:T(256)} %constant.42.clone.1), dimensions={} | broadcast | bytes 12582914 | tf_op jit(solution)/shard_map/broadcast_in_dim | solution.py:119
  24.1 23.8 %collective-permute-done = bf16[3,1024,256]{2,1,0:T(8,128)(2,1)} collective-permute-done((bf16[3,1024,256]{2,1,0:T(8,128)(2,1)}, bf16[3,1024,256]{2,1,0:T(8,128)(2,1)}, u32[]{:S(2)}, u32[]{:S(2)}) %collective-permute-start) | collective-permute-done | bytes 1572896 | tf_op jit(solution)/shard_map/ppermute | solution.py:116
  47.9 34.5 %collective-permute-done.1 = bf16[3,1024,256]{2,1,0:T(8,128)(2,1)} collective-permute-done((bf16[3,1024,256]{2,1,0:T(8,128)(2,1)}, bf16[3,1024,256]{2,1,0:T(8,128)(2,1)}, u32[]{:S(2)}, u32[]{:S(2)}) %collective-permute-start.1) | collective-permute-done | bytes 1572896 | tf_op jit(solution)/shard_map/ppermute | solution.py:116
  83.6 2.6 %copy.29 = bf16[3,1024,256]{1,2,0:T(8,128)(2,1)} copy(bf16[3,1024,256]{2,1,0:T(8,128)(2,1)} %collective-permute-done) | data formatting | bytes 3145728 | tf_op jit(solution)/shard_map/ppermute | solution.py:116
  86.2 2.6 %copy.30 = bf16[3,1024,256]{1,2,0:T(8,128)(2,1)} copy(bf16[3,1024,256]{2,1,0:T(8,128)(2,1)} %collective-permute-done.1) | data formatting | bytes 3145728 | tf_op jit(solution)/shard_map/ppermute | solution.py:116
  88.8 1.7 copy.31
  90.6 1.7 copy.32
  92.3 3.0 %constant_dynamic-update-slice_fusion.6 = bf16[3,8192,256]{1,2,0:T(8,128)(2,1)} fusion(bf16[3,8192,256]{1,2,0:T(8,128)(2,1)} %constant_dynamic-update-slice_fusion.7, bf16[3,1024,256]{1,2,0:T(8,128)(2,1)} %copy.29, s32[]{:T(128)S(6)} %select_n.45), kind=kLoop, calls=%fused_computation.41 | loop fusion | bytes 3145732 | tf_op jit(solution)/shard_map/dynamic_update_slice | solution.py:121
  99.2 1.7 copy.33
  101.0 1.7 copy.34
  102.7 2.6 %copy.35 = bf16[3,1024,256]{1,2,0:T(8,128)(2,1)} copy(bf16[3,1024,256]{2,1,0:T(8,128)(2,1)} %collective-permute-done.6) | data formatting | bytes 3145728 | tf_op jit(solution)/shard_map/ppermute | solution.py:118
  109.2 41.4 %all-gather.2.cloned.1.call-done = bf16[1024,8192]{1,0:T(8,128)(2,1)} async-done(((bf16[32,8192]{1,0:T(8,128)(2,1)}), bf16[1024,8192]{1,0:T(8,128)(2,1)}) %all-gather.2.cloned.1.call-update) | async-done | bytes 16777232 | tf_op jit(solution)/shard_map/all_gather | solution.py:129
  150.7 18.8 %fusion.11 = bf16[3,1024,256]{2,1,0:T(8,128)(2,1)S(1)} fusion(bf16[3,8192,256]{1,2,0:T(8,128)(2,1)} %constant_dynamic-update-slice_fusion, bf16[1024,8192]{1,0:T(8,128)(2,1)} %all-gather.2.cloned.1.call-done), kind=kOutput, calls=%fused_computation.17 | convolution fusion | flops 12885688320 | bytes 30932992 | tf_op jit(solution)/shard_map/tf,ifc->itc/dot_general | solution.py:132
  171.9 2.6 %fusion.2 = f32[3,1024,256]{2,1,0:T(8,128)S(1)} fusion(f32[3,1030,256]{2,1,0:T(8,128)S(1)} %maximum_convert_fusion, f32[3,256]{1,0:T(4,128)S(1)} %get-tuple-element.17, f32[3,256]{1,0:T(4,128)S(1)} %get-tuple-element.18, f32[3,256]{1,0:T(4,128)S(1)} %get-tuple-element.19, f32[3,256]{1,0:T(4,128)S(1)} %get-tuple-element.20, ...), kind=kLoop, calls=%fused_computation.3 | loop fusion | flops 10223616 | bytes 25187328 | tf_op jit(solution)/shard_map/add | solution.py:146
  174.5 1.5 slice_bitcast_fusion
  176.0 4.2 %shard_map.73 = f32[16,256]{1,0:T(8,128)} custom-call(f32[1024,256]{1,0:T(8,128)} %get-tuple-element.6.x_ref, f32[16,256]{1,0:T(8,128)} %get-tuple-element.15.r_ref, f32[16,256]{1,0:T(8,128)} %get-tuple-element.16.b_ref), custom_call_target="tpu_custom_call" | custom-call | tf_op jit(solution)/shard_map/pallas_call | solution.py:74
  181.1 13.1 %all_to_all.24 = f32[8,16,256]{2,1,0:T(8,128)S(1)} all-to-all(f32[8,16,256]{2,1,0:T(8,128)S(1)} %select_multiply_fusion), channel_id=1, replica_groups=mesh['ctx'=8,'ch'=32] {'ctx'}, dimensions={0} | all-to-all | bytes 262144 | tf_op jit(solution)/shard_map/all_to_all | solution.py:160
  194.7 7.4 %shard_map.74 = bf16[1024,256]{1,0:T(8,128)(2,1)} custom-call(f32[1024,256]{1,0:T(8,128)} %get-tuple-element.6.x_ref, f32[1024,256]{1,0:T(8,128)} %get-tuple-element.5.q_ref, f32[16,256]{1,0:T(8,128)} %get-tuple-element.15.r_ref, f32[16,256]{1,0:T(8,128)} %get-tuple-element.16.b_ref, f32[16,256]{1,0:T(8,128)} %res_ref.1, f32[1,256]{1,0:T(1,128)} %bitcast.37, ...), custom_call_target="tpu_custom_call" | custom-call | tf_op jit(solution)/shard_map/pallas_call | solution.py:92
  202.1 25.1 %all_to_all.25 = bf16[32,32,256]{2,1,0:T(8,128)(2,1)S(1)} all-to-all(bf16[32,32,256]{2,1,0:T(8,128)(2,1)} %bitcast.34), channel_id=1, replica_groups=mesh['ctx'=8,'ch'=32] {'ch'}, dimensions={0} | all-to-all | bytes 1048576 | tf_op jit(solution)/shard_map/all_to_all | solution.py:163
  (45 shorter events, 15.8 us)
Async XLA Ops:
  6.5 9.2 %copy-start.2 = (bf16[3,1024,256]{2,1,0:T(8,128)(2,1)S(1)}, bf16[3,1024,256]{2,1,0:T(8,128)(2,1)}, u32[]{:S(2)}) copy-start(bf16[3,1024,256]{2,1,0:T(8,128)(2,1)} %param.9) | copy-start | bytes 4718596
  6.5 144.1 %all-gather.2.cloned.1.call-start = ((), (), s32[]{:S(2)}) async-start(), calls=%async_computation.2 | async-start | bytes 17301504 | tf_op jit(solution)/shard_map/all_gather | solution.py:129
  10.0 37.9 %collective-permute-start = (bf16[3,1024,256]{2,1,0:T(8,128)(2,1)}, bf16[3,1024,256]{2,1,0:T(8,128)(2,1)}, u32[]{:S(2)}, u32[]{:S(2)}) collective-permute-start(bf16[3,1024,256]{2,1,0:T(8,128)(2,1)} %param.9), channel_id=1, source_target_pairs={{0,64},{32,96},{64,128},{96,160},{128,192},{160,224},{192,0},{224,... | collective-permute-start | bytes 4718600 | tf_op jit(solution)/shard_map/ppermute | solution.py:116
  11.5 70.9 %collective-permute-start.1 = (bf16[3,1024,256]{2,1,0:T(8,128)(2,1)}, bf16[3,1024,256]{2,1,0:T(8,128)(2,1)}, u32[]{:S(2)}, u32[]{:S(2)}) collective-permute-start(bf16[3,1024,256]{2,1,0:T(8,128)(2,1)} %param.9), channel_id=1, source_target_pairs={{0,128},{32,160},{64,192},{96,224},{128,0},{160,32},{192,64},{224,... | collective-permute-start | bytes 4718600 | tf_op jit(solution)/shard_map/ppermute | solution.py:116
  14.3 68.1 %collective-permute-start.2 = (bf16[3,1024,256]{2,1,0:T(8,128)(2,1)}, bf16[3,1024,256]{2,1,0:T(8,128)(2,1)}, u32[]{:S(2)}, u32[]{:S(2)}) collective-permute-start(bf16[3,1024,256]{2,1,0:T(8,128)(2,1)} %param.9), channel_id=1, source_target_pairs={{0,192},{32,224},{64,0},{96,32},{128,64},{160,96},{192,128},{224,1... | collective-permute-start | bytes 4718600 | tf_op jit(solution)/shard_map/ppermute | solution.py:116
  15.7 74.9 %collective-permute-start.3 = (bf16[3,1024,256]{2,1,0:T(8,128)(2,1)}, bf16[3,1024,256]{2,1,0:T(8,128)(2,1)}, u32[]{:S(2)}, u32[]{:S(2)}) collective-permute-start(bf16[3,1024,256]{2,1,0:T(8,128)(2,1)} %param.9), channel_id=1, source_target_pairs={{0,32},{32,0},{64,96},{96,64},{128,160},{160,128},{192,224},{224,1... | collective-permute-start | bytes 4718600 | tf_op jit(solution)/shard_map/ppermute | solution.py:118
  22.7 1.3 copy-start.3
  22.7 60.2 %copy-start.4 = (f32[16,256]{1,0:T(8,128)S(1)}, f32[16,256]{1,0:T(8,128)}, u32[]{:S(2)}) copy-start(f32[16,256]{1,0:T(8,128)} %param.11) | copy-start | bytes 49156
  47.9 51.4 %collective-permute-start.4 = (bf16[3,1024,256]{2,1,0:T(8,128)(2,1)}, bf16[3,1024,256]{2,1,0:T(8,128)(2,1)}, u32[]{:S(2)}, u32[]{:S(2)}) collective-permute-start(bf16[3,1024,256]{2,1,0:T(8,128)(2,1)} %collective-permute-done), channel_id=1, source_target_pairs={{0,32},{32,0},{64,96},{96,64},{128,160},{160,128},{192,224},{224,1... | collective-permute-start | bytes 4718600 | tf_op jit(solution)/shard_map/ppermute | solution.py:118
  82.4 18.6 %collective-permute-start.5 = (bf16[3,1024,256]{2,1,0:T(8,128)(2,1)}, bf16[3,1024,256]{2,1,0:T(8,128)(2,1)}, u32[]{:S(2)}, u32[]{:S(2)}) collective-permute-start(bf16[3,1024,256]{2,1,0:T(8,128)(2,1)} %collective-permute-done.1), channel_id=1, source_target_pairs={{0,32},{32,0},{64,96},{96,64},{128,160},{160,128},{192,224},{224,1... | collective-permute-start | bytes 4718600 | tf_op jit(solution)/shard_map/ppermute | solution.py:118
  82.4 20.3 %collective-permute-start.6 = (bf16[3,1024,256]{2,1,0:T(8,128)(2,1)}, bf16[3,1024,256]{2,1,0:T(8,128)(2,1)}, u32[]{:S(2)}, u32[]{:S(2)}) collective-permute-start(bf16[3,1024,256]{2,1,0:T(8,128)(2,1)} %collective-permute-done.2), channel_id=1, source_target_pairs={{0,32},{32,0},{64,96},{96,64},{128,160},{160,128},{192,224},{224,1... | collective-permute-start | bytes 4718600 | tf_op jit(solution)/shard_map/ppermute | solution.py:118
  92.3 3.1 %copy-start = (bf16[3,1024,256]{1,2,0:T(8,128)(2,1)S(1)}, bf16[3,1024,256]{1,2,0:T(8,128)(2,1)}, u32[]{:S(2)}) copy-start(bf16[3,1024,256]{1,2,0:T(8,128)(2,1)} %copy.30) | copy-start | bytes 4718596
  105.3 2.6 %copy-start.1 = (bf16[3,1024,256]{1,2,0:T(8,128)(2,1)S(1)}, bf16[3,1024,256]{1,2,0:T(8,128)(2,1)}, u32[]{:S(2)}) copy-start(bf16[3,1024,256]{1,2,0:T(8,128)(2,1)} %copy.35) | copy-start | bytes 4718596
  169.5 2.1 collective-permute-start.7
Sparse Core Ops, SparseCore 0:
  10.1 140.5 all-gather.1

commit v8 on v7

--- a/solution.py
+++ b/solution.py
@@ -16,24 +16,34 @@
 LANES = 128
 
 
+CHUNKS = 4
+
+
 def ends_kernel(x_ref, r_ref, b_ref, end_ref):
     half = r_ref.shape[0] // 2
     r0, r1 = r_ref[:half, :], r_ref[half:, :]
     b0, b1 = b_ref[:half, :], b_ref[half:, :]
+    chunks = end_ref.shape[0]
+    span = x_ref.shape[0] // chunks
 
     def step8(i, carry):
-        s0, s1 = carry
-        xb = x_ref[pl.ds(pl.multiple_of(i * 8, 8), 8), :]
-        for k in range(8):
-            xt = xb[k : k + 1, :]
-            s0 = r0 * s0 + b0 * xt
-            s1 = r1 * s1 + b1 * xt
-        return s0, s1
+        carry = list(carry)
+        at = pl.multiple_of(i * 8, 8)
+        for c in range(chunks):
+            s0, s1 = carry[2 * c], carry[2 * c + 1]
+            xb = x_ref[pl.ds(c * span + at, 8), :]
+            for k in range(8):
+                xt = xb[k : k + 1, :]
+                s0 = r0 * s0 + b0 * xt
+                s1 = r1 * s1 + b1 * xt
+            carry[2 * c], carry[2 * c + 1] = s0, s1
+        return tuple(carry)
 
     zero = jnp.zeros((half, x_ref.shape[1]), jnp.float32)
-    s0, s1 = lax.fori_loop(0, x_ref.shape[0] // 8, step8, (zero, zero))
-    end_ref[:half, :] = s0
-    end_ref[half:, :] = s1
+    ends = lax.fori_loop(0, span // 8, step8, (zero,) * (2 * chunks))
+    for c in range(chunks):
+        end_ref[c, :half, :] = ends[2 * c]
+        end_ref[c, half:, :] = ends[2 * c + 1]
 
 
 def gate_kernel(x_ref, q_ref, r_ref, b_ref, res_ref, skip_ref, init_ref, out_ref):
@@ -42,24 +52,31 @@
     b0, b1 = b_ref[:half, :], b_ref[half:, :]
     q0, q1 = res_ref[:half, :], res_ref[half:, :]
     skip = skip_ref[...]
+    chunks = init_ref.shape[0]
+    span = x_ref.shape[0] // chunks
 
     def step16(i, carry):
-        s0, s1 = carry
+        carry = list(carry)
         at = pl.multiple_of(i * 16, 16)
-        xb = x_ref[pl.ds(at, 16), :]
-        outs = []
-        for k in range(16):
-            xt = xb[k : k + 1, :]
-            s0 = r0 * s0 + b0 * xt
-            s1 = r1 * s1 + b1 * xt
-            outs.append(jnp.sum(q0 * s0 + q1 * s1, axis=0, keepdims=True))
-        filtered = jnp.concatenate(outs, axis=0)
-        out_ref[pl.ds(at, 16), :] = (q_ref[pl.ds(at, 16), :] * (filtered + skip * xb)).astype(
-            out_ref.dtype
-        )
-        return s0, s1
-
-    lax.fori_loop(0, x_ref.shape[0] // 16, step16, (init_ref[:half, :], init_ref[half:, :]))
+        for c in range(chunks):
+            s0, s1 = carry[2 * c], carry[2 * c + 1]
+            rows = pl.ds(c * span + at, 16)
+            xb = x_ref[rows, :]
+            outs = []
+            for k in range(16):
+                xt = xb[k : k + 1, :]
+                s0 = r0 * s0 + b0 * xt
+                s1 = r1 * s1 + b1 * xt
+                outs.append(jnp.sum(q0 * s0 + q1 * s1, axis=0, keepdims=True))
+            filtered = jnp.concatenate(outs, axis=0)
+            out_ref[rows, :] = (q_ref[rows, :] * (filtered + skip * xb)).astype(out_ref.dtype)
+            carry[2 * c], carry[2 * c + 1] = s0, s1
+        return tuple(carry)
+
+    init = []
+    for c in range(chunks):
+        init += [init_ref[c, :half, :], init_ref[c, half:, :]]
+    lax.fori_loop(0, span // 16, step16, tuple(init))
 
 
 def lane_block(chans):
@@ -79,8 +96,8 @@
             pl.BlockSpec((modes, lanes), col),
             pl.BlockSpec((modes, lanes), col),
         ],
-        out_specs=pl.BlockSpec((modes, lanes), col),
-        out_shape=jax.ShapeDtypeStruct((modes, chans), jnp.float32),
+        out_specs=pl.BlockSpec((CHUNKS, modes, lanes), lambda i: (0, 0, i)),
+        out_shape=jax.ShapeDtypeStruct((CHUNKS, modes, chans), jnp.float32),
     )(x, retention, in_scale)
 
 
@@ -99,7 +116,7 @@
             pl.BlockSpec((modes, lanes), col),
             pl.BlockSpec((modes, lanes), col),
             pl.BlockSpec((1, lanes), col),
-            pl.BlockSpec((modes, lanes), col),
+            pl.BlockSpec((CHUNKS, modes, lanes), lambda i: (0, 0, i)),
         ],
         out_specs=pl.BlockSpec((rows, lanes), col),
         out_shape=jax.ShapeDtypeStruct((rows, chans), jnp.bfloat16),
@@ -151,14 +168,21 @@
     mixed = featured[1] * featured[2]
     retention = jnp.exp(-decay_rate)
     in_scale = jnp.sqrt(-jnp.expm1(-2.0 * decay_rate))
-    local_end = modal_ends(mixed, retention, in_scale)
+    chunk_ends = modal_ends(mixed, retention, in_scale)
+    chunk_decay = jnp.exp(-decay_rate * float(row_count // CHUNKS))
+    local_end = chunk_ends[0]
+    for c in range(1, CHUNKS):
+        local_end = chunk_decay * local_end + chunk_ends[c]
     range_count = lax.axis_size("ctx")
     later = jnp.arange(range_count) - lax.axis_index("ctx") - 1
     lag = (float(row_count) * jnp.maximum(later, 0).astype(jnp.float32))[:, None, None]
     sent = jnp.where((later >= 0)[:, None, None], jnp.exp(-decay_rate[None] * lag), 0.0)
     sent = sent * local_end[None]
     received = lax.all_to_all(sent, "ctx", split_axis=0, concat_axis=0, tiled=True)
-    incoming = jnp.sum(received, axis=0)
+    starts = [jnp.sum(received, axis=0)]
+    for c in range(1, CHUNKS):
+        starts.append(chunk_decay * starts[-1] + chunk_ends[c - 1])
+    incoming = jnp.stack(starts)
     gated = modal_gate(mixed, queries, retention, in_scale, residue, skip_gain, incoming)
     return lax.all_to_all(gated, "ch", split_axis=0, concat_axis=1, tiled=True)
 

time: 235 us -> 235 us (level)
  no operation moved by 1% of the time
where the time goes in v8:
time: 235 us
  waiting for transfers between devices  101 us (43%)
  blocking collectives  38.1 us (16%)
  local copies, waits for them, and re-layouts  34.6 us (15%)
  matrix products  18.8 us (8%)
  between operations  13.7 us (6%)
  other arithmetic  10.8 us (5%)
  Pallas kernels  10.6 us (5%)
  starting transfers between devices  7.54 us (3%)
    ppermute x3, waiting for transfers between devices, gathered_weight(): held.append((lax.ppermute(block, 'ctx', pairs), (me - by) % count))  58.3 us
    all_gather x1, waiting for transfers between devices, on_device_body(): gathered = lax.all_gather(normed, 'ch', axis=0, tiled=True)  41.5 us
    all_to_all x1, blocking collectives, on_device_body(): return lax.all_to_all(gated, 'ch', split_axis=0, concat_axis=1, tiled=True)  25.1 us
    dot_general x1, matrix products, on_device_body(): jnp.einsum('tf,ifc->itc', gathered, gathered_weight(proj_weight), preferr...  18.8 us
    all_to_all x1, blocking collectives, on_device_body(): lax.all_to_all(sent, 'ctx', split_axis=0, concat_axis=0, tiled=True)  13.1 us
    dynamic_update_slice x8, local copies, waits for them, and re-layouts, gathered_weight(): full = lax.dynamic_update_slice(full, part, (0, src * width, 0))  12.1 us
    ppermute x4, local copies, waits for them, and re-layouts, gathered_weight(): lax.ppermute(part, 'ctx', sibling)  7.79 us
    ppermute x3, local copies, waits for them, and re-layouts, gathered_weight(): held.append((lax.ppermute(block, 'ctx', pairs), (me - by) % count))  6.92 us
  transfers between devices with their start and end apart: 9, of which 4 were waited for; matrix products, arithmetic and copies ran while one was open for 15% of the time, Pallas kernels for 0%

profile of v8, /device:TPU:32, one launch (start us, length us, event | category | flops | bytes accessed | tf_op | source)
XLA Modules:
  0.0 234.8 jit_solution(15439329946707326712)
XLA Ops:
  6.5 1.4 fusion.14
  7.9 2.0 fusion.16
  10.0 1.6 collective-permute-start
  11.5 2.7 %collective-permute-start.1 = (bf16[3,1024,256]{2,1,0:T(8,128)(2,1)}, bf16[3,1024,256]{2,1,0:T(8,128)(2,1)}, u32[]{:S(2)}, u32[]{:S(2)}) collective-permute-start(bf16[3,1024,256]{2,1,0:T(8,128)(2,1)} %param.9), channel_id=1, source_target_pairs={{0,128},{32,160},{64,192},{96,224},{128,0},{160,32},{192,64},{224,... | collective-permute-start | bytes 4718600 | tf_op jit(solution)/shard_map/ppermute | solution.py:133
  14.3 1.4 collective-permute-start.2
  16.7 6.1 %broadcast_in_dim.14 = bf16[3,8192,256]{1,2,0:T(8,128)(2,1)} broadcast(bf16[]{:T(256)} %constant.43.clone.1), dimensions={} | broadcast | bytes 12582914 | tf_op jit(solution)/shard_map/broadcast_in_dim | solution.py:136
  24.1 23.8 %collective-permute-done = bf16[3,1024,256]{2,1,0:T(8,128)(2,1)} collective-permute-done((bf16[3,1024,256]{2,1,0:T(8,128)(2,1)}, bf16[3,1024,256]{2,1,0:T(8,128)(2,1)}, u32[]{:S(2)}, u32[]{:S(2)}) %collective-permute-start) | collective-permute-done | bytes 1572896 | tf_op jit(solution)/shard_map/ppermute | solution.py:133
  47.9 34.5 %collective-permute-done.1 = bf16[3,1024,256]{2,1,0:T(8,128)(2,1)} collective-permute-done((bf16[3,1024,256]{2,1,0:T(8,128)(2,1)}, bf16[3,1024,256]{2,1,0:T(8,128)(2,1)}, u32[]{:S(2)}, u32[]{:S(2)}) %collective-permute-start.1) | collective-permute-done | bytes 1572896 | tf_op jit(solution)/shard_map/ppermute | solution.py:133
  83.6 2.6 %copy.29 = bf16[3,1024,256]{1,2,0:T(8,128)(2,1)} copy(bf16[3,1024,256]{2,1,0:T(8,128)(2,1)} %collective-permute-done) | data formatting | bytes 3145728 | tf_op jit(solution)/shard_map/ppermute | solution.py:133
  86.2 2.6 %copy.30 = bf16[3,1024,256]{1,2,0:T(8,128)(2,1)} copy(bf16[3,1024,256]{2,1,0:T(8,128)(2,1)} %collective-permute-done.1) | data formatting | bytes 3145728 | tf_op jit(solution)/shard_map/ppermute | solution.py:133
  88.8 1.7 copy.31
  90.5 1.7 copy.32
  92.3 3.1 %constant_dynamic-update-slice_fusion.6 = bf16[3,8192,256]{1,2,0:T(8,128)(2,1)} fusion(bf16[3,8192,256]{1,2,0:T(8,128)(2,1)} %constant_dynamic-update-slice_fusion.7, bf16[3,1024,256]{1,2,0:T(8,128)(2,1)} %copy.29, s32[]{:T(128)S(6)} %select_n.45), kind=kLoop, calls=%fused_computation.52 | loop fusion | bytes 3145732 | tf_op jit(solution)/shard_map/dynamic_update_slice | solution.py:138
  99.2 1.7 copy.33
  100.9 1.7 copy.34
  102.7 2.6 %copy.35 = bf16[3,1024,256]{1,2,0:T(8,128)(2,1)} copy(bf16[3,1024,256]{2,1,0:T(8,128)(2,1)} %collective-permute-done.6) | data formatting | bytes 3145728 | tf_op jit(solution)/shard_map/ppermute | solution.py:135
  109.2 41.5 %all-gather.2.cloned.1.call-done = bf16[1024,8192]{1,0:T(8,128)(2,1)} async-done(((bf16[32,8192]{1,0:T(8,128)(2,1)}), bf16[1024,8192]{1,0:T(8,128)(2,1)}) %all-gather.2.cloned.1.call-update) | async-done | bytes 16777232 | tf_op jit(solution)/shard_map/all_gather | solution.py:146
  150.7 18.8 %fusion.11 = bf16[3,1024,256]{2,1,0:T(8,128)(2,1)S(1)} fusion(bf16[3,8192,256]{1,2,0:T(8,128)(2,1)} %constant_dynamic-update-slice_fusion, bf16[1024,8192]{1,0:T(8,128)(2,1)} %all-gather.2.cloned.1.call-done), kind=kOutput, calls=%fused_computation.17 | convolution fusion | flops 12885688320 | bytes 30932992 | tf_op jit(solution)/shard_map/tf,ifc->itc/dot_general | solution.py:149
  171.9 2.6 %fusion.2 = f32[3,1024,256]{2,1,0:T(8,128)S(1)} fusion(f32[3,1030,256]{2,1,0:T(8,128)S(1)} %maximum_convert_fusion, f32[3,256]{1,0:T(4,128)S(1)} %get-tuple-element.20, f32[3,256]{1,0:T(4,128)S(1)} %get-tuple-element.21, f32[3,256]{1,0:T(4,128)S(1)} %get-tuple-element.22, f32[3,256]{1,0:T(4,128)S(1)} %get-tuple-element.23, ...), kind=kLoop, calls=%fused_computation.3 | loop fusion | flops 10223616 | bytes 25187328 | tf_op jit(solution)/shard_map/add | solution.py:163
  174.5 1.5 slice_bitcast_fusion
  176.0 3.8 %shard_map.73 = f32[4,16,256]{2,1,0:T(8,128)} custom-call(f32[1024,256]{1,0:T(8,128)} %get-tuple-element.6.x_ref, f32[16,256]{1,0:T(8,128)} %get-tuple-element.18.r_ref, f32[16,256]{1,0:T(8,128)} %get-tuple-element.19.b_ref), custom_call_target="tpu_custom_call" | custom-call | tf_op jit(solution)/shard_map/pallas_call | solution.py:91
  180.7 13.1 %all_to_all.24 = f32[8,16,256]{2,1,0:T(8,128)S(1)} all-to-all(f32[8,16,256]{2,1,0:T(8,128)S(1)} %select_multiply_fusion), channel_id=1, replica_groups=mesh['ctx'=8,'ch'=32] {'ctx'}, dimensions={0} | all-to-all | bytes 262144 | tf_op jit(solution)/shard_map/all_to_all | solution.py:181
  195.2 6.9 %shard_map.74 = bf16[1024,256]{1,0:T(8,128)(2,1)} custom-call(f32[1024,256]{1,0:T(8,128)} %get-tuple-element.6.x_ref, f32[1024,256]{1,0:T(8,128)} %get-tuple-element.5.q_ref, f32[16,256]{1,0:T(8,128)} %get-tuple-element.18.r_ref, f32[16,256]{1,0:T(8,128)} %get-tuple-element.19.b_ref, f32[16,256]{1,0:T(8,128)} %res_ref.1, f32[1,256]{1,0:T(1,128)} %bitcast.79, ...), custom_call_target="tpu_custom_call" | custom-call | tf_op jit(solution)/shard_map/pallas_call | solution.py:109
  202.1 25.1 %all_to_all.25 = bf16[32,32,256]{2,1,0:T(8,128)(2,1)S(1)} all-to-all(bf16[32,32,256]{2,1,0:T(8,128)(2,1)} %bitcast.75), channel_id=1, replica_groups=mesh['ctx'=8,'ch'=32] {'ch'}, dimensions={0} | all-to-all | bytes 1048576 | tf_op jit(solution)/shard_map/all_to_all | solution.py:187
  (48 shorter events, 16.7 us)
Async XLA Ops:
  6.5 9.2 %copy-start.2 = (bf16[3,1024,256]{2,1,0:T(8,128)(2,1)S(1)}, bf16[3,1024,256]{2,1,0:T(8,128)(2,1)}, u32[]{:S(2)}) copy-start(bf16[3,1024,256]{2,1,0:T(8,128)(2,1)} %param.9) | copy-start | bytes 4718596
  6.5 144.1 %all-gather.2.cloned.1.call-start = ((), (), s32[]{:S(2)}) async-start(), calls=%async_computation.2 | async-start | bytes 17301504 | tf_op jit(solution)/shard_map/all_gather | solution.py:146
  10.0 37.9 %collective-permute-start = (bf16[3,1024,256]{2,1,0:T(8,128)(2,1)}, bf16[3,1024,256]{2,1,0:T(8,128)(2,1)}, u32[]{:S(2)}, u32[]{:S(2)}) collective-permute-start(bf16[3,1024,256]{2,1,0:T(8,128)(2,1)} %param.9), channel_id=1, source_target_pairs={{0,64},{32,96},{64,128},{96,160},{128,192},{160,224},{192,0},{224,... | collective-permute-start | bytes 4718600 | tf_op jit(solution)/shard_map/ppermute | solution.py:133
  11.5 70.9 %collective-permute-start.1 = (bf16[3,1024,256]{2,1,0:T(8,128)(2,1)}, bf16[3,1024,256]{2,1,0:T(8,128)(2,1)}, u32[]{:S(2)}, u32[]{:S(2)}) collective-permute-start(bf16[3,1024,256]{2,1,0:T(8,128)(2,1)} %param.9), channel_id=1, source_target_pairs={{0,128},{32,160},{64,192},{96,224},{128,0},{160,32},{192,64},{224,... | collective-permute-start | bytes 4718600 | tf_op jit(solution)/shard_map/ppermute | solution.py:133
  14.3 68.1 %collective-permute-start.2 = (bf16[3,1024,256]{2,1,0:T(8,128)(2,1)}, bf16[3,1024,256]{2,1,0:T(8,128)(2,1)}, u32[]{:S(2)}, u32[]{:S(2)}) collective-permute-start(bf16[3,1024,256]{2,1,0:T(8,128)(2,1)} %param.9), channel_id=1, source_target_pairs={{0,192},{32,224},{64,0},{96,32},{128,64},{160,96},{192,128},{224,1... | collective-permute-start | bytes 4718600 | tf_op jit(solution)/shard_map/ppermute | solution.py:133
  15.7 74.8 %collective-permute-start.3 = (bf16[3,1024,256]{2,1,0:T(8,128)(2,1)}, bf16[3,1024,256]{2,1,0:T(8,128)(2,1)}, u32[]{:S(2)}, u32[]{:S(2)}) collective-permute-start(bf16[3,1024,256]{2,1,0:T(8,128)(2,1)} %param.9), channel_id=1, source_target_pairs={{0,32},{32,0},{64,96},{96,64},{128,160},{160,128},{192,224},{224,1... | collective-permute-start | bytes 4718600 | tf_op jit(solution)/shard_map/ppermute | solution.py:135
  22.7 1.3 copy-start.4
  22.7 60.2 %copy-start.3 = (f32[16,256]{1,0:T(8,128)S(1)}, f32[16,256]{1,0:T(8,128)}, u32[]{:S(2)}) copy-start(f32[16,256]{1,0:T(8,128)} %param.11) | copy-start | bytes 49156
  47.9 51.3 %collective-permute-start.4 = (bf16[3,1024,256]{2,1,0:T(8,128)(2,1)}, bf16[3,1024,256]{2,1,0:T(8,128)(2,1)}, u32[]{:S(2)}, u32[]{:S(2)}) collective-permute-start(bf16[3,1024,256]{2,1,0:T(8,128)(2,1)} %collective-permute-done), channel_id=1, source_target_pairs={{0,32},{32,0},{64,96},{96,64},{128,160},{160,128},{192,224},{224,1... | collective-permute-start | bytes 4718600 | tf_op jit(solution)/shard_map/ppermute | solution.py:135
  82.4 18.5 %collective-permute-start.5 = (bf16[3,1024,256]{2,1,0:T(8,128)(2,1)}, bf16[3,1024,256]{2,1,0:T(8,128)(2,1)}, u32[]{:S(2)}, u32[]{:S(2)}) collective-permute-start(bf16[3,1024,256]{2,1,0:T(8,128)(2,1)} %collective-permute-done.1), channel_id=1, source_target_pairs={{0,32},{32,0},{64,96},{96,64},{128,160},{160,128},{192,224},{224,1... | collective-permute-start | bytes 4718600 | tf_op jit(solution)/shard_map/ppermute | solution.py:135
  82.4 20.3 %collective-permute-start.6 = (bf16[3,1024,256]{2,1,0:T(8,128)(2,1)}, bf16[3,1024,256]{2,1,0:T(8,128)(2,1)}, u32[]{:S(2)}, u32[]{:S(2)}) collective-permute-start(bf16[3,1024,256]{2,1,0:T(8,128)(2,1)} %collective-permute-done.2), channel_id=1, source_target_pairs={{0,32},{32,0},{64,96},{96,64},{128,160},{160,128},{192,224},{224,1... | collective-permute-start | bytes 4718600 | tf_op jit(solution)/shard_map/ppermute | solution.py:135
  92.3 3.1 %copy-start = (bf16[3,1024,256]{1,2,0:T(8,128)(2,1)S(1)}, bf16[3,1024,256]{1,2,0:T(8,128)(2,1)}, u32[]{:S(2)}) copy-start(bf16[3,1024,256]{1,2,0:T(8,128)(2,1)} %copy.30) | copy-start | bytes 4718596
  105.3 2.6 %copy-start.1 = (bf16[3,1024,256]{1,2,0:T(8,128)(2,1)S(1)}, bf16[3,1024,256]{1,2,0:T(8,128)(2,1)}, u32[]{:S(2)}) copy-start(bf16[3,1024,256]{1,2,0:T(8,128)(2,1)} %copy.35) | copy-start | bytes 4718596
  169.5 2.1 collective-permute-start.7
Sparse Core Ops, SparseCore 0:
  10.1 140.5 all-gather.1

commit v9 on v7

--- a/solution.py
+++ b/solution.py
@@ -128,27 +128,29 @@
     normed = (widened * lax.rsqrt(mean_square + norm_eps) * norm_gain[None, :]).astype(jnp.bfloat16)
     gathered = lax.all_gather(normed, "ch", axis=0, tiled=True)
     row_count = gathered.shape[0]
-    chan_count = proj_weight.shape[2]
-    summed = jnp.einsum(
-        "tf,ifc->itc",
-        gathered,
-        gathered_weight(proj_weight),
-        preferred_element_type=jnp.float32,
-    )
-    projected = summed.astype(jnp.bfloat16)
-    tap_count = conv_weight.shape[1]
-    reach = tap_count - 1
-    rim_rows = shifted(projected[:, row_count - reach :, :], "ctx", 1)
-    padded = jnp.concatenate([rim_rows, projected], axis=1).astype(jnp.float32)
-    featured = jnp.zeros((3, row_count, chan_count), jnp.float32)
-    for shift_idx in range(tap_count):
-        featured = (
-            featured
-            + conv_weight[:, shift_idx, None, :]
-            * padded[:, reach - shift_idx : reach - shift_idx + row_count, :]
+    weight = gathered_weight(proj_weight)
+
+    def featured_of(part):
+        summed = jnp.einsum(
+            "tf,ifc->itc", gathered, weight[part], preferred_element_type=jnp.float32
         )
-    queries = featured[0]
-    mixed = featured[1] * featured[2]
+        projected = summed.astype(jnp.bfloat16)
+        tap_count = conv_weight.shape[1]
+        reach = tap_count - 1
+        rim_rows = shifted(projected[:, row_count - reach :, :], "ctx", 1)
+        padded = jnp.concatenate([rim_rows, projected], axis=1).astype(jnp.float32)
+        taps = conv_weight[part]
+        featured = jnp.zeros(projected.shape, jnp.float32)
+        for shift_idx in range(tap_count):
+            featured = (
+                featured
+                + taps[:, shift_idx, None, :]
+                * padded[:, reach - shift_idx : reach - shift_idx + row_count, :]
+            )
+        return featured
+
+    keys_values = featured_of(slice(1, 3))
+    mixed = keys_values[0] * keys_values[1]
     retention = jnp.exp(-decay_rate)
     in_scale = jnp.sqrt(-jnp.expm1(-2.0 * decay_rate))
     local_end = modal_ends(mixed, retention, in_scale)
@@ -159,6 +161,7 @@
     sent = sent * local_end[None]
     received = lax.all_to_all(sent, "ctx", split_axis=0, concat_axis=0, tiled=True)
     incoming = jnp.sum(received, axis=0)
+    queries = featured_of(slice(0, 1))[0]
     gated = modal_gate(mixed, queries, retention, in_scale, residue, skip_gain, incoming)
     return lax.all_to_all(gated, "ch", split_axis=0, concat_axis=1, tiled=True)
 

time: 235 us -> 242 us (1.030)
  waiting for transfers between devices: 101 us -> 115 us
  blocking collectives: 38.1 us -> 25.1 us
  local copies, waits for them, and re-layouts: 34.6 us -> 24 us
  starting transfers between devices: 7.54 us -> 16.7 us
  matrix products: 18.8 us -> 24.3 us
    ppermute x7 -> x0, local copies, waits for them, and re-layouts: 14.7 us -> none  [the longest x4 7.79 us: gathered_weight(): lax.ppermute(part, 'ctx', sibling)]
    all_to_all x1 -> x0, blocking collectives: 13.1 us -> none  [on_device_body(): lax.all_to_all(sent, 'ctx', split_axis=0, concat_axis=0, tiled=True)]
    ppermute x3, waiting for transfers between devices: 58.4 us -> 66.3 us  [gathered_weight(): held.append((lax.ppermute(block, 'ctx', pairs), (me - by) % count))]
    dot_general x1 -> x2, matrix products: 18.8 us -> 24.3 us  [featured_of(): jnp.einsum('tf,ifc->itc', gathered, weight[part], preferred_element_type=...]
    all_to_all x0 -> x1, starting transfers between devices: none -> 4.94 us  [on_device_body(): lax.all_to_all(sent, 'ctx', split_axis=0, concat_axis=0, tiled=True)]
    ppermute x1 -> x2, starting transfers between devices: 1.29 us -> 5.57 us  [shifted(): return lax.ppermute(shard, axis, pairs)]
    all_to_all x0 -> x1, waiting for transfers between devices: none -> 4.25 us  [on_device_body(): lax.all_to_all(sent, 'ctx', split_axis=0, concat_axis=0, tiled=True)]
    dynamic_update_slice x8, local copies, waits for them, and re-layouts: 12.1 us -> 16.1 us  [gathered_weight(): full = lax.dynamic_update_slice(full, part, (0, src * width, 0))]
  transfers between devices with their start and end apart: 9 -> 11, of which waited for: 4 -> 5; matrix products, arithmetic and copies ran while one was open for 15% -> 16% of each run, Pallas kernels for 0% -> 0%
where the time goes in v9:
time: 242 us
  waiting for transfers between devices  115 us (48%)
  blocking collectives  25.1 us (10%)
  matrix products  24.3 us (10%)
  local copies, waits for them, and re-layouts  24 us (10%)
  starting transfers between devices  16.7 us (7%)
  between operations  13.7 us (6%)
  Pallas kernels  11.6 us (5%)
  other arithmetic  11.1 us (5%)
    ppermute x3, waiting for transfers between devices, gathered_weight(): held.append((lax.ppermute(block, 'ctx', pairs), (me - by) % count))  66.3 us
    all_gather x1, waiting for transfers between devices, on_device_body(): gathered = lax.all_gather(normed, 'ch', axis=0, tiled=True)  44.2 us
    all_to_all x1, blocking collectives, on_device_body(): return lax.all_to_all(gated, 'ch', split_axis=0, concat_axis=1, tiled=True)  25.1 us
    dot_general x2, matrix products, featured_of(): jnp.einsum('tf,ifc->itc', gathered, weight[part], preferred_element_type=...  24.3 us
    dynamic_update_slice x8, local copies, waits for them, and re-layouts, gathered_weight(): full = lax.dynamic_update_slice(full, part, (0, src * width, 0))  16.1 us
    pallas_call x1, Pallas kernels, modal_gate(): pl.pallas_call(gate_kernel, grid=(chans // lanes,), in_specs=[pl.BlockSpe...  7.35 us
    broadcast_in_dim x1, local copies, waits for them, and re-layouts, gathered_weight(): jnp.zeros((block.shape[0], count * width, block.shape[2]), block.dtype)  6.08 us
    ppermute x3, starting transfers between devices, gathered_weight(): held.append((lax.ppermute(block, 'ctx', pairs), (me - by) % count))  5.73 us
  transfers between devices with their start and end apart: 11, of which 5 were waited for; matrix products, arithmetic and copies ran while one was open for 16% of the time, Pallas kernels for 0%

profile of v9, /device:TPU:32, one launch (start us, length us, event | category | flops | bytes accessed | tf_op | source)
XLA Modules:
  0.0 241.8 jit_solution(17320921823797229109)
XLA Ops:
  7.9 2.0 fusion.19
  10.9 1.6 collective-permute-start
  12.4 2.7 %collective-permute-start.1 = (bf16[3,1024,256]{1,2,0:T(8,128)(2,1)S(1)}, bf16[3,1024,256]{1,2,0:T(8,128)(2,1)}, u32[]{:S(2)}, u32[]{:S(2)}) collective-permute-start(bf16[3,1024,256]{1,2,0:T(8,128)(2,1)S(1)} %copy.24), channel_id=1, source_target_pairs={{0,128},{32,160},{64,192},{96,224},{128,0},{160,32},{192,64},{224,... | collective-permute-start | bytes 4718600 | tf_op jit(solution)/shard_map/ppermute | solution.py:116
  15.2 1.4 collective-permute-start.2
  16.6 31.9 %collective-permute-done = bf16[3,1024,256]{1,2,0:T(8,128)(2,1)} collective-permute-done((bf16[3,1024,256]{1,2,0:T(8,128)(2,1)S(1)}, bf16[3,1024,256]{1,2,0:T(8,128)(2,1)}, u32[]{:S(2)}, u32[]{:S(2)}) %collective-permute-start) | collective-permute-done | bytes 1572896 | tf_op jit(solution)/shard_map/ppermute | solution.py:116
  48.7 34.4 %collective-permute-done.1 = bf16[3,1024,256]{1,2,0:T(8,128)(2,1)} collective-permute-done((bf16[3,1024,256]{1,2,0:T(8,128)(2,1)S(1)}, bf16[3,1024,256]{1,2,0:T(8,128)(2,1)}, u32[]{:S(2)}, u32[]{:S(2)}) %collective-permute-start.1) | collective-permute-done | bytes 1572896 | tf_op jit(solution)/shard_map/ppermute | solution.py:116
  83.1 6.1 %broadcast_in_dim.14 = bf16[3,8192,256]{1,2,0:T(8,128)(2,1)} broadcast(bf16[]{:T(256)} %constant.42.clone.1), dimensions={} | broadcast | bytes 12582914 | tf_op jit(solution)/shard_map/broadcast_in_dim | solution.py:119
  91.6 2.7 %constant_dynamic-update-slice_fusion.6 = bf16[3,8192,256]{1,2,0:T(8,128)(2,1)} fusion(bf16[3,8192,256]{1,2,0:T(8,128)(2,1)} %constant_dynamic-update-slice_fusion.7, bf16[3,1024,256]{1,2,0:T(8,128)(2,1)} %collective-permute-done, s32[]{:T(128)S(6)} %select_n.45), kind=kLoop, calls=%fused_computation.59 | loop fusion | bytes 3145732 | tf_op jit(solution)/shard_map/dynamic_update_slice | solution.py:121
  94.3 2.7 %constant_dynamic-update-slice_fusion.5 = bf16[3,8192,256]{1,2,0:T(8,128)(2,1)} fusion(bf16[3,8192,256]{1,2,0:T(8,128)(2,1)} %constant_dynamic-update-slice_fusion.6, bf16[3,1024,256]{1,2,0:T(8,128)(2,1)} %collective-permute-done.1, s32[]{:T(128)S(6)} %select_n.47), kind=kLoop, calls=%fused_computation.58 | loop fusion | bytes 3145732 | tf_op jit(solution)/shard_map/dynamic_update_slice | solution.py:121
  98.4 2.7 %constant_dynamic-update-slice_fusion.3 = bf16[3,8192,256]{1,2,0:T(8,128)(2,1)} fusion(bf16[3,8192,256]{1,2,0:T(8,128)(2,1)} %constant_dynamic-update-slice_fusion.4, bf16[3,1024,256]{1,2,0:T(8,128)(2,1)} %collective-permute-done.3, s32[]{:T(128)S(6)} %select_n.50), kind=kLoop, calls=%fused_computation.56 | loop fusion | bytes 3145732 | tf_op jit(solution)/shard_map/dynamic_update_slice | solution.py:121
  101.1 2.7 %constant_dynamic-update-slice_fusion.2 = bf16[3,8192,256]{1,2,0:T(8,128)(2,1)} fusion(bf16[3,8192,256]{1,2,0:T(8,128)(2,1)} %constant_dynamic-update-slice_fusion.3, bf16[3,1024,256]{1,2,0:T(8,128)(2,1)} %collective-permute-done.4, s32[]{:T(128)S(6)} %select_n.51), kind=kLoop, calls=%fused_computation.55 | loop fusion | bytes 3145732 | tf_op jit(solution)/shard_map/dynamic_update_slice | solution.py:121
  106.5 44.2 %all-gather.2.cloned.1.call-done = bf16[1024,8192]{1,0:T(8,128)(2,1)} async-done(((bf16[32,8192]{1,0:T(8,128)(2,1)}), bf16[1024,8192]{1,0:T(8,128)(2,1)}) %all-gather.2.cloned.1.call-update) | async-done | bytes 16777232 | tf_op jit(solution)/shard_map/all_gather | solution.py:129
  150.7 11.7 %fusion.16 = bf16[1,1024,256]{2,1,0:T(8,128)(2,1)S(1)} fusion(bf16[1024,8192]{1,0:T(8,128)(2,1)} %all-gather.2.cloned.1.call-done, bf16[3,8192,256]{1,2,0:T(8,128)(2,1)} %constant_dynamic-update-slice_fusion), kind=kOutput, calls=%fused_computation.22 | convolution fusion | flops 4295229440 | bytes 21495808 | tf_op jit(solution)/shard_map/tf,ifc->itc/dot_general | solution.py:134
  162.4 1.5 collective-permute-start.8
  163.9 12.6 %fusion.12 = bf16[2,1024,256]{2,1,0:T(8,128)(2,1)S(1)} fusion(bf16[3,8192,256]{1,2,0:T(8,128)(2,1)S(1)} %copy-done, bf16[1024,8192]{1,0:T(8,128)(2,1)} %all-gather.2.cloned.1.call-done), kind=kOutput, calls=%fused_computation.18 | convolution fusion | flops 8590458880 | bytes 30408704 | tf_op jit(solution)/shard_map/tf,ifc->itc/dot_general | solution.py:134
  176.5 4.1 %collective-permute-start.7 = (bf16[2,6,256]{2,1,0:T(8,128)(2,1)S(1)}, bf16[2,6,256]{2,1,0:T(8,128)(2,1)S(1)}, u32[]{:S(2)}, u32[]{:S(2)}) collective-permute-start(bf16[2,6,256]{2,1,0:T(8,128)(2,1)S(1)} %slice.152), channel_id=1, source_target_pairs={{0,32},{32,64},{64,96},{96,128},{128,160},{160,192},{192,224},{1,3... | collective-permute-start | bytes 18440 | tf_op jit(solution)/shard_map/ppermute | solution.py:13
  181.6 1.7 fusion.3
  184.4 4.2 %shard_map.73 = f32[16,256]{1,0:T(8,128)} custom-call(f32[1024,256]{1,0:T(8,128)} %fusion.27.x_ref, f32[16,256]{1,0:T(8,128)} %get-tuple-element.20.r_ref, f32[16,256]{1,0:T(8,128)} %get-tuple-element.21.b_ref), custom_call_target="tpu_custom_call" | custom-call | tf_op jit(solution)/shard_map/pallas_call | solution.py:74
  188.6 1.5 select_multiply_fusion
  190.1 4.9 %all-to-all-start = ((f32[8,16,256]{2,1,0:T(8,128)}), f32[8,16,256]{2,1,0:T(8,128)S(1)}, u32[]{:S(2)}, u32[]{:S(2)}) async-start(f32[8,16,256]{2,1,0:T(8,128)} %select_multiply_fusion), calls=%async_computation | async-start | bytes 262144 | tf_op jit(solution)/shard_map/all_to_all | solution.py:162
  195.0 1.8 fusion.21.q_ref
  196.9 4.3 %all-to-all-done = f32[8,16,256]{2,1,0:T(8,128)S(1)} async-done(((f32[8,16,256]{2,1,0:T(8,128)}), f32[8,16,256]{2,1,0:T(8,128)S(1)}, u32[]{:S(2)}, u32[]{:S(2)}) %all-to-all-start) | async-done | bytes 131104 | tf_op jit(solution)/shard_map/all_to_all | solution.py:162
  201.7 7.4 %shard_map.74 = bf16[1024,256]{1,0:T(8,128)(2,1)} custom-call(f32[1024,256]{1,0:T(8,128)} %fusion.27.x_ref, f32[1024,256]{1,0:T(8,128)} %fusion.21.q_ref, f32[16,256]{1,0:T(8,128)} %get-tuple-element.20.r_ref, f32[16,256]{1,0:T(8,128)} %get-tuple-element.21.b_ref, f32[16,256]{1,0:T(8,128)} %res_ref.1, f32[1,256]{1,0:T(1,128)} %bitcast.63, ...), custom_call_target="tpu_custom_call" | custom-call | tf_op jit(solution)/shard_map/pallas_call | solution.py:92
  209.1 25.1 %all_to_all.24 = bf16[32,32,256]{2,1,0:T(8,128)(2,1)S(1)} all-to-all(bf16[32,32,256]{2,1,0:T(8,128)(2,1)} %bitcast.53), channel_id=1, replica_groups=mesh['ctx'=8,'ch'=32] {'ch'}, dimensions={0} | all-to-all | bytes 1048576 | tf_op jit(solution)/shard_map/all_to_all | solution.py:166
  (44 shorter events, 12.2 us)
Async XLA Ops:
  6.5 3.4 %copy-start.1 = (bf16[3,1024,256]{2,1,0:T(8,128)(2,1)S(1)}, bf16[3,1024,256]{2,1,0:T(8,128)(2,1)}, u32[]{:S(2)}) copy-start(bf16[3,1024,256]{2,1,0:T(8,128)(2,1)} %param.9) | copy-start | bytes 4718596
  6.5 144.1 %all-gather.2.cloned.1.call-start = ((), (), s32[]{:S(2)}) async-start(), calls=%async_computation.2 | async-start | bytes 17301504 | tf_op jit(solution)/shard_map/all_gather | solution.py:129
  10.0 6.7 %copy-start.2 = (f32[3,7,256]{2,1,0:T(8,128)S(1)}, f32[3,7,256]{2,1,0:T(8,128)}, u32[]{:S(2)}) copy-start(f32[3,7,256]{2,1,0:T(8,128)} %param.10) | copy-start | bytes 64516
  10.9 37.7 %collective-permute-start = (bf16[3,1024,256]{1,2,0:T(8,128)(2,1)S(1)}, bf16[3,1024,256]{1,2,0:T(8,128)(2,1)}, u32[]{:S(2)}, u32[]{:S(2)}) collective-permute-start(bf16[3,1024,256]{1,2,0:T(8,128)(2,1)S(1)} %copy.24), channel_id=1, source_target_pairs={{0,64},{32,96},{64,128},{96,160},{128,192},{160,224},{192,0},{224,... | collective-permute-start | bytes 4718600 | tf_op jit(solution)/shard_map/ppermute | solution.py:116
  12.4 70.6 %collective-permute-start.1 = (bf16[3,1024,256]{1,2,0:T(8,128)(2,1)S(1)}, bf16[3,1024,256]{1,2,0:T(8,128)(2,1)}, u32[]{:S(2)}, u32[]{:S(2)}) collective-permute-start(bf16[3,1024,256]{1,2,0:T(8,128)(2,1)S(1)} %copy.24), channel_id=1, source_target_pairs={{0,128},{32,160},{64,192},{96,224},{128,0},{160,32},{192,64},{224,... | collective-permute-start | bytes 4718600 | tf_op jit(solution)/shard_map/ppermute | solution.py:116
  15.2 75.3 %collective-permute-start.2 = (bf16[3,1024,256]{1,2,0:T(8,128)(2,1)S(1)}, bf16[3,1024,256]{1,2,0:T(8,128)(2,1)S(1)}, u32[]{:S(2)}, u32[]{:S(2)}) collective-permute-start(bf16[3,1024,256]{1,2,0:T(8,128)(2,1)S(1)} %copy.24), channel_id=1, source_target_pairs={{0,192},{32,224},{64,0},{96,32},{128,64},{160,96},{192,128},{224,1... | collective-permute-start | bytes 4718600 | tf_op jit(solution)/shard_map/ppermute | solution.py:116
  16.6 81.8 %collective-permute-start.3 = (bf16[3,1024,256]{1,2,0:T(8,128)(2,1)S(1)}, bf16[3,1024,256]{1,2,0:T(8,128)(2,1)}, u32[]{:S(2)}, u32[]{:S(2)}) collective-permute-start(bf16[3,1024,256]{1,2,0:T(8,128)(2,1)S(1)} %copy.24), channel_id=1, source_target_pairs={{0,32},{32,0},{64,96},{96,64},{128,160},{160,128},{192,224},{224,1... | collective-permute-start | bytes 4718600 | tf_op jit(solution)/shard_map/ppermute | solution.py:118
  48.5 52.6 %collective-permute-start.4 = (bf16[3,1024,256]{1,2,0:T(8,128)(2,1)}, bf16[3,1024,256]{1,2,0:T(8,128)(2,1)}, u32[]{:S(2)}, u32[]{:S(2)}) collective-permute-start(bf16[3,1024,256]{1,2,0:T(8,128)(2,1)} %collective-permute-done), channel_id=1, source_target_pairs={{0,32},{32,0},{64,96},{96,64},{128,160},{160,128},{192,224},{224,1... | collective-permute-start | bytes 4718600 | tf_op jit(solution)/shard_map/ppermute | solution.py:118
  83.1 20.8 %collective-permute-start.5 = (bf16[3,1024,256]{1,2,0:T(8,128)(2,1)}, bf16[3,1024,256]{1,2,0:T(8,128)(2,1)S(1)}, u32[]{:S(2)}, u32[]{:S(2)}) collective-permute-start(bf16[3,1024,256]{1,2,0:T(8,128)(2,1)} %collective-permute-done.1), channel_id=1, source_target_pairs={{0,32},{32,0},{64,96},{96,64},{128,160},{160,128},{192,224},{224,1... | collective-permute-start | bytes 4718600 | tf_op jit(solution)/shard_map/ppermute | solution.py:118
  89.2 1.8 copy-start.3
  90.5 14.7 %collective-permute-start.6 = (bf16[3,1024,256]{1,2,0:T(8,128)(2,1)S(1)}, bf16[3,1024,256]{1,2,0:T(8,128)(2,1)S(1)}, u32[]{:S(2)}, u32[]{:S(2)}) collective-permute-start(bf16[3,1024,256]{1,2,0:T(8,128)(2,1)S(1)} %collective-permute-done.2), channel_id=1, source_target_pairs={{0,32},{32,0},{64,96},{96,64},{128,160},{160,128},{192,224},{224,1... | collective-permute-start | bytes 4718600 | tf_op jit(solution)/shard_map/ppermute | solution.py:118
  150.7 13.2 %copy-start = (bf16[3,8192,256]{1,2,0:T(8,128)(2,1)S(1)}, bf16[3,8192,256]{1,2,0:T(8,128)(2,1)}, u32[]{:S(2)}) copy-start(bf16[3,8192,256]{1,2,0:T(8,128)(2,1)} %constant_dynamic-update-slice_fusion) | copy-start | bytes 37748740
  162.4 18.2 %collective-permute-start.8 = (bf16[1,6,256]{2,1,0:T(8,128)(2,1)S(1)}, bf16[1,6,256]{2,1,0:T(8,128)(2,1)S(1)}, u32[]{:S(2)}, u32[]{:S(2)}) collective-permute-start(bf16[1,6,256]{2,1,0:T(8,128)(2,1)S(1)} %slice.163), channel_id=1, source_target_pairs={{0,32},{32,64},{64,96},{96,128},{128,160},{160,192},{192,224},{1,3... | collective-permute-start | bytes 9224 | tf_op jit(solution)/shard_map/ppermute | solution.py:13
  176.5 4.9 %collective-permute-start.7 = (bf16[2,6,256]{2,1,0:T(8,128)(2,1)S(1)}, bf16[2,6,256]{2,1,0:T(8,128)(2,1)S(1)}, u32[]{:S(2)}, u32[]{:S(2)}) collective-permute-start(bf16[2,6,256]{2,1,0:T(8,128)(2,1)S(1)} %slice.152), channel_id=1, source_target_pairs={{0,32},{32,64},{64,96},{96,128},{128,160},{160,192},{192,224},{1,3... | collective-permute-start | bytes 18440 | tf_op jit(solution)/shard_map/ppermute | solution.py:13
  190.1 11.0 %all-to-all-start = ((f32[8,16,256]{2,1,0:T(8,128)}), f32[8,16,256]{2,1,0:T(8,128)S(1)}, u32[]{:S(2)}, u32[]{:S(2)}) async-start(f32[8,16,256]{2,1,0:T(8,128)} %select_multiply_fusion), calls=%async_computation | async-start | bytes 262144 | tf_op jit(solution)/shard_map/all_to_all | solution.py:162
Sparse Core Ops, SparseCore 0:
  10.1 140.5 all-gather.1

commit v10 on v7

--- a/solution.py
+++ b/solution.py
@@ -106,6 +106,26 @@
     )(x, queries, retention, in_scale, residue, skip_gain.reshape(1, chans), incoming)
 
 
+def norm_kernel(x_ref, gain_ref, out_ref):
+    widened = x_ref[...].astype(jnp.float32)
+    mean_square = jnp.mean(widened * widened, axis=-1, keepdims=True)
+    out_ref[...] = (widened * lax.rsqrt(mean_square + norm_eps) * gain_ref[...]).astype(out_ref.dtype)
+
+
+def rms_norm(tokens, gain):
+    rows, width = tokens.shape
+    return pl.pallas_call(
+        norm_kernel,
+        grid=(1,),
+        in_specs=[
+            pl.BlockSpec((rows, width), lambda i: (0, 0)),
+            pl.BlockSpec((1, width), lambda i: (0, 0)),
+        ],
+        out_specs=pl.BlockSpec((rows, width), lambda i: (0, 0)),
+        out_shape=jax.ShapeDtypeStruct((rows, width), jnp.bfloat16),
+    )(tokens, gain.reshape(1, width))
+
+
 def gathered_weight(block):
     count = lax.axis_size("ctx")
     me = lax.axis_index("ctx")
@@ -123,9 +143,7 @@
 
 
 def on_device_body(tokens_in, norm_gain, proj_weight, conv_weight, decay_rate, residue, skip_gain):
-    widened = tokens_in.astype(jnp.float32)
-    mean_square = jnp.mean(widened * widened, axis=-1, keepdims=True)
-    normed = (widened * lax.rsqrt(mean_square + norm_eps) * norm_gain[None, :]).astype(jnp.bfloat16)
+    normed = rms_norm(tokens_in, norm_gain)
     gathered = lax.all_gather(normed, "ch", axis=0, tiled=True)
     row_count = gathered.shape[0]
     chan_count = proj_weight.shape[2]

time: 235 us -> 235 us (level)
  other arithmetic: 9.9 us -> 6.5 us
where the time goes in v10:
time: 235 us
  waiting for transfers between devices  101 us (43%)
  blocking collectives  38.1 us (16%)
  local copies, waits for them, and re-layouts  35.4 us (15%)
  matrix products  18.8 us (8%)
  Pallas kernels  13.7 us (6%)
  between operations  13.6 us (6%)
  starting transfers between devices  7.54 us (3%)
  other arithmetic  6.5 us (3%)
    ppermute x3, waiting for transfers between devices, gathered_weight(): held.append((lax.ppermute(block, 'ctx', pairs), (me - by) % count))  57.5 us
    all_gather x1, waiting for transfers between devices, on_device_body(): gathered = lax.all_gather(normed, 'ch', axis=0, tiled=True)  42.7 us
    all_to_all x1, blocking collectives, on_device_body(): return lax.all_to_all(gated, 'ch', split_axis=0, concat_axis=1, tiled=True)  25.1 us
    dot_general x1, matrix products, on_device_body(): jnp.einsum('tf,ifc->itc', gathered, gathered_weight(proj_weight), preferr...  18.8 us
    all_to_all x1, blocking collectives, on_device_body(): lax.all_to_all(sent, 'ctx', split_axis=0, concat_axis=0, tiled=True)  13.1 us
    dynamic_update_slice x8, local copies, waits for them, and re-layouts, gathered_weight(): full = lax.dynamic_update_slice(full, part, (0, src * width, 0))  11.9 us
    ppermute x4, local copies, waits for them, and re-layouts, gathered_weight(): lax.ppermute(part, 'ctx', sibling)  7.81 us
    pallas_call x1, Pallas kernels, modal_gate(): pl.pallas_call(gate_kernel, grid=(chans // lanes,), in_specs=[pl.BlockSpe...  7.35 us
  transfers between devices with their start and end apart: 9, of which 4 were waited for; matrix products, arithmetic and copies ran while one was open for 15% of the time, Pallas kernels for 0%

profile of v10, /device:TPU:32, one launch (start us, length us, event | category | flops | bytes accessed | tf_op | source)
XLA Modules:
  0.0 234.7 jit_solution(9764930689197437338)
XLA Ops:
  6.5 2.2 shard_map.73
  8.7 1.6 collective-permute-start
  10.3 2.7 %collective-permute-start.1 = (bf16[3,1024,256]{2,1,0:T(8,128)(2,1)}, bf16[3,1024,256]{2,1,0:T(8,128)(2,1)}, u32[]{:S(2)}, u32[]{:S(2)}) collective-permute-start(bf16[3,1024,256]{2,1,0:T(8,128)(2,1)} %param.9), channel_id=1, source_target_pairs={{0,128},{32,160},{64,192},{96,224},{128,0},{160,32},{192,64},{224,... | collective-permute-start | bytes 4718600 | tf_op jit(solution)/shard_map/ppermute | solution.py:136
  13.0 1.4 collective-permute-start.2
  14.5 1.7 copy.28
  16.3 6.1 %broadcast_in_dim.19 = bf16[3,8192,256]{1,2,0:T(8,128)(2,1)} broadcast(bf16[]{:T(256)} %constant.39.clone.1), dimensions={} | broadcast | bytes 12582914 | tf_op jit(solution)/shard_map/broadcast_in_dim | solution.py:139
  23.7 22.9 %collective-permute-done = bf16[3,1024,256]{2,1,0:T(8,128)(2,1)} collective-permute-done((bf16[3,1024,256]{2,1,0:T(8,128)(2,1)}, bf16[3,1024,256]{2,1,0:T(8,128)(2,1)}, u32[]{:S(2)}, u32[]{:S(2)}) %collective-permute-start) | collective-permute-done | bytes 1572896 | tf_op jit(solution)/shard_map/ppermute | solution.py:136
  46.6 34.5 %collective-permute-done.1 = bf16[3,1024,256]{2,1,0:T(8,128)(2,1)} collective-permute-done((bf16[3,1024,256]{2,1,0:T(8,128)(2,1)}, bf16[3,1024,256]{2,1,0:T(8,128)(2,1)}, u32[]{:S(2)}, u32[]{:S(2)}) %collective-permute-start.1) | collective-permute-done | bytes 1572896 | tf_op jit(solution)/shard_map/ppermute | solution.py:136
  82.3 2.6 %copy.29 = bf16[3,1024,256]{1,2,0:T(8,128)(2,1)} copy(bf16[3,1024,256]{2,1,0:T(8,128)(2,1)} %collective-permute-done) | data formatting | bytes 3145728 | tf_op jit(solution)/shard_map/ppermute | solution.py:136
  85.0 2.6 %copy.30 = bf16[3,1024,256]{1,2,0:T(8,128)(2,1)} copy(bf16[3,1024,256]{2,1,0:T(8,128)(2,1)} %collective-permute-done.1) | data formatting | bytes 3145728 | tf_op jit(solution)/shard_map/ppermute | solution.py:136
  87.6 1.7 copy.31
  89.3 1.7 copy.32
  91.0 2.8 %constant_dynamic-update-slice_fusion.6 = bf16[3,8192,256]{1,2,0:T(8,128)(2,1)} fusion(bf16[3,8192,256]{1,2,0:T(8,128)(2,1)} %constant_dynamic-update-slice_fusion.7, bf16[3,1024,256]{1,2,0:T(8,128)(2,1)} %copy.29, s32[]{:T(128)S(6)} %select_n.45), kind=kLoop, calls=%fused_computation.36 | loop fusion | bytes 3145732 | tf_op jit(solution)/shard_map/dynamic_update_slice | solution.py:141
  97.7 1.7 copy.33
  99.5 1.7 copy.34
  101.2 2.6 %copy.35 = bf16[3,1024,256]{1,2,0:T(8,128)(2,1)} copy(bf16[3,1024,256]{2,1,0:T(8,128)(2,1)} %collective-permute-done.6) | data formatting | bytes 3145728 | tf_op jit(solution)/shard_map/ppermute | solution.py:138
  107.8 42.7 %all-gather.2.cloned.1.call-done = bf16[1024,8192]{1,0:T(8,128)(2,1)} async-done(((bf16[32,8192]{1,0:T(8,128)(2,1)}), bf16[1024,8192]{1,0:T(8,128)(2,1)}) %all-gather.2.cloned.1.call-update) | async-done | bytes 16777232 | tf_op jit(solution)/shard_map/all_gather | solution.py:147
  150.5 18.8 %fusion.11 = bf16[3,1024,256]{2,1,0:T(8,128)(2,1)S(1)} fusion(bf16[3,8192,256]{1,2,0:T(8,128)(2,1)} %constant_dynamic-update-slice_fusion, bf16[1024,8192]{1,0:T(8,128)(2,1)} %all-gather.2.cloned.1.call-done), kind=kOutput, calls=%fused_computation.17 | convolution fusion | flops 12885688320 | bytes 30932992 | tf_op jit(solution)/shard_map/tf,ifc->itc/dot_general | solution.py:150
  171.7 2.6 %fusion.2 = f32[3,1024,256]{2,1,0:T(8,128)S(1)} fusion(f32[3,1030,256]{2,1,0:T(8,128)S(1)} %maximum_convert_fusion, f32[3,256]{1,0:T(4,128)S(1)} %get-tuple-element.17, f32[3,256]{1,0:T(4,128)S(1)} %get-tuple-element.18, f32[3,256]{1,0:T(4,128)S(1)} %get-tuple-element.19, f32[3,256]{1,0:T(4,128)S(1)} %get-tuple-element.20, ...), kind=kLoop, calls=%fused_computation.3 | loop fusion | flops 10223616 | bytes 25187328 | tf_op jit(solution)/shard_map/add | solution.py:164
  174.3 1.5 slice_bitcast_fusion
  175.9 4.2 %shard_map.74 = f32[16,256]{1,0:T(8,128)} custom-call(f32[1024,256]{1,0:T(8,128)} %get-tuple-element.6.x_ref, f32[16,256]{1,0:T(8,128)} %get-tuple-element.15.r_ref, f32[16,256]{1,0:T(8,128)} %get-tuple-element.16.b_ref), custom_call_target="tpu_custom_call" | custom-call | tf_op jit(solution)/shard_map/pallas_call | solution.py:74
  180.9 13.1 %all_to_all.24 = f32[8,16,256]{2,1,0:T(8,128)S(1)} all-to-all(f32[8,16,256]{2,1,0:T(8,128)S(1)} %select_multiply_fusion), channel_id=1, replica_groups=mesh['ctx'=8,'ch'=32] {'ctx'}, dimensions={0} | all-to-all | bytes 262144 | tf_op jit(solution)/shard_map/all_to_all | solution.py:178
  194.6 7.4 %shard_map.75 = bf16[1024,256]{1,0:T(8,128)(2,1)} custom-call(f32[1024,256]{1,0:T(8,128)} %get-tuple-element.6.x_ref, f32[1024,256]{1,0:T(8,128)} %get-tuple-element.5.q_ref, f32[16,256]{1,0:T(8,128)} %get-tuple-element.15.r_ref, f32[16,256]{1,0:T(8,128)} %get-tuple-element.16.b_ref, f32[16,256]{1,0:T(8,128)} %res_ref.1, f32[1,256]{1,0:T(1,128)} %bitcast.39, ...), custom_call_target="tpu_custom_call" | custom-call | tf_op jit(solution)/shard_map/pallas_call | solution.py:92
  201.9 25.1 %all_to_all.25 = bf16[32,32,256]{2,1,0:T(8,128)(2,1)S(1)} all-to-all(bf16[32,32,256]{2,1,0:T(8,128)(2,1)} %bitcast.35), channel_id=1, replica_groups=mesh['ctx'=8,'ch'=32] {'ch'}, dimensions={0} | all-to-all | bytes 1048576 | tf_op jit(solution)/shard_map/all_to_all | solution.py:181
  (41 shorter events, 15.0 us)
Async XLA Ops:
  6.5 144.0 %all-gather.2.cloned.1.call-start = ((), (), s32[]{:S(2)}) async-start(), calls=%async_computation.2 | async-start | bytes 17301504 | tf_op jit(solution)/shard_map/all_gather | solution.py:147
  8.7 37.9 %collective-permute-start = (bf16[3,1024,256]{2,1,0:T(8,128)(2,1)}, bf16[3,1024,256]{2,1,0:T(8,128)(2,1)}, u32[]{:S(2)}, u32[]{:S(2)}) collective-permute-start(bf16[3,1024,256]{2,1,0:T(8,128)(2,1)} %param.9), channel_id=1, source_target_pairs={{0,64},{32,96},{64,128},{96,160},{128,192},{160,224},{192,0},{224,... | collective-permute-start | bytes 4718600 | tf_op jit(solution)/shard_map/ppermute | solution.py:136
  10.3 70.9 %collective-permute-start.1 = (bf16[3,1024,256]{2,1,0:T(8,128)(2,1)}, bf16[3,1024,256]{2,1,0:T(8,128)(2,1)}, u32[]{:S(2)}, u32[]{:S(2)}) collective-permute-start(bf16[3,1024,256]{2,1,0:T(8,128)(2,1)} %param.9), channel_id=1, source_target_pairs={{0,128},{32,160},{64,192},{96,224},{128,0},{160,32},{192,64},{224,... | collective-permute-start | bytes 4718600 | tf_op jit(solution)/shard_map/ppermute | solution.py:136
  13.0 68.1 %collective-permute-start.2 = (bf16[3,1024,256]{2,1,0:T(8,128)(2,1)}, bf16[3,1024,256]{2,1,0:T(8,128)(2,1)}, u32[]{:S(2)}, u32[]{:S(2)}) collective-permute-start(bf16[3,1024,256]{2,1,0:T(8,128)(2,1)} %param.9), channel_id=1, source_target_pairs={{0,192},{32,224},{64,0},{96,32},{128,64},{160,96},{192,128},{224,1... | collective-permute-start | bytes 4718600 | tf_op jit(solution)/shard_map/ppermute | solution.py:136
  14.5 74.8 %collective-permute-start.3 = (bf16[3,1024,256]{2,1,0:T(8,128)(2,1)}, bf16[3,1024,256]{2,1,0:T(8,128)(2,1)}, u32[]{:S(2)}, u32[]{:S(2)}) collective-permute-start(bf16[3,1024,256]{2,1,0:T(8,128)(2,1)} %param.9), channel_id=1, source_target_pairs={{0,32},{32,0},{64,96},{96,64},{128,160},{160,128},{192,224},{224,1... | collective-permute-start | bytes 4718600 | tf_op jit(solution)/shard_map/ppermute | solution.py:138
  22.4 1.3 copy-start.2
  22.4 59.3 %copy-start.3 = (f32[16,256]{1,0:T(8,128)S(1)}, f32[16,256]{1,0:T(8,128)}, u32[]{:S(2)}) copy-start(f32[16,256]{1,0:T(8,128)} %param.11) | copy-start | bytes 49156
  46.6 51.1 %collective-permute-start.4 = (bf16[3,1024,256]{2,1,0:T(8,128)(2,1)}, bf16[3,1024,256]{2,1,0:T(8,128)(2,1)}, u32[]{:S(2)}, u32[]{:S(2)}) collective-permute-start(bf16[3,1024,256]{2,1,0:T(8,128)(2,1)} %collective-permute-done), channel_id=1, source_target_pairs={{0,32},{32,0},{64,96},{96,64},{128,160},{160,128},{192,224},{224,1... | collective-permute-start | bytes 4718600 | tf_op jit(solution)/shard_map/ppermute | solution.py:138
  81.2 18.3 %collective-permute-start.5 = (bf16[3,1024,256]{2,1,0:T(8,128)(2,1)}, bf16[3,1024,256]{2,1,0:T(8,128)(2,1)}, u32[]{:S(2)}, u32[]{:S(2)}) collective-permute-start(bf16[3,1024,256]{2,1,0:T(8,128)(2,1)} %collective-permute-done.1), channel_id=1, source_target_pairs={{0,32},{32,0},{64,96},{96,64},{128,160},{160,128},{192,224},{224,1... | collective-permute-start | bytes 4718600 | tf_op jit(solution)/shard_map/ppermute | solution.py:138
  81.2 20.1 %collective-permute-start.6 = (bf16[3,1024,256]{2,1,0:T(8,128)(2,1)}, bf16[3,1024,256]{2,1,0:T(8,128)(2,1)}, u32[]{:S(2)}, u32[]{:S(2)}) collective-permute-start(bf16[3,1024,256]{2,1,0:T(8,128)(2,1)} %collective-permute-done.2), channel_id=1, source_target_pairs={{0,32},{32,0},{64,96},{96,64},{128,160},{160,128},{192,224},{224,1... | collective-permute-start | bytes 4718600 | tf_op jit(solution)/shard_map/ppermute | solution.py:138
  91.0 2.8 %copy-start = (bf16[3,1024,256]{1,2,0:T(8,128)(2,1)S(1)}, bf16[3,1024,256]{1,2,0:T(8,128)(2,1)}, u32[]{:S(2)}) copy-start(bf16[3,1024,256]{1,2,0:T(8,128)(2,1)} %copy.30) | copy-start | bytes 4718596
  103.9 2.6 %copy-start.1 = (bf16[3,1024,256]{1,2,0:T(8,128)(2,1)S(1)}, bf16[3,1024,256]{1,2,0:T(8,128)(2,1)}, u32[]{:S(2)}) copy-start(bf16[3,1024,256]{1,2,0:T(8,128)(2,1)} %copy.35) | copy-start | bytes 4718596
  169.3 2.1 collective-permute-start.7
Sparse Core Ops, SparseCore 0:
  9.9 140.5 all-gather.1

commit v11 on v7

--- a/solution.py
+++ b/solution.py
@@ -16,24 +16,34 @@
 LANES = 128
 
 
+CHUNKS = 8
+
+
 def ends_kernel(x_ref, r_ref, b_ref, end_ref):
     half = r_ref.shape[0] // 2
     r0, r1 = r_ref[:half, :], r_ref[half:, :]
     b0, b1 = b_ref[:half, :], b_ref[half:, :]
+    chunks = end_ref.shape[0]
+    span = x_ref.shape[0] // chunks
 
     def step8(i, carry):
-        s0, s1 = carry
-        xb = x_ref[pl.ds(pl.multiple_of(i * 8, 8), 8), :]
-        for k in range(8):
-            xt = xb[k : k + 1, :]
-            s0 = r0 * s0 + b0 * xt
-            s1 = r1 * s1 + b1 * xt
-        return s0, s1
+        carry = list(carry)
+        at = pl.multiple_of(i * 8, 8)
+        for c in range(chunks):
+            s0, s1 = carry[2 * c], carry[2 * c + 1]
+            xb = x_ref[pl.ds(c * span + at, 8), :]
+            for k in range(8):
+                xt = xb[k : k + 1, :]
+                s0 = r0 * s0 + b0 * xt
+                s1 = r1 * s1 + b1 * xt
+            carry[2 * c], carry[2 * c + 1] = s0, s1
+        return tuple(carry)
 
     zero = jnp.zeros((half, x_ref.shape[1]), jnp.float32)
-    s0, s1 = lax.fori_loop(0, x_ref.shape[0] // 8, step8, (zero, zero))
-    end_ref[:half, :] = s0
-    end_ref[half:, :] = s1
+    ends = lax.fori_loop(0, span // 8, step8, (zero,) * (2 * chunks))
+    for c in range(chunks):
+        end_ref[c, :half, :] = ends[2 * c]
+        end_ref[c, half:, :] = ends[2 * c + 1]
 
 
 def gate_kernel(x_ref, q_ref, r_ref, b_ref, res_ref, skip_ref, init_ref, out_ref):
@@ -79,8 +89,8 @@
             pl.BlockSpec((modes, lanes), col),
             pl.BlockSpec((modes, lanes), col),
         ],
-        out_specs=pl.BlockSpec((modes, lanes), col),
-        out_shape=jax.ShapeDtypeStruct((modes, chans), jnp.float32),
+        out_specs=pl.BlockSpec((CHUNKS, modes, lanes), lambda i: (0, 0, i)),
+        out_shape=jax.ShapeDtypeStruct((CHUNKS, modes, chans), jnp.float32),
     )(x, retention, in_scale)
 
 
@@ -151,7 +161,11 @@
     mixed = featured[1] * featured[2]
     retention = jnp.exp(-decay_rate)
     in_scale = jnp.sqrt(-jnp.expm1(-2.0 * decay_rate))
-    local_end = modal_ends(mixed, retention, in_scale)
+    chunk_ends = modal_ends(mixed, retention, in_scale)
+    chunk_decay = jnp.exp(-decay_rate * float(row_count // CHUNKS))
+    local_end = chunk_ends[0]
+    for c in range(1, CHUNKS):
+        local_end = chunk_decay * local_end + chunk_ends[c]
     range_count = lax.axis_size("ctx")
     later = jnp.arange(range_count) - lax.axis_index("ctx") - 1
     lag = (float(row_count) * jnp.maximum(later, 0).astype(jnp.float32))[:, None, None]

time: 235 us -> 235 us (level)
  no operation moved by 1% of the time
where the time goes in v11:
time: 235 us; the launch traced here: 234 us
  waiting for transfers between devices  101 us (43%)
  blocking collectives  38.1 us (16%)
  local copies, waits for them, and re-layouts  34.6 us (15%)
  matrix products  18.8 us (8%)
  between operations  13.7 us (6%)
  Pallas kernels  11.1 us (5%)
  other arithmetic  10.1 us (4%)
  starting transfers between devices  7.54 us (3%)
    ppermute x3, waiting for transfers between devices, gathered_weight(): held.append((lax.ppermute(block, 'ctx', pairs), (me - by) % count))  58.4 us
    all_gather x1, waiting for transfers between devices, on_device_body(): gathered = lax.all_gather(normed, 'ch', axis=0, tiled=True)  41.4 us
    all_to_all x1, blocking collectives, on_device_body(): return lax.all_to_all(gated, 'ch', split_axis=0, concat_axis=1, tiled=True)  25.1 us
    dot_general x1, matrix products, on_device_body(): jnp.einsum('tf,ifc->itc', gathered, gathered_weight(proj_weight), preferr...  18.8 us
    all_to_all x1, blocking collectives, on_device_body(): lax.all_to_all(sent, 'ctx', split_axis=0, concat_axis=0, tiled=True)  13.1 us
    dynamic_update_slice x8, local copies, waits for them, and re-layouts, gathered_weight(): full = lax.dynamic_update_slice(full, part, (0, src * width, 0))  12.1 us
    ppermute x4, local copies, waits for them, and re-layouts, gathered_weight(): lax.ppermute(part, 'ctx', sibling)  7.79 us
    pallas_call x1, Pallas kernels, modal_gate(): pl.pallas_call(gate_kernel, grid=(chans // lanes,), in_specs=[pl.BlockSpe...  7.35 us
  transfers between devices with their start and end apart: 9, of which 4 were waited for; matrix products, arithmetic and copies ran while one was open for 15% of the time, Pallas kernels for 0%

profile of v11, /device:TPU:32, one launch (start us, length us, event | category | flops | bytes accessed | tf_op | source)
XLA Modules:
  0.0 234.5 jit_solution(15209699321369953656)
XLA Ops:
  6.5 1.4 fusion.14
  7.9 2.0 fusion.16
  10.0 1.6 collective-permute-start
  11.5 2.7 %collective-permute-start.1 = (bf16[3,1024,256]{2,1,0:T(8,128)(2,1)}, bf16[3,1024,256]{2,1,0:T(8,128)(2,1)}, u32[]{:S(2)}, u32[]{:S(2)}) collective-permute-start(bf16[3,1024,256]{2,1,0:T(8,128)(2,1)} %param.9), channel_id=1, source_target_pairs={{0,128},{32,160},{64,192},{96,224},{128,0},{160,32},{192,64},{224,... | collective-permute-start | bytes 4718600 | tf_op jit(solution)/shard_map/ppermute | solution.py:126
  14.3 1.4 collective-permute-start.2
  16.7 6.1 %broadcast_in_dim.14 = bf16[3,8192,256]{1,2,0:T(8,128)(2,1)} broadcast(bf16[]{:T(256)} %constant.43.clone.1), dimensions={} | broadcast | bytes 12582914 | tf_op jit(solution)/shard_map/broadcast_in_dim | solution.py:129
  24.1 23.8 %collective-permute-done = bf16[3,1024,256]{2,1,0:T(8,128)(2,1)} collective-permute-done((bf16[3,1024,256]{2,1,0:T(8,128)(2,1)}, bf16[3,1024,256]{2,1,0:T(8,128)(2,1)}, u32[]{:S(2)}, u32[]{:S(2)}) %collective-permute-start) | collective-permute-done | bytes 1572896 | tf_op jit(solution)/shard_map/ppermute | solution.py:126
  47.9 34.5 %collective-permute-done.1 = bf16[3,1024,256]{2,1,0:T(8,128)(2,1)} collective-permute-done((bf16[3,1024,256]{2,1,0:T(8,128)(2,1)}, bf16[3,1024,256]{2,1,0:T(8,128)(2,1)}, u32[]{:S(2)}, u32[]{:S(2)}) %collective-permute-start.1) | collective-permute-done | bytes 1572896 | tf_op jit(solution)/shard_map/ppermute | solution.py:126
  83.6 2.6 %copy.29 = bf16[3,1024,256]{1,2,0:T(8,128)(2,1)} copy(bf16[3,1024,256]{2,1,0:T(8,128)(2,1)} %collective-permute-done) | data formatting | bytes 3145728 | tf_op jit(solution)/shard_map/ppermute | solution.py:126
  86.2 2.6 %copy.30 = bf16[3,1024,256]{1,2,0:T(8,128)(2,1)} copy(bf16[3,1024,256]{2,1,0:T(8,128)(2,1)} %collective-permute-done.1) | data formatting | bytes 3145728 | tf_op jit(solution)/shard_map/ppermute | solution.py:126
  88.8 1.7 copy.31
  90.6 1.7 copy.32
  92.3 3.0 %constant_dynamic-update-slice_fusion.6 = bf16[3,8192,256]{1,2,0:T(8,128)(2,1)} fusion(bf16[3,8192,256]{1,2,0:T(8,128)(2,1)} %constant_dynamic-update-slice_fusion.7, bf16[3,1024,256]{1,2,0:T(8,128)(2,1)} %copy.29, s32[]{:T(128)S(6)} %select_n.45), kind=kLoop, calls=%fused_computation.63 | loop fusion | bytes 3145732 | tf_op jit(solution)/shard_map/dynamic_update_slice | solution.py:131
  99.2 1.7 copy.33
  101.0 1.7 copy.34
  102.7 2.6 %copy.35 = bf16[3,1024,256]{1,2,0:T(8,128)(2,1)} copy(bf16[3,1024,256]{2,1,0:T(8,128)(2,1)} %collective-permute-done.6) | data formatting | bytes 3145728 | tf_op jit(solution)/shard_map/ppermute | solution.py:128
  109.2 41.4 %all-gather.2.cloned.1.call-done = bf16[1024,8192]{1,0:T(8,128)(2,1)} async-done(((bf16[32,8192]{1,0:T(8,128)(2,1)}), bf16[1024,8192]{1,0:T(8,128)(2,1)}) %all-gather.2.cloned.1.call-update) | async-done | bytes 16777232 | tf_op jit(solution)/shard_map/all_gather | solution.py:139
  150.7 18.8 %fusion.11 = bf16[3,1024,256]{2,1,0:T(8,128)(2,1)S(1)} fusion(bf16[3,8192,256]{1,2,0:T(8,128)(2,1)} %constant_dynamic-update-slice_fusion, bf16[1024,8192]{1,0:T(8,128)(2,1)} %all-gather.2.cloned.1.call-done), kind=kOutput, calls=%fused_computation.17 | convolution fusion | flops 12885688320 | bytes 30932992 | tf_op jit(solution)/shard_map/tf,ifc->itc/dot_general | solution.py:142
  171.9 2.6 %fusion.2 = f32[3,1024,256]{2,1,0:T(8,128)S(1)} fusion(f32[3,1030,256]{2,1,0:T(8,128)S(1)} %maximum_convert_fusion, f32[3,256]{1,0:T(4,128)S(1)} %get-tuple-element.17, f32[3,256]{1,0:T(4,128)S(1)} %get-tuple-element.18, f32[3,256]{1,0:T(4,128)S(1)} %get-tuple-element.19, f32[3,256]{1,0:T(4,128)S(1)} %get-tuple-element.20, ...), kind=kLoop, calls=%fused_computation.3 | loop fusion | flops 10223616 | bytes 25187328 | tf_op jit(solution)/shard_map/add | solution.py:156
  174.5 1.5 slice_bitcast_fusion
  176.0 3.7 %shard_map.73 = f32[8,16,256]{2,1,0:T(8,128)} custom-call(f32[1024,256]{1,0:T(8,128)} %get-tuple-element.6.x_ref, f32[16,256]{1,0:T(8,128)} %get-tuple-element.15.r_ref, f32[16,256]{1,0:T(8,128)} %get-tuple-element.16.b_ref), custom_call_target="tpu_custom_call" | custom-call | tf_op jit(solution)/shard_map/pallas_call | solution.py:84
  180.7 13.1 %all_to_all.24 = f32[8,16,256]{2,1,0:T(8,128)S(1)} all-to-all(f32[8,16,256]{2,1,0:T(8,128)S(1)} %select_multiply_fusion), channel_id=1, replica_groups=mesh['ctx'=8,'ch'=32] {'ctx'}, dimensions={0} | all-to-all | bytes 262144 | tf_op jit(solution)/shard_map/all_to_all | solution.py:174
  194.4 7.4 %shard_map.74 = bf16[1024,256]{1,0:T(8,128)(2,1)} custom-call(f32[1024,256]{1,0:T(8,128)} %get-tuple-element.6.x_ref, f32[1024,256]{1,0:T(8,128)} %get-tuple-element.5.q_ref, f32[16,256]{1,0:T(8,128)} %get-tuple-element.15.r_ref, f32[16,256]{1,0:T(8,128)} %get-tuple-element.16.b_ref, f32[16,256]{1,0:T(8,128)} %res_ref.1, f32[1,256]{1,0:T(1,128)} %bitcast.95, ...), custom_call_target="tpu_custom_call" | custom-call | tf_op jit(solution)/shard_map/pallas_call | solution.py:102
  201.7 25.1 %all_to_all.25 = bf16[32,32,256]{2,1,0:T(8,128)(2,1)S(1)} all-to-all(bf16[32,32,256]{2,1,0:T(8,128)(2,1)} %bitcast.92), channel_id=1, replica_groups=mesh['ctx'=8,'ch'=32] {'ch'}, dimensions={0} | all-to-all | bytes 1048576 | tf_op jit(solution)/shard_map/all_to_all | solution.py:177
  (46 shorter events, 15.9 us)
Async XLA Ops:
  6.5 9.2 %copy-start.2 = (bf16[3,1024,256]{2,1,0:T(8,128)(2,1)S(1)}, bf16[3,1024,256]{2,1,0:T(8,128)(2,1)}, u32[]{:S(2)}) copy-start(bf16[3,1024,256]{2,1,0:T(8,128)(2,1)} %param.9) | copy-start | bytes 4718596
  6.5 144.1 %all-gather.2.cloned.1.call-start = ((), (), s32[]{:S(2)}) async-start(), calls=%async_computation.2 | async-start | bytes 17301504 | tf_op jit(solution)/shard_map/all_gather | solution.py:139
  10.0 37.9 %collective-permute-start = (bf16[3,1024,256]{2,1,0:T(8,128)(2,1)}, bf16[3,1024,256]{2,1,0:T(8,128)(2,1)}, u32[]{:S(2)}, u32[]{:S(2)}) collective-permute-start(bf16[3,1024,256]{2,1,0:T(8,128)(2,1)} %param.9), channel_id=1, source_target_pairs={{0,64},{32,96},{64,128},{96,160},{128,192},{160,224},{192,0},{224,... | collective-permute-start | bytes 4718600 | tf_op jit(solution)/shard_map/ppermute | solution.py:126
  11.5 70.9 %collective-permute-start.1 = (bf16[3,1024,256]{2,1,0:T(8,128)(2,1)}, bf16[3,1024,256]{2,1,0:T(8,128)(2,1)}, u32[]{:S(2)}, u32[]{:S(2)}) collective-permute-start(bf16[3,1024,256]{2,1,0:T(8,128)(2,1)} %param.9), channel_id=1, source_target_pairs={{0,128},{32,160},{64,192},{96,224},{128,0},{160,32},{192,64},{224,... | collective-permute-start | bytes 4718600 | tf_op jit(solution)/shard_map/ppermute | solution.py:126
  14.3 68.1 %collective-permute-start.2 = (bf16[3,1024,256]{2,1,0:T(8,128)(2,1)}, bf16[3,1024,256]{2,1,0:T(8,128)(2,1)}, u32[]{:S(2)}, u32[]{:S(2)}) collective-permute-start(bf16[3,1024,256]{2,1,0:T(8,128)(2,1)} %param.9), channel_id=1, source_target_pairs={{0,192},{32,224},{64,0},{96,32},{128,64},{160,96},{192,128},{224,1... | collective-permute-start | bytes 4718600 | tf_op jit(solution)/shard_map/ppermute | solution.py:126
  15.7 74.9 %collective-permute-start.3 = (bf16[3,1024,256]{2,1,0:T(8,128)(2,1)}, bf16[3,1024,256]{2,1,0:T(8,128)(2,1)}, u32[]{:S(2)}, u32[]{:S(2)}) collective-permute-start(bf16[3,1024,256]{2,1,0:T(8,128)(2,1)} %param.9), channel_id=1, source_target_pairs={{0,32},{32,0},{64,96},{96,64},{128,160},{160,128},{192,224},{224,1... | collective-permute-start | bytes 4718600 | tf_op jit(solution)/shard_map/ppermute | solution.py:128
  22.7 1.3 copy-start.4
  22.7 60.2 %copy-start.3 = (f32[16,256]{1,0:T(8,128)S(1)}, f32[16,256]{1,0:T(8,128)}, u32[]{:S(2)}) copy-start(f32[16,256]{1,0:T(8,128)} %param.11) | copy-start | bytes 49156
  47.9 51.4 %collective-permute-start.4 = (bf16[3,1024,256]{2,1,0:T(8,128)(2,1)}, bf16[3,1024,256]{2,1,0:T(8,128)(2,1)}, u32[]{:S(2)}, u32[]{:S(2)}) collective-permute-start(bf16[3,1024,256]{2,1,0:T(8,128)(2,1)} %collective-permute-done), channel_id=1, source_target_pairs={{0,32},{32,0},{64,96},{96,64},{128,160},{160,128},{192,224},{224,1... | collective-permute-start | bytes 4718600 | tf_op jit(solution)/shard_map/ppermute | solution.py:128
  82.4 18.6 %collective-permute-start.5 = (bf16[3,1024,256]{2,1,0:T(8,128)(2,1)}, bf16[3,1024,256]{2,1,0:T(8,128)(2,1)}, u32[]{:S(2)}, u32[]{:S(2)}) collective-permute-start(bf16[3,1024,256]{2,1,0:T(8,128)(2,1)} %collective-permute-done.1), channel_id=1, source_target_pairs={{0,32},{32,0},{64,96},{96,64},{128,160},{160,128},{192,224},{224,1... | collective-permute-start | bytes 4718600 | tf_op jit(solution)/shard_map/ppermute | solution.py:128
  82.4 20.3 %collective-permute-start.6 = (bf16[3,1024,256]{2,1,0:T(8,128)(2,1)}, bf16[3,1024,256]{2,1,0:T(8,128)(2,1)}, u32[]{:S(2)}, u32[]{:S(2)}) collective-permute-start(bf16[3,1024,256]{2,1,0:T(8,128)(2,1)} %collective-permute-done.2), channel_id=1, source_target_pairs={{0,32},{32,0},{64,96},{96,64},{128,160},{160,128},{192,224},{224,1... | collective-permute-start | bytes 4718600 | tf_op jit(solution)/shard_map/ppermute | solution.py:128
  92.3 3.1 %copy-start = (bf16[3,1024,256]{1,2,0:T(8,128)(2,1)S(1)}, bf16[3,1024,256]{1,2,0:T(8,128)(2,1)}, u32[]{:S(2)}) copy-start(bf16[3,1024,256]{1,2,0:T(8,128)(2,1)} %copy.30) | copy-start | bytes 4718596
  105.3 2.6 %copy-start.1 = (bf16[3,1024,256]{1,2,0:T(8,128)(2,1)S(1)}, bf16[3,1024,256]{1,2,0:T(8,128)(2,1)}, u32[]{:S(2)}) copy-start(bf16[3,1024,256]{1,2,0:T(8,128)(2,1)} %copy.35) | copy-start | bytes 4718596
  169.5 2.1 collective-permute-start.7
Sparse Core Ops, SparseCore 0:
  10.1 140.5 all-gather.1
